TPU v7x, 512 devices: a whole 4x4x16 slice. The times are simulated.
512 devices in a mesh: head: 4 (over x_lo, core), seq: 128 (over x_hi, z, y).
Axes of the slice: x: 4 (x_hi: 2, x_lo: 2; x = x_hi * 2 + x_lo), y: 4, z: 16, core: 2. Of those that a mesh axis runs over, the one named last changes fastest.
Arguments:
- queries: bfloat16 [32768, 32, 128], P('seq', 'head'), may hold values from -6 to 6
- normed_keys: bfloat16 [32768, 16, 128], P('seq', 'head'), may hold values from -6 to 6
- value_matrix: bfloat16 [32768, 16, 128], P('seq', 'head'), may hold values from -6 to 6
- forward_out: bfloat16 [32768, 32, 128], P('seq', 'head'), may hold values from -1.75 to 1.75
- output_gradient: bfloat16 [32768, 32, 128], P(('seq', 'head')), may hold values from -96 to 96
- row_log_total: float32 [32, 32768], P('head', 'seq'), may hold values from 6 to 8
- pair_start: int32 [32768], P('seq'), may hold values from 0 to 32256, as said below
Outputs:
- query_grad: bfloat16 [32768, 32, 128], P(('seq', 'head'))
- key_grad: bfloat16 [32768, 16, 128], P(('seq', 'head'))
- value_grad: bfloat16 [32768, 16, 128], P(('seq', 'head'))
Inputs may be any that keep to these rules, and one draw needn't show every extreme that they name: pair_start[p] is the first position of the pair that holds token p: it never falls, never exceeds p, and equals p at each pair's first token; the last pair holds the final 1024 / 2 tokens, the pair before it at most 1024 tokens, and every other pair 1024 / 8 to 1024 tokens.
All inputs are finite; a program needn't handle non-finite values.
Results may differ from a plain program's by a relative error of at most 0.0059.
Values may be sent and summed in bfloat16 or wider, within the bound.
No kernel may reach another device: no remote copies, remote signals or barrier semaphores. Data moves between devices by JAX's collectives and lax.ppermute only.
A program may use at most 64 MiB of HBM per device.

v0:
```python
from functools import partial

import jax
import jax.numpy as jnp
from jax import lax
from jax.sharding import PartitionSpec as P

WINDOW_LENGTH = 1024


score_scale = 168.0 ** (-0.5)


def shifted(value, axis, by):
    size = lax.axis_size(axis)
    pairs = [(i, i + by) for i in range(size) if 0 <= i + by < size]
    return lax.ppermute(value, axis, pairs)


def visible_pairs(start_part, query_base, rows, key_base, cols):
    query_place = query_base + jnp.arange(rows, dtype=jnp.int32)
    key_place = key_base + jnp.arange(cols, dtype=jnp.int32)
    gap = query_place[:, None] - key_place[None, :]
    return (gap >= 0) & (gap < WINDOW_LENGTH) & (key_place[None, :] >= start_part[:, None])


def tile_terms(
    visible,
    query_part,
    grad_part,
    logsum_part,
    delta_part,
    key_part,
    value_part,
    want_query,
    want_keys,
):
    scores = (
        jnp.einsum("ikgd,jkd->kgij", query_part, key_part, preferred_element_type=jnp.float32)
        * score_scale
    )
    probs = jnp.where(visible, jnp.exp(scores - logsum_part[..., None]), 0.0)
    dprobs = jnp.einsum("ikgd,jkd->kgij", grad_part, value_part, preferred_element_type=jnp.float32)
    low_scores = (probs * (dprobs - delta_part[..., None])).astype(jnp.bfloat16)
    terms = []
    terms.append(
        jnp.einsum("kgij,jkd->ikgd", low_scores, key_part, preferred_element_type=jnp.float32)
    )
    low_probs = probs.astype(jnp.bfloat16)
    terms.append(
        jnp.einsum("kgij,ikgd->jkd", low_scores, query_part, preferred_element_type=jnp.float32)
    )
    terms.append(
        jnp.einsum("kgij,ikgd->jkd", low_probs, grad_part, preferred_element_type=jnp.float32)
    )
    return tuple(terms)


def run_tile(
    query_part,
    grad_part,
    logsum_part,
    delta_part,
    start_part,
    query_base,
    key_part,
    value_part,
    key_base,
):
    visible = visible_pairs(
        start_part, query_base, query_part.shape[0], key_base, key_part.shape[0]
    )
    work = partial(
        tile_terms,
        visible,
        query_part,
        grad_part,
        logsum_part,
        delta_part,
        key_part,
        value_part,
        True,
        True,
    )
    return work()


def on_device(
    queries, normed_keys, value_matrix, forward_out, output_gradient, row_log_total, pair_start
):
    grad_rows = lax.all_to_all(output_gradient, "head", split_axis=1, concat_axis=0, tiled=True)
    local_tokens, query_heads, depth = queries.shape
    key_heads = normed_keys.shape[1]
    group_size = query_heads // key_heads
    delta_rows = jnp.einsum(
        "thd,thd->th", forward_out, grad_rows, preferred_element_type=jnp.float32
    )
    query_four = queries.reshape(local_tokens, key_heads, group_size, depth)
    grad_four = grad_rows.reshape(local_tokens, key_heads, group_size, depth)
    logsum_three = row_log_total.reshape(key_heads, group_size, local_tokens)
    delta_three = delta_rows.T.reshape(key_heads, group_size, local_tokens)
    position = lax.axis_index("seq") * local_tokens
    reach = WINDOW_LENGTH // local_tokens
    query_sum, key_sum, value_sum = run_tile(
        query_four,
        grad_four,
        logsum_three,
        delta_three,
        pair_start,
        position,
        normed_keys,
        value_matrix,
        position,
    )
    for back in range(1, reach + 1):
        key_far, value_far = shifted((normed_keys, value_matrix), "seq", back)
        far_base = position - back * local_tokens
        query_term, key_term, value_term = run_tile(
            query_four,
            grad_four,
            logsum_three,
            delta_three,
            pair_start,
            position,
            key_far,
            value_far,
            far_base,
        )
        query_sum = query_sum + query_term
        key_back, value_back = shifted((key_term, value_term), "seq", -back)
        key_sum = key_sum + key_back
        value_sum = value_sum + value_back
    query_grad = (
        (query_sum * score_scale).astype(jnp.bfloat16).reshape(local_tokens, query_heads, depth)
    )
    key_grad = (key_sum * score_scale).astype(jnp.bfloat16)
    value_grad = value_sum.astype(jnp.bfloat16)
    return (
        lax.all_to_all(query_grad, "head", split_axis=0, concat_axis=1, tiled=True),
        lax.all_to_all(key_grad, "head", split_axis=0, concat_axis=1, tiled=True),
        lax.all_to_all(value_grad, "head", split_axis=0, concat_axis=1, tiled=True),
    )


def solution(mesh):
    placed = (
        P("seq", "head", None),
        P("seq", "head", None),
        P("seq", "head", None),
        P("seq", "head", None),
        P(("seq", "head"), None, None),
        P("head", "seq"),
        P("seq"),
    )
    return jax.shard_map(
        on_device,
        mesh=mesh,
        in_specs=placed,
        out_specs=(
            P(("seq", "head"), None, None),
            P(("seq", "head"), None, None),
            P(("seq", "head"), None, None),
        ),
        check_vma=False,
    )
```

profile of v0, /device:TPU:484, one launch (start us, length us, event | category | flops | bytes accessed | tf_op | source)
XLA Modules:
  0.0 204.8 jit_solution(5845024021670637629)
XLA Ops:
  0.7 1.8 copy.49
  2.4 1.3 collective-permute-start.7
  3.7 4.9 %collective-permute-start.5 = (bf16[256,4,128]{2,0,1:T(8,128)(2,1)}, bf16[256,4,128]{2,0,1:T(8,128)(2,1)}, u32[]{:S(2)}, u32[]{:S(2)}) collective-permute-start(bf16[256,4,128]{2,0,1:T(8,128)(2,1)} %copy.49), channel_id=1, source_target_pairs={{0,3},{1,4},{2,5},{3,6},{4,7},{5,8},{6,9},{7,10},{8,11},{9,12},{10... | collective-permute-start | bytes 786440 | tf_op jit(solution)/shard_map/ppermute | solution.py:17
  8.7 1.9 collective-permute-start.3
  10.6 2.1 %collective-permute-start.1 = (bf16[256,4,128]{2,0,1:T(8,128)(2,1)}, bf16[256,4,128]{2,0,1:T(8,128)(2,1)}, u32[]{:S(2)}, u32[]{:S(2)}) collective-permute-start(bf16[256,4,128]{2,0,1:T(8,128)(2,1)} %copy.49), channel_id=1, source_target_pairs={{0,1},{1,2},{2,3},{3,4},{4,5},{5,6},{6,7},{7,8},{8,9},{9,10},{10,1... | collective-permute-start | bytes 786440 | tf_op jit(solution)/shard_map/ppermute | solution.py:17
  12.7 1.7 copy.47
  14.4 1.9 collective-permute-start.2
  16.3 2.0 copy.42
  18.4 3.5 %all-to-all-start = ((bf16[64,32,128]{2,0,1:T(8,128)(2,1)}), bf16[64,32,128]{2,0,1:T(8,128)(2,1)S(1)}, u32[]{:S(2)}, u32[]{:S(2)}) async-start(bf16[64,32,128]{2,0,1:T(8,128)(2,1)} %copy.42), calls=%async_computation | async-start | bytes 1048576 | tf_op jit(solution)/shard_map/all_to_all | solution.py:91
  22.4 2.0 fusion.19
  24.4 12.9 %collective-permute-done.2 = bf16[256,4,128]{2,0,1:T(8,128)(2,1)S(1)} collective-permute-done((bf16[256,4,128]{2,0,1:T(8,128)(2,1)}, bf16[256,4,128]{2,0,1:T(8,128)(2,1)S(1)}, u32[]{:S(2)}, u32[]{:S(2)}) %collective-permute-start.2) | collective-permute-done | bytes 262176 | tf_op jit(solution)/shard_map/ppermute | solution.py:17
  37.3 7.0 %collective-permute-start = (bf16[256,4,128]{2,0,1:T(8,128)(2,1)}, bf16[256,4,128]{2,0,1:T(8,128)(2,1)S(1)}, u32[]{:S(2)}, u32[]{:S(2)}) collective-permute-start(bf16[256,4,128]{2,0,1:T(8,128)(2,1)} %copy.47), channel_id=1, source_target_pairs={{0,1},{1,2},{2,3},{3,4},{4,5},{5,6},{6,7},{7,8},{8,9},{9,10},{10,1... | collective-permute-start | bytes 786440 | tf_op jit(solution)/shard_map/ppermute | solution.py:17
  44.2 1.9 fusion.11
  46.2 3.1 %collective-permute-done = bf16[256,4,128]{2,0,1:T(8,128)(2,1)S(1)} collective-permute-done((bf16[256,4,128]{2,0,1:T(8,128)(2,1)}, bf16[256,4,128]{2,0,1:T(8,128)(2,1)S(1)}, u32[]{:S(2)}, u32[]{:S(2)}) %collective-permute-start) | collective-permute-done | bytes 262176 | tf_op jit(solution)/shard_map/ppermute | solution.py:17
  49.2 1.9 collective-permute-start.4
  51.2 0.6 fusion.15
  51.8 7.0 %collective-permute-done.4 = bf16[256,4,128]{2,0,1:T(8,128)(2,1)S(1)} collective-permute-done((bf16[256,4,128]{2,0,1:T(8,128)(2,1)}, bf16[256,4,128]{2,0,1:T(8,128)(2,1)S(1)}, u32[]{:S(2)}, u32[]{:S(2)}) %collective-permute-start.4) | collective-permute-done | bytes 262176 | tf_op jit(solution)/shard_map/ppermute | solution.py:17
  58.8 1.3 collective-permute-start.6
  60.1 2.0 fusion.7
  62.1 5.2 %collective-permute-done.6 = bf16[256,4,128]{2,0,1:T(8,128)(2,1)S(1)} collective-permute-done((bf16[256,4,128]{2,0,1:T(8,128)(2,1)}, bf16[256,4,128]{2,0,1:T(8,128)(2,1)S(1)}, u32[]{:S(2)}, u32[]{:S(2)}) %collective-permute-start.6) | collective-permute-done | bytes 262176 | tf_op jit(solution)/shard_map/ppermute | solution.py:17
  67.2 0.7 copy-done.17
  67.9 2.0 fusion.3
  69.9 0.8 copy-done.7
  70.7 1.1 copy.43
  71.9 0.7 multiply_reduce_fusion
  72.7 2.2 %convolution_bitcast_fusion.2 = f32[256,4,128]{2,0,1:T(8,128)S(1)} fusion(bf16[256,4,2,128]{3,0,2,1:T(8,128)(2,1)S(1)} %bitcast.242, f32[4,2,256,256]{2,3,1,0:T(8,128)} %fusion.11), kind=kOutput, calls=%fused_computation.38 | convolution fusion | flops 134742016 | bytes 3145728 | tf_op jit(solution)/shard_map/kgij,ikgd->jkd/dot_general | solution.py:54
  74.9 1.4 fusion.9
  76.3 1.2 convolution_bitcast_fusion.7
  77.6 5.3 %collective-permute-start.9 = (f32[256,4,128]{2,0,1:T(8,128)}, f32[256,4,128]{2,0,1:T(8,128)}, u32[]{:S(2)}, u32[]{:S(2)}) collective-permute-start(f32[256,4,128]{2,0,1:T(8,128)} %convolution_bitcast_fusion.7), channel_id=1, source_target_pairs={{2,0},{3,1},{4,2},{5,3},{6,4},{7,5},{8,6},{9,7},{10,8},{11,9},{12,... | collective-permute-start | bytes 1572872 | tf_op jit(solution)/shard_map/ppermute | solution.py:17
  82.9 2.6 %collective-permute-start.13 = (f32[256,4,128]{2,0,1:T(8,128)S(1)}, f32[256,4,128]{2,0,1:T(8,128)S(1)}, u32[]{:S(2)}, u32[]{:S(2)}) collective-permute-start(f32[256,4,128]{2,0,1:T(8,128)S(1)} %convolution_bitcast_fusion.2), channel_id=1, source_target_pairs={{2,0},{3,1},{4,2},{5,3},{6,4},{7,5},{8,6},{9,7},{10,8},{11,9},{12,... | collective-permute-start | bytes 1572872 | tf_op jit(solution)/shard_map/ppermute | solution.py:17
  86.4 3.4 %collective-permute-start.12 = (f32[256,4,128]{2,0,1:T(8,128)S(1)}, f32[256,4,128]{2,0,1:T(8,128)S(1)}, u32[]{:S(2)}, u32[]{:S(2)}) collective-permute-start(f32[256,4,128]{2,0,1:T(8,128)S(1)} %convolution_bitcast_fusion.3), channel_id=1, source_target_pairs={{1,0},{2,1},{3,2},{4,3},{5,4},{6,5},{7,6},{8,7},{9,8},{10,9},{11,1... | collective-permute-start | bytes 1572872 | tf_op jit(solution)/shard_map/ppermute | solution.py:17
  89.8 1.4 fusion.5
  91.2 1.2 convolution_bitcast_fusion.6
  92.5 1.2 convolution_bitcast_fusion
  93.7 0.5 copy-done.1
  95.2 4.9 %collective-permute-start.14 = (f32[256,4,128]{2,0,1:T(8,128)S(1)}, f32[256,4,128]{2,0,1:T(8,128)S(1)}, u32[]{:S(2)}, u32[]{:S(2)}) collective-permute-start(f32[256,4,128]{2,0,1:T(8,128)S(1)} %convolution_bitcast_fusion.1), channel_id=1, source_target_pairs={{3,0},{4,1},{5,2},{6,3},{7,4},{8,5},{9,6},{10,7},{11,8},{12,9},{13... | collective-permute-start | bytes 1572872 | tf_op jit(solution)/shard_map/ppermute | solution.py:17
  100.2 1.4 fusion.13
  101.6 0.5 fusion.45
  102.1 6.1 %collective-permute-start.15 = (f32[256,4,128]{2,0,1:T(8,128)}, f32[256,4,128]{2,0,1:T(8,128)}, u32[]{:S(2)}, u32[]{:S(2)}) collective-permute-start(f32[256,4,128]{2,0,1:T(8,128)} %convolution_bitcast_fusion), channel_id=1, source_target_pairs={{4,0},{5,1},{6,2},{7,3},{8,4},{9,5},{10,6},{11,7},{12,8},{13,9},{1... | collective-permute-start | bytes 1572872 | tf_op jit(solution)/shard_map/ppermute | solution.py:17
  108.2 1.4 fusion.1
  110.2 1.3 convolution_bitcast_fusion.8
  111.4 0.5 convolution_add_fusion.1
  112.0 1.2 convolution_bitcast_fusion.5
  113.2 2.5 %collective-permute-start.8 = (f32[256,4,128]{2,0,1:T(8,128)}, f32[256,4,128]{2,0,1:T(8,128)}, u32[]{:S(2)}, u32[]{:S(2)}) collective-permute-start(f32[256,4,128]{2,0,1:T(8,128)} %convolution_bitcast_fusion.8), channel_id=1, source_target_pairs={{1,0},{2,1},{3,2},{4,3},{5,4},{6,5},{7,6},{8,7},{9,8},{10,9},{11,1... | collective-permute-start | bytes 1572872 | tf_op jit(solution)/shard_map/ppermute | solution.py:17
  115.7 2.6 %collective-permute-done.12 = f32[256,4,128]{2,0,1:T(8,128)S(1)} collective-permute-done((f32[256,4,128]{2,0,1:T(8,128)S(1)}, f32[256,4,128]{2,0,1:T(8,128)S(1)}, u32[]{:S(2)}, u32[]{:S(2)}) %collective-permute-start.12) | collective-permute-done | bytes 524320 | tf_op jit(solution)/shard_map/ppermute | solution.py:17
  118.3 2.0 collective-permute-start.10
  120.3 9.2 %collective-permute-done.14 = f32[256,4,128]{2,0,1:T(8,128)S(1)} collective-permute-done((f32[256,4,128]{2,0,1:T(8,128)S(1)}, f32[256,4,128]{2,0,1:T(8,128)S(1)}, u32[]{:S(2)}, u32[]{:S(2)}) %collective-permute-start.14) | collective-permute-done | bytes 524320 | tf_op jit(solution)/shard_map/ppermute | solution.py:17
  129.5 3.2 %collective-permute-start.11 = (f32[256,4,128]{2,0,1:T(8,128)}, f32[256,4,128]{2,0,1:T(8,128)}, u32[]{:S(2)}, u32[]{:S(2)}) collective-permute-start(f32[256,4,128]{2,0,1:T(8,128)} %convolution_bitcast_fusion.5), channel_id=1, source_target_pairs={{4,0},{5,1},{6,2},{7,3},{8,4},{9,5},{10,6},{11,7},{12,8},{13,9},{1... | collective-permute-start | bytes 1572872 | tf_op jit(solution)/shard_map/ppermute | solution.py:17
  132.8 0.5 fusion.23
  133.3 1.1 copy.63
  134.5 3.5 %all-to-all-start.1 = ((bf16[256,8,128]{2,1,0:T(8,128)(2,1)}), bf16[256,8,128]{2,1,0:T(8,128)(2,1)S(1)}, u32[]{:S(2)}, u32[]{:S(2)}) async-start(bf16[256,8,128]{2,1,0:T(8,128)(2,1)} %copy.63), calls=%async_computation.1 | async-start | bytes 1048576 | tf_op jit(solution)/shard_map/all_to_all | solution.py:139
  138.0 2.9 %collective-permute-done.15 = f32[256,4,128]{2,0,1:T(8,128)} collective-permute-done((f32[256,4,128]{2,0,1:T(8,128)}, f32[256,4,128]{2,0,1:T(8,128)}, u32[]{:S(2)}, u32[]{:S(2)}) %collective-permute-start.15) | collective-permute-done | bytes 524320 | tf_op jit(solution)/shard_map/ppermute | solution.py:17
  140.9 2.4 %fusion.33 = bf16[256,4,128]{2,0,1:T(8,128)(2,1)S(1)} fusion(f32[256,4,128]{2,0,1:T(8,128)} %collective-permute-done.15, f32[256,4,128]{2,0,1:T(8,128)} %copy-done.13, f32[256,4,128]{2,0,1:T(8,128)S(1)} %copy-done.11, f32[256,4,128]{2,0,1:T(8,128)} %copy-done.12, bf16[256,4,2,128]{3,0,2,1:T(8,128)(2,1)S(1)} %bitcast.251, f32[4,2,256,256]{2,3,1,0:T(8,128)} %fusion.19), kind=kOutput, calls=%fused_computation.55 | convolution fusion | flops 135397376 | bytes 4980736 | tf_op jit(solution)/shard_map/kgij,ikgd->jkd/dot_general | solution.py:54
  143.3 0.9 copy.72
  144.2 41.1 %all-to-all-done.1 = bf16[256,8,128]{2,1,0:T(8,128)(2,1)S(1)} async-done(((bf16[256,8,128]{2,1,0:T(8,128)(2,1)}), bf16[256,8,128]{2,1,0:T(8,128)(2,1)S(1)}, u32[]{:S(2)}, u32[]{:S(2)}) %all-to-all-start.1) | async-done | bytes 524320 | tf_op jit(solution)/shard_map/all_to_all | solution.py:139
  185.3 3.4 %all-to-all-start.3 = ((bf16[256,4,128]{2,1,0:T(4,128)(2,1)}), bf16[256,4,128]{2,1,0:T(4,128)(2,1)S(1)}, u32[]{:S(2)}, u32[]{:S(2)}) async-start(bf16[256,4,128]{2,1,0:T(4,128)(2,1)} %copy.72), calls=%async_computation.3 | async-start | bytes 524288 | tf_op jit(solution)/shard_map/all_to_all | solution.py:141
  188.7 1.9 fusion.34
  190.7 0.9 copy.70
  191.6 3.1 %all-to-all-done.3 = bf16[256,4,128]{2,1,0:T(4,128)(2,1)S(1)} async-done(((bf16[256,4,128]{2,1,0:T(4,128)(2,1)}), bf16[256,4,128]{2,1,0:T(4,128)(2,1)S(1)}, u32[]{:S(2)}, u32[]{:S(2)}) %all-to-all-start.3) | async-done | bytes 262176 | tf_op jit(solution)/shard_map/all_to_all | solution.py:141
  194.7 3.4 %all-to-all-start.2 = ((bf16[256,4,128]{2,1,0:T(4,128)(2,1)}), bf16[256,4,128]{2,1,0:T(4,128)(2,1)S(1)}, u32[]{:S(2)}, u32[]{:S(2)}) async-start(bf16[256,4,128]{2,1,0:T(4,128)(2,1)} %copy.70), calls=%async_computation.2 | async-start | bytes 524288 | tf_op jit(solution)/shard_map/all_to_all | solution.py:140
  198.1 0.9 copy.141
  199.0 0.8 copy.73
  199.8 4.3 %all-to-all-done.2 = bf16[256,4,128]{2,1,0:T(4,128)(2,1)S(1)} async-done(((bf16[256,4,128]{2,1,0:T(4,128)(2,1)}), bf16[256,4,128]{2,1,0:T(4,128)(2,1)S(1)}, u32[]{:S(2)}, u32[]{:S(2)}) %all-to-all-start.2) | async-done | bytes 262176 | tf_op jit(solution)/shard_map/all_to_all | solution.py:140
  204.0 0.8 copy.71
  (70 shorter events, 3.1 us)
Async XLA Ops:
  0.6 21.8 %copy-start = (bf16[256,8,128]{2,1,0:T(8,128)(2,1)S(1)}, bf16[256,8,128]{2,1,0:T(8,128)(2,1)}, u32[]{:S(2)}) copy-start(bf16[256,8,128]{2,1,0:T(8,128)(2,1)} %param.7) | copy-start | bytes 1572868
  0.6 21.8 %copy-start.8 = (bf16[256,4,128]{2,1,0:T(4,128)(2,1)S(1)}, bf16[256,4,128]{2,1,0:T(4,128)(2,1)}, u32[]{:S(2)}) copy-start(bf16[256,4,128]{2,1,0:T(4,128)(2,1)} %param.8) | copy-start | bytes 786436
  0.7 21.2 %copy-start.23 = (f32[8,256]{1,0:T(8,128)S(1)}, f32[8,256]{1,0:T(8,128)}, u32[]{:S(2)}) copy-start(f32[8,256]{1,0:T(8,128)} %param.12) | copy-start | bytes 24580
  0.7 21.3 %copy-start.24 = (s32[256]{0:T(256)S(1)}, s32[256]{0:T(256)}, u32[]{:S(2)}) copy-start(s32[256]{0:T(256)} %param.13) | copy-start | bytes 3076
  2.4 99.7 %collective-permute-start.7 = (bf16[256,4,128]{2,0,1:T(8,128)(2,1)}, bf16[256,4,128]{2,0,1:T(8,128)(2,1)}, u32[]{:S(2)}, u32[]{:S(2)}) collective-permute-start(bf16[256,4,128]{2,0,1:T(8,128)(2,1)} %copy.49), channel_id=1, source_target_pairs={{0,4},{1,5},{2,6},{3,7},{4,8},{5,9},{6,10},{7,11},{8,12},{9,13},{1... | collective-permute-start | bytes 786440 | tf_op jit(solution)/shard_map/ppermute | solution.py:17
  3.7 82.7 %collective-permute-start.5 = (bf16[256,4,128]{2,0,1:T(8,128)(2,1)}, bf16[256,4,128]{2,0,1:T(8,128)(2,1)}, u32[]{:S(2)}, u32[]{:S(2)}) collective-permute-start(bf16[256,4,128]{2,0,1:T(8,128)(2,1)} %copy.49), channel_id=1, source_target_pairs={{0,3},{1,4},{2,5},{3,6},{4,7},{5,8},{6,9},{7,10},{8,11},{9,12},{10... | collective-permute-start | bytes 786440 | tf_op jit(solution)/shard_map/ppermute | solution.py:17
  8.7 66.2 %collective-permute-start.3 = (bf16[256,4,128]{2,0,1:T(8,128)(2,1)}, bf16[256,4,128]{2,0,1:T(8,128)(2,1)}, u32[]{:S(2)}, u32[]{:S(2)}) collective-permute-start(bf16[256,4,128]{2,0,1:T(8,128)(2,1)} %copy.49), channel_id=1, source_target_pairs={{0,2},{1,3},{2,4},{3,5},{4,6},{5,7},{6,8},{7,9},{8,10},{9,11},{10,... | collective-permute-start | bytes 786440 | tf_op jit(solution)/shard_map/ppermute | solution.py:17
  10.6 84.7 %collective-permute-start.1 = (bf16[256,4,128]{2,0,1:T(8,128)(2,1)}, bf16[256,4,128]{2,0,1:T(8,128)(2,1)}, u32[]{:S(2)}, u32[]{:S(2)}) collective-permute-start(bf16[256,4,128]{2,0,1:T(8,128)(2,1)} %copy.49), channel_id=1, source_target_pairs={{0,1},{1,2},{2,3},{3,4},{4,5},{5,6},{6,7},{7,8},{8,9},{9,10},{10,1... | collective-permute-start | bytes 786440 | tf_op jit(solution)/shard_map/ppermute | solution.py:17
  14.4 22.8 %collective-permute-start.2 = (bf16[256,4,128]{2,0,1:T(8,128)(2,1)}, bf16[256,4,128]{2,0,1:T(8,128)(2,1)S(1)}, u32[]{:S(2)}, u32[]{:S(2)}) collective-permute-start(bf16[256,4,128]{2,0,1:T(8,128)(2,1)} %copy.47), channel_id=1, source_target_pairs={{0,2},{1,3},{2,4},{3,5},{4,6},{5,7},{6,8},{7,9},{8,10},{9,11},{10,... | collective-permute-start | bytes 786440 | tf_op jit(solution)/shard_map/ppermute | solution.py:17
  18.4 51.5 %all-to-all-start = ((bf16[64,32,128]{2,0,1:T(8,128)(2,1)}), bf16[64,32,128]{2,0,1:T(8,128)(2,1)S(1)}, u32[]{:S(2)}, u32[]{:S(2)}) async-start(bf16[64,32,128]{2,0,1:T(8,128)(2,1)} %copy.42), calls=%async_computation | async-start | bytes 1048576 | tf_op jit(solution)/shard_map/all_to_all | solution.py:91
  37.3 13.9 %copy-start.15 = (bf16[256,4,128]{2,0,1:T(8,128)(2,1)}, bf16[256,4,128]{2,0,1:T(8,128)(2,1)S(1)}, u32[]{:S(2)}) copy-start(bf16[256,4,128]{2,0,1:T(8,128)(2,1)S(1)} %collective-permute-done.2) | copy-start | bytes 786436
  37.3 12.0 %collective-permute-start = (bf16[256,4,128]{2,0,1:T(8,128)(2,1)}, bf16[256,4,128]{2,0,1:T(8,128)(2,1)S(1)}, u32[]{:S(2)}, u32[]{:S(2)}) collective-permute-start(bf16[256,4,128]{2,0,1:T(8,128)(2,1)} %copy.47), channel_id=1, source_target_pairs={{0,1},{1,2},{2,3},{3,4},{4,5},{5,6},{6,7},{7,8},{8,9},{9,10},{10,1... | collective-permute-start | bytes 786440 | tf_op jit(solution)/shard_map/ppermute | solution.py:17
  49.2 2.6 %copy-start.21 = (bf16[256,4,128]{2,0,1:T(8,128)(2,1)}, bf16[256,4,128]{2,0,1:T(8,128)(2,1)S(1)}, u32[]{:S(2)}) copy-start(bf16[256,4,128]{2,0,1:T(8,128)(2,1)S(1)} %collective-permute-done) | copy-start | bytes 786436
  49.2 9.5 %collective-permute-start.4 = (bf16[256,4,128]{2,0,1:T(8,128)(2,1)}, bf16[256,4,128]{2,0,1:T(8,128)(2,1)S(1)}, u32[]{:S(2)}, u32[]{:S(2)}) collective-permute-start(bf16[256,4,128]{2,0,1:T(8,128)(2,1)} %copy.47), channel_id=1, source_target_pairs={{0,3},{1,4},{2,5},{3,6},{4,7},{5,8},{6,9},{7,10},{8,11},{9,12},{10... | collective-permute-start | bytes 786440 | tf_op jit(solution)/shard_map/ppermute | solution.py:17
  51.8 33.7 %copy-start.2 = (f32[4,2,256,256]{2,3,1,0:T(8,128)}, f32[4,2,256,256]{2,3,1,0:T(8,128)S(1)}, u32[]{:S(2)}) copy-start(f32[4,2,256,256]{2,3,1,0:T(8,128)S(1)} %fusion.15) | copy-start | bytes 6291460
  58.8 8.5 %copy-start.19 = (bf16[256,4,128]{2,0,1:T(8,128)(2,1)}, bf16[256,4,128]{2,0,1:T(8,128)(2,1)S(1)}, u32[]{:S(2)}) copy-start(bf16[256,4,128]{2,0,1:T(8,128)(2,1)S(1)} %collective-permute-done.4) | copy-start | bytes 786436
  58.8 8.5 %collective-permute-start.6 = (bf16[256,4,128]{2,0,1:T(8,128)(2,1)}, bf16[256,4,128]{2,0,1:T(8,128)(2,1)S(1)}, u32[]{:S(2)}, u32[]{:S(2)}) collective-permute-start(bf16[256,4,128]{2,0,1:T(8,128)(2,1)} %copy.47), channel_id=1, source_target_pairs={{0,4},{1,5},{2,6},{3,7},{4,8},{5,9},{6,10},{7,11},{8,12},{9,13},{1... | collective-permute-start | bytes 786440 | tf_op jit(solution)/shard_map/ppermute | solution.py:17
  67.2 0.7 copy-start.17
  69.9 0.8 copy-start.7
  70.7 1.2 copy-start.14
  72.7 2.2 %copy-start.6 = (f32[4,2,256,256]{2,3,1,0:T(8,128)S(1)}, f32[4,2,256,256]{2,3,1,0:T(8,128)}, u32[]{:S(2)}) copy-start(f32[4,2,256,256]{2,3,1,0:T(8,128)} %fusion.11) | copy-start | bytes 6291460
  77.6 8.4 %copy-start.5 = (f32[4,2,256,256]{2,3,1,0:T(8,128)S(1)}, f32[4,2,256,256]{2,3,1,0:T(8,128)}, u32[]{:S(2)}) copy-start(f32[4,2,256,256]{2,3,1,0:T(8,128)} %fusion.7) | copy-start | bytes 6291460
  77.6 111.1 %collective-permute-start.9 = (f32[256,4,128]{2,0,1:T(8,128)}, f32[256,4,128]{2,0,1:T(8,128)}, u32[]{:S(2)}, u32[]{:S(2)}) collective-permute-start(f32[256,4,128]{2,0,1:T(8,128)} %convolution_bitcast_fusion.7), channel_id=1, source_target_pairs={{2,0},{3,1},{4,2},{5,3},{6,4},{7,5},{8,6},{9,7},{10,8},{11,9},{12,... | collective-permute-start | bytes 1572872 | tf_op jit(solution)/shard_map/ppermute | solution.py:17
  82.9 30.3 %collective-permute-start.13 = (f32[256,4,128]{2,0,1:T(8,128)S(1)}, f32[256,4,128]{2,0,1:T(8,128)S(1)}, u32[]{:S(2)}, u32[]{:S(2)}) collective-permute-start(f32[256,4,128]{2,0,1:T(8,128)S(1)} %convolution_bitcast_fusion.2), channel_id=1, source_target_pairs={{2,0},{3,1},{4,2},{5,3},{6,4},{7,5},{8,6},{9,7},{10,8},{11,9},{12,... | collective-permute-start | bytes 1572872 | tf_op jit(solution)/shard_map/ppermute | solution.py:17
  86.4 6.1 %copy-start.4 = (f32[4,2,256,256]{2,3,1,0:T(8,128)S(1)}, f32[4,2,256,256]{2,3,1,0:T(8,128)}, u32[]{:S(2)}) copy-start(f32[4,2,256,256]{2,3,1,0:T(8,128)} %fusion.3) | copy-start | bytes 6291460
  86.4 31.9 %collective-permute-start.12 = (f32[256,4,128]{2,0,1:T(8,128)S(1)}, f32[256,4,128]{2,0,1:T(8,128)S(1)}, u32[]{:S(2)}, u32[]{:S(2)}) collective-permute-start(f32[256,4,128]{2,0,1:T(8,128)S(1)} %convolution_bitcast_fusion.3), channel_id=1, source_target_pairs={{1,0},{2,1},{3,2},{4,3},{5,4},{6,5},{7,6},{8,7},{9,8},{10,9},{11,1... | collective-permute-start | bytes 1572872 | tf_op jit(solution)/shard_map/ppermute | solution.py:17
  92.5 1.8 copy-start.1
  92.5 1.8 copy-start.9
  94.7 5.5 %copy-start.3 = (f32[4,2,256,256]{2,3,1,0:T(8,128)S(1)}, f32[4,2,256,256]{2,3,1,0:T(8,128)}, u32[]{:S(2)}) copy-start(f32[4,2,256,256]{2,3,1,0:T(8,128)} %copy-done.2) | copy-start | bytes 6291460
  95.2 6.4 %copy-start.20 = (bf16[256,4,128]{2,0,1:T(8,128)(2,1)S(1)}, bf16[256,4,128]{2,0,1:T(8,128)(2,1)}, u32[]{:S(2)}) copy-start(bf16[256,4,128]{2,0,1:T(8,128)(2,1)} %copy-done.19) | copy-start | bytes 786436
  95.2 34.3 %collective-permute-start.14 = (f32[256,4,128]{2,0,1:T(8,128)S(1)}, f32[256,4,128]{2,0,1:T(8,128)S(1)}, u32[]{:S(2)}, u32[]{:S(2)}) collective-permute-start(f32[256,4,128]{2,0,1:T(8,128)S(1)} %convolution_bitcast_fusion.1), channel_id=1, source_target_pairs={{3,0},{4,1},{5,2},{6,3},{7,4},{8,5},{9,6},{10,7},{11,8},{12,9},{13... | collective-permute-start | bytes 1572872 | tf_op jit(solution)/shard_map/ppermute | solution.py:17
  102.1 7.5 %copy-start.18 = (bf16[256,4,128]{2,0,1:T(8,128)(2,1)S(1)}, bf16[256,4,128]{2,0,1:T(8,128)(2,1)}, u32[]{:S(2)}) copy-start(bf16[256,4,128]{2,0,1:T(8,128)(2,1)} %copy-done.17) | copy-start | bytes 786436
  102.1 38.7 %collective-permute-start.15 = (f32[256,4,128]{2,0,1:T(8,128)}, f32[256,4,128]{2,0,1:T(8,128)}, u32[]{:S(2)}, u32[]{:S(2)}) collective-permute-start(f32[256,4,128]{2,0,1:T(8,128)} %convolution_bitcast_fusion), channel_id=1, source_target_pairs={{4,0},{5,1},{6,2},{7,3},{8,4},{9,5},{10,6},{11,7},{12,8},{13,9},{1... | collective-permute-start | bytes 1572872 | tf_op jit(solution)/shard_map/ppermute | solution.py:17
  109.6 1.8 copy-start.22
  111.4 21.3 %copy-start.16 = (bf16[256,4,128]{2,0,1:T(8,128)(2,1)S(1)}, bf16[256,4,128]{2,0,1:T(8,128)(2,1)}, u32[]{:S(2)}) copy-start(bf16[256,4,128]{2,0,1:T(8,128)(2,1)} %copy-done.15) | copy-start | bytes 786436
  113.2 16.3 %copy-start.10 = (f32[256,4,128]{2,0,1:T(8,128)}, f32[256,4,128]{2,0,1:T(8,128)S(1)}, u32[]{:S(2)}) copy-start(f32[256,4,128]{2,0,1:T(8,128)S(1)} %collective-permute-done.13) | copy-start | bytes 1572868
  113.2 75.5 %collective-permute-start.8 = (f32[256,4,128]{2,0,1:T(8,128)}, f32[256,4,128]{2,0,1:T(8,128)}, u32[]{:S(2)}, u32[]{:S(2)}) collective-permute-start(f32[256,4,128]{2,0,1:T(8,128)} %convolution_bitcast_fusion.8), channel_id=1, source_target_pairs={{1,0},{2,1},{3,2},{4,3},{5,4},{6,5},{7,6},{8,7},{9,8},{10,9},{11,1... | collective-permute-start | bytes 1572872 | tf_op jit(solution)/shard_map/ppermute | solution.py:17
  118.3 15.0 %copy-start.12 = (f32[256,4,128]{2,0,1:T(8,128)}, f32[256,4,128]{2,0,1:T(8,128)S(1)}, u32[]{:S(2)}) copy-start(f32[256,4,128]{2,0,1:T(8,128)S(1)} %collective-permute-done.12) | copy-start | bytes 1572868
  118.3 70.4 %collective-permute-start.10 = (f32[256,4,128]{2,0,1:T(8,128)}, f32[256,4,128]{2,0,1:T(8,128)}, u32[]{:S(2)}, u32[]{:S(2)}) collective-permute-start(f32[256,4,128]{2,0,1:T(8,128)} %convolution_bitcast_fusion.6), channel_id=1, source_target_pairs={{3,0},{4,1},{5,2},{6,3},{7,4},{8,5},{9,6},{10,7},{11,8},{12,9},{13... | collective-permute-start | bytes 1572872 | tf_op jit(solution)/shard_map/ppermute | solution.py:17
  129.5 3.8 %copy-start.13 = (f32[256,4,128]{2,0,1:T(8,128)}, f32[256,4,128]{2,0,1:T(8,128)S(1)}, u32[]{:S(2)}) copy-start(f32[256,4,128]{2,0,1:T(8,128)S(1)} %collective-permute-done.14) | copy-start | bytes 1572868
  129.5 59.2 %collective-permute-start.11 = (f32[256,4,128]{2,0,1:T(8,128)}, f32[256,4,128]{2,0,1:T(8,128)}, u32[]{:S(2)}, u32[]{:S(2)}) collective-permute-start(f32[256,4,128]{2,0,1:T(8,128)} %convolution_bitcast_fusion.5), channel_id=1, source_target_pairs={{4,0},{5,1},{6,2},{7,3},{8,4},{9,5},{10,6},{11,7},{12,8},{13,9},{1... | collective-permute-start | bytes 1572872 | tf_op jit(solution)/shard_map/ppermute | solution.py:17
  133.3 7.5 %copy-start.11 = (f32[256,4,128]{2,0,1:T(8,128)S(1)}, f32[256,4,128]{2,0,1:T(8,128)}, u32[]{:S(2)}) copy-start(f32[256,4,128]{2,0,1:T(8,128)} %copy-done.10) | copy-start | bytes 1572868
  134.5 50.8 %all-to-all-start.1 = ((bf16[256,8,128]{2,1,0:T(8,128)(2,1)}), bf16[256,8,128]{2,1,0:T(8,128)(2,1)S(1)}, u32[]{:S(2)}, u32[]{:S(2)}) async-start(bf16[256,8,128]{2,1,0:T(8,128)(2,1)} %copy.63), calls=%async_computation.1 | async-start | bytes 1048576 | tf_op jit(solution)/shard_map/all_to_all | solution.py:139
  185.3 9.4 %all-to-all-start.3 = ((bf16[256,4,128]{2,1,0:T(4,128)(2,1)}), bf16[256,4,128]{2,1,0:T(4,128)(2,1)S(1)}, u32[]{:S(2)}, u32[]{:S(2)}) async-start(bf16[256,4,128]{2,1,0:T(4,128)(2,1)} %copy.72), calls=%async_computation.3 | async-start | bytes 524288 | tf_op jit(solution)/shard_map/all_to_all | solution.py:141
  194.7 9.4 %all-to-all-start.2 = ((bf16[256,4,128]{2,1,0:T(4,128)(2,1)}), bf16[256,4,128]{2,1,0:T(4,128)(2,1)S(1)}, u32[]{:S(2)}, u32[]{:S(2)}) async-start(bf16[256,4,128]{2,1,0:T(4,128)(2,1)} %copy.70), calls=%async_computation.2 | async-start | bytes 524288 | tf_op jit(solution)/shard_map/all_to_all | solution.py:140
where the time goes:
time: 206 us; the launch traced here: 205 us
  waiting for transfers between devices  91.2 us (44%)
  starting transfers between devices  66.2 us (32%)
  matrix products  30.7 us (15%)
  local copies, waits for them, and re-layouts  14.3 us (7%)
    ppermute x16, starting transfers between devices, shifted(): return lax.ppermute(value, axis, pairs)  52.4 us
    ppermute x16, waiting for transfers between devices, shifted(): return lax.ppermute(value, axis, pairs)  42.8 us
    all_to_all x1, waiting for transfers between devices, on_device(): lax.all_to_all(query_grad, 'head', split_axis=0, concat_axis=1, tiled=True)  41.1 us
    dot_general x5, matrix products, tile_terms(): jnp.einsum('ikgd,jkd->kgij', query_part, key_part, preferred_element_type...  8.5 us
    unnamed x53, local copies, waits for them, and re-layouts  7.66 us
    dot_general x5, matrix products, tile_terms(): jnp.einsum('kgij,ikgd->jkd', low_scores, query_part, preferred_element_ty...  6.89 us
    dot_general x5, matrix products, tile_terms(): jnp.einsum('kgij,ikgd->jkd', low_probs, grad_part, preferred_element_type...  6.66 us
    dot_general x5, matrix products, tile_terms(): jnp.einsum('ikgd,jkd->kgij', grad_part, value_part, preferred_element_typ...  6.02 us
  transfers between devices with their start and end apart: 20, of which 10 were waited for; matrix products, arithmetic and copies ran while one was open for 20% of the time, Pallas kernels for 0%

commit v1 on v0

v1 whole, which is shorter than its diff:
```python
import jax
import jax.numpy as jnp
from jax import lax
from jax.sharding import Mesh
from jax.sharding import PartitionSpec as P

WINDOW_LENGTH = 1024
BLOCK = 256

score_scale = 168.0 ** (-0.5)


def shifted(value, axis, by):
    size = lax.axis_size(axis)
    pairs = [(i, i + by) for i in range(size) if 0 <= i + by < size]
    return lax.ppermute(value, axis, pairs)


def band_terms(query, grad, logsum, delta, start, base, keys, values):
    tokens, group, depth = query.shape
    tiles = tokens // BLOCK
    span = WINDOW_LENGTH + BLOCK
    query_t = query.reshape(tiles, BLOCK, group, depth)
    grad_t = grad.reshape(tiles, BLOCK, group, depth)
    logsum_t = logsum.reshape(group, tiles, BLOCK).transpose(1, 0, 2)
    delta_t = delta.reshape(group, tiles, BLOCK).transpose(1, 0, 2)
    start_t = start.reshape(tiles, BLOCK)
    key_w = jnp.stack([keys[t * BLOCK : t * BLOCK + span] for t in range(tiles)])
    value_w = jnp.stack([values[t * BLOCK : t * BLOCK + span] for t in range(tiles)])
    tile_base = base + BLOCK * jnp.arange(tiles, dtype=jnp.int32)
    query_place = tile_base[:, None] + jnp.arange(BLOCK, dtype=jnp.int32)[None, :]
    key_place = tile_base[:, None] - WINDOW_LENGTH + jnp.arange(span, dtype=jnp.int32)[None, :]
    gap = query_place[:, :, None] - key_place[:, None, :]
    visible = (gap >= 0) & (gap < WINDOW_LENGTH) & (key_place[:, None, :] >= start_t[:, :, None])
    scores = (
        jnp.einsum("tigd,tjd->tgij", query_t, key_w, preferred_element_type=jnp.float32)
        * score_scale
    )
    probs = jnp.where(visible[:, None], jnp.exp(scores - logsum_t[..., None]), 0.0)
    dprobs = jnp.einsum("tigd,tjd->tgij", grad_t, value_w, preferred_element_type=jnp.float32)
    low_scores = (probs * (dprobs - delta_t[..., None])).astype(jnp.bfloat16)
    low_probs = probs.astype(jnp.bfloat16)
    query_term = jnp.einsum("tgij,tjd->tigd", low_scores, key_w, preferred_element_type=jnp.float32)
    key_w_term = jnp.einsum("tgij,tigd->tjd", low_scores, query_t, preferred_element_type=jnp.float32)
    value_w_term = jnp.einsum("tgij,tigd->tjd", low_probs, grad_t, preferred_element_type=jnp.float32)
    total = WINDOW_LENGTH + tokens
    key_term = jnp.zeros((total, depth), jnp.float32)
    value_term = jnp.zeros((total, depth), jnp.float32)
    for t in range(tiles):
        key_term = key_term.at[t * BLOCK : t * BLOCK + span].add(key_w_term[t])
        value_term = value_term.at[t * BLOCK : t * BLOCK + span].add(value_w_term[t])
    return query_term.reshape(tokens, group, depth), key_term, value_term


def on_device(
    queries, normed_keys, value_matrix, forward_out, output_gradient, row_log_total, pair_start
):
    grad_rows = lax.all_to_all(output_gradient, "head", split_axis=1, concat_axis=0, tiled=True)
    delta_rows = jnp.einsum(
        "thd,thd->ht", forward_out, grad_rows, preferred_element_type=jnp.float32
    )
    ring = lax.axis_size("sl")
    query_g = lax.all_to_all(queries, "sl", split_axis=1, concat_axis=0, tiled=True)
    grad_g = lax.all_to_all(grad_rows, "sl", split_axis=1, concat_axis=0, tiled=True)
    key_g = lax.all_to_all(normed_keys, "sl", split_axis=1, concat_axis=0, tiled=True)
    value_g = lax.all_to_all(value_matrix, "sl", split_axis=1, concat_axis=0, tiled=True)
    logsum_g = lax.all_to_all(row_log_total, "sl", split_axis=0, concat_axis=1, tiled=True)
    delta_g = lax.all_to_all(delta_rows, "sl", split_axis=0, concat_axis=1, tiled=True)
    start_g = lax.all_gather(pair_start, "sl", axis=0, tiled=True)
    tokens, group, depth = query_g.shape
    base = lax.axis_index("sh") * tokens
    key_own = key_g[:, 0]
    value_own = value_g[:, 0]
    key_far = shifted(key_own, "sh", 1)
    value_far = shifted(value_own, "sh", 1)
    keys = jnp.concatenate([key_far, key_own], axis=0)
    values = jnp.concatenate([value_far, value_own], axis=0)
    query_sum, key_sum, value_sum = band_terms(
        query_g, grad_g, logsum_g, delta_g, start_g, base, keys, values
    )
    key_back = shifted(key_sum[:WINDOW_LENGTH], "sh", -1)
    value_back = shifted(value_sum[:WINDOW_LENGTH], "sh", -1)
    key_total = key_sum[WINDOW_LENGTH:] + key_back
    value_total = value_sum[WINDOW_LENGTH:] + value_back
    query_grad = (query_sum * score_scale).astype(jnp.bfloat16)
    key_grad = (key_total * score_scale).astype(jnp.bfloat16)[:, None]
    value_grad = value_total.astype(jnp.bfloat16)[:, None]

    def back(x):
        x = lax.all_to_all(x, "sl", split_axis=0, concat_axis=1, tiled=True)
        return lax.all_to_all(x, "head", split_axis=0, concat_axis=1, tiled=True)

    return back(query_grad), back(key_grad), back(value_grad)


def solution(mesh):
    head, seq = mesh.devices.shape
    ring = WINDOW_LENGTH // BLOCK
    grouped = Mesh(mesh.devices.reshape(head, seq // ring, ring), ("head", "sh", "sl"))
    seq_axes = ("sh", "sl")
    placed = (
        P(seq_axes, "head", None),
        P(seq_axes, "head", None),
        P(seq_axes, "head", None),
        P(seq_axes, "head", None),
        P(seq_axes + ("head",), None, None),
        P("head", seq_axes),
        P(seq_axes),
    )
    out = P(seq_axes + ("head",), None, None)
    return jax.shard_map(
        on_device,
        mesh=grouped,
        in_specs=placed,
        out_specs=(out, out, out),
        check_vma=False,
    )
```

time: 206 us -> 183 us (0.89)
  the two profiles are of different devices: /device:TPU:484 before, /device:TPU:4 now
where the time goes in v1:
time: 183 us; the launch traced here: 182 us
  starting transfers between devices  66.9 us (37%)
  waiting for transfers between devices  47.6 us (26%)
  local copies, waits for them, and re-layouts  22.3 us (12%)
  matrix products  20.6 us (11%)
  other arithmetic  12.9 us (7%)
  blocking collectives  10.4 us (6%)
    ppermute x4, starting transfers between devices, shifted(): return lax.ppermute(value, axis, pairs)  19 us
    all_to_all x3, waiting for transfers between devices, back(): return lax.all_to_all(x, 'head', split_axis=0, concat_axis=1, tiled=True)  16.6 us
    all_to_all x3, waiting for transfers between devices, back(): x = lax.all_to_all(x, 'sl', split_axis=0, concat_axis=1, tiled=True)  14.2 us
    all_to_all x3, starting transfers between devices, back(): x = lax.all_to_all(x, 'sl', split_axis=0, concat_axis=1, tiled=True)  11.6 us
    all_gather x1, blocking collectives, on_device(): start_g = lax.all_gather(pair_start, 'sl', axis=0, tiled=True)  10.4 us
    all_to_all x3, starting transfers between devices, back(): return lax.all_to_all(x, 'head', split_axis=0, concat_axis=1, tiled=True)  10.3 us
    unnamed x25, local copies, waits for them, and re-layouts  9.52 us
    all_to_all x1, waiting for transfers between devices, on_device(): lax.all_to_all(value_matrix, 'sl', split_axis=1, concat_axis=0, tiled=True)  6.65 us
  transfers between devices with their start and end apart: 17, of which 10 were waited for; matrix products, arithmetic and copies ran while one was open for 29% of the time, Pallas kernels for 0%

profile of v1, /device:TPU:4, one launch (start us, length us, event | category | flops | bytes accessed | tf_op | source)
XLA Modules:
  0.0 181.9 jit_solution(7914831301998009179)
XLA Ops:
  0.6 1.7 copy.58
  2.3 4.5 %all-to-all-start = ((bf16[256,4,128]{2,0,1:T(8,128)(2,1)}), bf16[256,4,128]{2,0,1:T(8,128)(2,1)S(1)}, u32[]{:S(2)}, u32[]{:S(2)}) async-start(bf16[256,4,128]{2,0,1:T(8,128)(2,1)} %copy.58), calls=%async_computation | async-start | bytes 524288 | tf_op jit(solution)/shard_map/all_to_all | solution.py:65
  6.9 10.4 %all-gather = s32[4,1,256]{2,1,0:T(1,128)S(1)} all-gather(s32[1,1,256]{2,1,0:T(1,128)} %bitcast.178), channel_id=1, replica_groups=mesh['head'=4,'sh'=32,'sl'=4] {'sl'}, dimensions={0}, use_global_device_ids=true | all-gather | bytes 5120 | tf_op jit(solution)/shard_map/all_gather | solution.py:69
  17.3 2.1 %copy.61 = bf16[64,32,128]{2,0,1:T(8,128)(2,1)} copy(bf16[64,32,128]{2,1,0:T(8,128)(2,1)} %param.27) | data formatting | bytes 1048576 | tf_op args[4]
  19.4 1.7 copy.60
  21.1 4.0 %all-to-all-start.3 = ((bf16[256,4,128]{2,0,1:T(8,128)(2,1)}), bf16[256,4,128]{2,0,1:T(8,128)(2,1)}, u32[]{:S(2)}, u32[]{:S(2)}) async-start(bf16[256,4,128]{2,0,1:T(8,128)(2,1)} %copy.60), calls=%async_computation.3 | async-start | bytes 524288 | tf_op jit(solution)/shard_map/all_to_all | solution.py:66
  25.2 6.7 %all-to-all-done.3 = bf16[256,4,128]{2,0,1:T(8,128)(2,1)} async-done(((bf16[256,4,128]{2,0,1:T(8,128)(2,1)}), bf16[256,4,128]{2,0,1:T(8,128)(2,1)}, u32[]{:S(2)}, u32[]{:S(2)}) %all-to-all-start.3) | async-done | bytes 262176 | tf_op jit(solution)/shard_map/all_to_all | solution.py:66
  31.8 3.5 %all-to-all-start.4 = ((bf16[64,32,128]{2,0,1:T(8,128)(2,1)}), bf16[64,32,128]{2,0,1:T(8,128)(2,1)S(1)}, u32[]{:S(2)}, u32[]{:S(2)}) async-start(bf16[64,32,128]{2,0,1:T(8,128)(2,1)} %copy.61), calls=%async_computation.4 | async-start | bytes 1048576 | tf_op jit(solution)/shard_map/all_to_all | solution.py:58
  35.3 1.9 %fusion.11 = pred[4,256,1280]{1,2,0:T(8,128)(4,1)S(1)} fusion(s32[4,256]{1,0:T(4,128)S(1)} %bitcast.177, s32[4,1280]{1,0:T(4,128)S(1)} %iota_add_fusion, s32[4,256]{1,0:T(4,128)S(1)} %iota_add_fusion.1), kind=kLoop, calls=%fused_computation.14 | loop fusion | flops 7864320 | bytes 1339392 | tf_op jit(solution)/shard_map/and | solution.py:34
  37.2 3.8 %collective-permute-start = (bf16[1024,128]{1,0:T(8,128)(2,1)S(1)}, bf16[1024,128]{1,0:T(8,128)(2,1)}, u32[]{:S(2)}, u32[]{:S(2)}) collective-permute-start(bf16[1024,128]{1,0:T(8,128)(2,1)S(1)} %bitcast.168), channel_id=1, source_target_pairs={{0,4},{4,8},{8,12},{12,16},{16,20},{20,24},{24,28},{28,32},{32,36}... | collective-permute-start | bytes 786440 | tf_op jit(solution)/shard_map/ppermute | solution.py:16
  41.0 1.1 bitcast_convert_fusion
  42.1 1.9 %copy.59 = bf16[256,8,128]{2,0,1:T(8,128)(2,1)} copy(bf16[256,8,128]{2,1,0:T(8,128)(2,1)} %param.23) | data formatting | bytes 1048576 | tf_op args[0]
  44.1 0.6 all_to_all.161
  44.7 3.8 %collective-permute-start.1 = (bf16[1024,128]{1,0:T(8,128)(2,1)}, bf16[1024,128]{1,0:T(8,128)(2,1)}, u32[]{:S(2)}, u32[]{:S(2)}) collective-permute-start(bf16[1024,128]{1,0:T(8,128)(2,1)} %bitcast.18), channel_id=1, source_target_pairs={{0,4},{4,8},{8,12},{12,16},{16,20},{20,24},{24,28},{28,32},{32,36}... | collective-permute-start | bytes 786440 | tf_op jit(solution)/shard_map/ppermute | solution.py:16
  48.5 3.2 %all-to-all-start.2 = ((f32[4,2,256]{2,1,0:T(2,128)}), f32[4,2,256]{2,1,0:T(2,128)S(1)}, u32[]{:S(2)}, u32[]{:S(2)}) async-start(f32[4,2,256]{2,1,0:T(2,128)} %all_to_all.161), calls=%async_computation.2 | async-start | bytes 16384 | tf_op jit(solution)/shard_map/all_to_all | solution.py:67
  51.7 0.9 copy.62
  52.6 1.4 multiply_reduce_fusion
  54.0 0.6 all_to_all.173
  54.6 2.4 %all-to-all-done.2 = f32[4,2,256]{2,1,0:T(2,128)S(1)} async-done(((f32[4,2,256]{2,1,0:T(2,128)}), f32[4,2,256]{2,1,0:T(2,128)S(1)}, u32[]{:S(2)}, u32[]{:S(2)}) %all-to-all-start.2) | async-done | bytes 8224 | tf_op jit(solution)/shard_map/all_to_all | solution.py:67
  57.0 3.5 %all-to-all-start.1 = ((bf16[256,8,128]{2,0,1:T(8,128)(2,1)}), bf16[256,8,128]{2,0,1:T(8,128)(2,1)S(1)}, u32[]{:S(2)}, u32[]{:S(2)}) async-start(bf16[256,8,128]{2,0,1:T(8,128)(2,1)} %copy.59), calls=%async_computation.1 | async-start | bytes 1048576 | tf_op jit(solution)/shard_map/all_to_all | solution.py:63
  60.5 1.3 fusion.47
  61.8 2.5 %fusion.41 = (bf16[1,1280,128]{2,1,0:T(8,128)(2,1)S(1)}, bf16[1,1280,128]{2,1,0:T(8,128)(2,1)}, bf16[1,1280,128]{2,1,0:T(8,128)(2,1)}, bf16[1,1280,128]{2,1,0:T(8,128)(2,1)}) fusion(bf16[1024,128]{1,0:T(8,128)(2,1)} %collective-permute-done.1, bf16[1024,128]{1,0:T(8,128)(2,1)} %bitcast.18), kind=kLoop, calls=%fused_computation.71 | loop fusion | flops 2621440 | bytes 1835008 | tf_op jit(solution)/shard_map/stack | solution.py:29
  64.4 5.2 %all-to-all-done.1 = bf16[256,8,128]{2,0,1:T(8,128)(2,1)S(1)} async-done(((bf16[256,8,128]{2,0,1:T(8,128)(2,1)}), bf16[256,8,128]{2,0,1:T(8,128)(2,1)S(1)}, u32[]{:S(2)}, u32[]{:S(2)}) %all-to-all-start.1) | async-done | bytes 524320 | tf_op jit(solution)/shard_map/all_to_all | solution.py:63
  69.5 4.1 %all-to-all-start.5 = ((bf16[256,8,128]{2,0,1:T(8,128)(2,1)}), bf16[256,8,128]{2,0,1:T(8,128)(2,1)}, u32[]{:S(2)}, u32[]{:S(2)}) async-start(bf16[256,8,128]{2,0,1:T(8,128)(2,1)} %bitcast.27), calls=%async_computation.5 | async-start | bytes 1048576 | tf_op jit(solution)/shard_map/all_to_all | solution.py:64
  73.7 5.5 %fusion.34 = f32[4,1280,256,2]{2,1,3,0:T(8,128)} fusion(bf16[4,256,2,128]{3,1,2,0:T(8,128)(2,1)S(1)} %bitcast.161, bf16[1,1280,128]{2,1,0:T(8,128)(2,1)S(1)} %get-tuple-element.105, bf16[1,1280,128]{2,1,0:T(8,128)(2,1)S(1)} %get-tuple-element.106, bf16[1,1280,128]{2,1,0:T(8,128)(2,1)S(1)} %get-tuple-element.104, ...), kind=kOutput, calls=%fused_computation.60 | convolution fusion | flops 676331520 | bytes 12320768 | tf_op jit(solution)/shard_map/tigd,tjd->tgij/dot_general | solution.py:36
  79.2 2.6 %all-to-all-done.5 = bf16[256,8,128]{2,0,1:T(8,128)(2,1)} async-done(((bf16[256,8,128]{2,0,1:T(8,128)(2,1)}), bf16[256,8,128]{2,0,1:T(8,128)(2,1)}, u32[]{:S(2)}, u32[]{:S(2)}) %all-to-all-start.5) | async-done | bytes 524320 | tf_op jit(solution)/shard_map/all_to_all | solution.py:64
  81.8 3.2 %all-to-all-start.6 = ((f32[4,2,256]{2,1,0:T(2,128)}), f32[4,2,256]{2,1,0:T(2,128)S(1)}, u32[]{:S(2)}, u32[]{:S(2)}) async-start(f32[4,2,256]{2,1,0:T(2,128)} %all_to_all.173), calls=%async_computation.6 | async-start | bytes 16384 | tf_op jit(solution)/shard_map/all_to_all | solution.py:68
  85.1 5.6 %fusion.13 = f32[4,1280,128]{2,1,0:T(8,128)S(1)} fusion(bf16[4,256,2,128]{3,1,2,0:T(8,128)(2,1)} %bitcast.29, f32[4,1280,256,2]{2,1,3,0:T(8,128)} %fusion.34, f32[4,2,256]{2,1,0:T(2,128)S(1)} %all-to-all-done.2, pred[4,256,1280]{1,2,0:T(8,128)(4,1)S(1)} %fusion.11), kind=kOutput, calls=%fused_computation.16 | convolution fusion | flops 681574400 | bytes 14950400 | tf_op jit(solution)/shard_map/tgij,tigd->tjd/dot_general | solution.py:45
  91.2 0.8 slice.261
  92.0 7.7 %collective-permute-start.3 = (f32[1024,128]{1,0:T(8,128)}, f32[1024,128]{1,0:T(8,128)}, u32[]{:S(2)}, u32[]{:S(2)}) collective-permute-start(f32[1024,128]{1,0:T(8,128)} %slice.261), channel_id=1, source_target_pairs={{4,0},{8,4},{12,8},{16,12},{20,16},{24,20},{28,24},{32,28},{36,32}... | collective-permute-start | bytes 1572872 | tf_op jit(solution)/shard_map/ppermute | solution.py:16
  99.8 6.2 %fusion.1 = bf16[4,2,256,1280]{2,3,1,0:T(8,128)(2,1)S(1)} fusion(f32[4,1280,256,2]{2,1,3,0:T(8,128)} %fusion.34, bf16[4,256,2,128]{3,1,2,0:T(8,128)(2,1)} %bitcast.29, f32[4,2,256]{2,1,0:T(2,128)S(1)} %all-to-all-done.6, f32[4,2,256]{2,1,0:T(2,128)S(1)} %all-to-all-done.2, pred[4,256,1280]{1,2,0:T(8,128)(4,1)S(1)} %fusion.11, ...), kind=kOutput, calls=%fused_computation.2 | convolution fusion | flops 692060160 | bytes 18890752 | tf_op jit(solution)/shard_map/tigd,tjd->tgij/dot_general | solution.py:40
  106.0 1.5 convolution_bitcast_fusion
  108.1 0.8 slice.253
  108.9 3.6 %collective-permute-start.2 = (f32[1024,128]{1,0:T(8,128)}, f32[1024,128]{1,0:T(8,128)}, u32[]{:S(2)}, u32[]{:S(2)}) collective-permute-start(f32[1024,128]{1,0:T(8,128)} %slice.253), channel_id=1, source_target_pairs={{4,0},{8,4},{12,8},{16,12},{20,16},{24,20},{28,24},{32,28},{36,32}... | collective-permute-start | bytes 1572872 | tf_op jit(solution)/shard_map/ppermute | solution.py:16
  112.6 1.7 fusion.23
  114.4 1.3 copy.65
  115.7 1.3 copy.66
  117.0 4.8 %all-to-all-start.7 = ((bf16[1024,2,128]{2,1,0:T(2,128)(2,1)}), bf16[1024,2,128]{2,1,0:T(2,128)(2,1)S(1)}, u32[]{:S(2)}, u32[]{:S(2)}) async-start(bf16[1024,2,128]{2,1,0:T(2,128)(2,1)} %copy.66), calls=%async_computation.7 | async-start | bytes 1048576 | tf_op jit(solution)/shard_map/all_to_all | solution.py:90
  121.8 1.1 fusion.53
  122.9 0.5 broadcast.185
  123.4 0.8 reduce.19
  124.2 0.8 reshape.299
  125.0 4.9 %all-to-all-done.7 = bf16[1024,2,128]{2,1,0:T(2,128)(2,1)S(1)} async-done(((bf16[1024,2,128]{2,1,0:T(2,128)(2,1)}), bf16[1024,2,128]{2,1,0:T(2,128)(2,1)S(1)}, u32[]{:S(2)}, u32[]{:S(2)}) %all-to-all-start.7) | async-done | bytes 524320 | tf_op jit(solution)/shard_map/all_to_all | solution.py:90
  129.8 3.4 %all-to-all-start.11 = ((bf16[4,2,16384]{2,1,0:T(2,128)(2,1)}), bf16[4,2,16384]{2,1,0:T(2,128)(2,1)S(1)}, u32[]{:S(2)}, u32[]{:S(2)}) async-start(bf16[4,2,16384]{2,1,0:T(2,128)(2,1)} %reshape.299), calls=%async_computation.11 | async-start | bytes 524288 | tf_op jit(solution)/shard_map/all_to_all | solution.py:90
  133.3 1.1 fusion.52
  134.4 0.8 reduce.18
  135.2 0.8 reshape.297
  136.0 3.9 %all-to-all-done.11 = bf16[4,2,16384]{2,1,0:T(2,128)(2,1)S(1)} async-done(((bf16[4,2,16384]{2,1,0:T(2,128)(2,1)}), bf16[4,2,16384]{2,1,0:T(2,128)(2,1)S(1)}, u32[]{:S(2)}, u32[]{:S(2)}) %all-to-all-start.11) | async-done | bytes 262176 | tf_op jit(solution)/shard_map/all_to_all | solution.py:90
  139.9 3.4 %all-to-all-start.9 = ((bf16[4,2,16384]{2,1,0:T(2,128)(2,1)}), bf16[4,2,16384]{2,1,0:T(2,128)(2,1)S(1)}, u32[]{:S(2)}, u32[]{:S(2)}) async-start(bf16[4,2,16384]{2,1,0:T(2,128)(2,1)} %reshape.297), calls=%async_computation.9 | async-start | bytes 524288 | tf_op jit(solution)/shard_map/all_to_all | solution.py:90
  143.4 1.1 copy.69
  144.6 5.4 %all-to-all-done.9 = bf16[4,2,16384]{2,1,0:T(2,128)(2,1)S(1)} async-done(((bf16[4,2,16384]{2,1,0:T(2,128)(2,1)}), bf16[4,2,16384]{2,1,0:T(2,128)(2,1)S(1)}, u32[]{:S(2)}, u32[]{:S(2)}) %all-to-all-start.9) | async-done | bytes 262176 | tf_op jit(solution)/shard_map/all_to_all | solution.py:90
  150.0 3.5 %all-to-all-start.8 = ((bf16[256,8,128]{2,1,0:T(8,128)(2,1)}), bf16[256,8,128]{2,1,0:T(8,128)(2,1)S(1)}, u32[]{:S(2)}, u32[]{:S(2)}) async-start(bf16[256,8,128]{2,1,0:T(8,128)(2,1)} %copy.69), calls=%async_computation.8 | async-start | bytes 1048576 | tf_op jit(solution)/shard_map/all_to_all | solution.py:91
  153.5 0.3 reshape.300
  153.8 0.9 copy.75
  154.7 7.6 %all-to-all-done.8 = bf16[256,8,128]{2,1,0:T(8,128)(2,1)S(1)} async-done(((bf16[256,8,128]{2,1,0:T(8,128)(2,1)}), bf16[256,8,128]{2,1,0:T(8,128)(2,1)S(1)}, u32[]{:S(2)}, u32[]{:S(2)}) %all-to-all-start.8) | async-done | bytes 524320 | tf_op jit(solution)/shard_map/all_to_all | solution.py:91
  162.3 3.4 %all-to-all-start.12 = ((bf16[256,4,128]{2,1,0:T(4,128)(2,1)}), bf16[256,4,128]{2,1,0:T(4,128)(2,1)S(1)}, u32[]{:S(2)}, u32[]{:S(2)}) async-start(bf16[256,4,128]{2,1,0:T(4,128)(2,1)} %copy.75), calls=%async_computation.12 | async-start | bytes 524288 | tf_op jit(solution)/shard_map/all_to_all | solution.py:91
  165.7 0.3 reshape.298
  166.0 0.9 copy.72
  166.9 4.7 %all-to-all-done.12 = bf16[256,4,128]{2,1,0:T(4,128)(2,1)S(1)} async-done(((bf16[256,4,128]{2,1,0:T(4,128)(2,1)}), bf16[256,4,128]{2,1,0:T(4,128)(2,1)S(1)}, u32[]{:S(2)}, u32[]{:S(2)}) %all-to-all-start.12) | async-done | bytes 262176 | tf_op jit(solution)/shard_map/all_to_all | solution.py:91
  171.7 3.4 %all-to-all-start.10 = ((bf16[256,4,128]{2,1,0:T(4,128)(2,1)}), bf16[256,4,128]{2,1,0:T(4,128)(2,1)S(1)}, u32[]{:S(2)}, u32[]{:S(2)}) async-start(bf16[256,4,128]{2,1,0:T(4,128)(2,1)} %copy.72), calls=%async_computation.10 | async-start | bytes 524288 | tf_op jit(solution)/shard_map/all_to_all | solution.py:91
  175.1 0.9 copy.97
  176.0 0.8 copy.76
  176.8 4.3 %all-to-all-done.10 = bf16[256,4,128]{2,1,0:T(4,128)(2,1)S(1)} async-done(((bf16[256,4,128]{2,1,0:T(4,128)(2,1)}), bf16[256,4,128]{2,1,0:T(4,128)(2,1)S(1)}, u32[]{:S(2)}, u32[]{:S(2)}) %all-to-all-start.10) | async-done | bytes 262176 | tf_op jit(solution)/shard_map/all_to_all | solution.py:91
  181.1 0.8 copy.73
  (41 shorter events, 1.4 us)
Async XLA Ops:
  2.3 18.7 %all-to-all-start = ((bf16[256,4,128]{2,0,1:T(8,128)(2,1)}), bf16[256,4,128]{2,0,1:T(8,128)(2,1)S(1)}, u32[]{:S(2)}, u32[]{:S(2)}) async-start(bf16[256,4,128]{2,0,1:T(8,128)(2,1)} %copy.58), calls=%async_computation | async-start | bytes 524288 | tf_op jit(solution)/shard_map/all_to_all | solution.py:65
  21.1 23.0 %copy-start.4 = (bf16[256,4,128]{2,0,1:T(8,128)(2,1)}, bf16[256,4,128]{2,0,1:T(8,128)(2,1)S(1)}, u32[]{:S(2)}) copy-start(bf16[256,4,128]{2,0,1:T(8,128)(2,1)S(1)} %all-to-all-done) | copy-start | bytes 786436
  21.1 10.8 %all-to-all-start.3 = ((bf16[256,4,128]{2,0,1:T(8,128)(2,1)}), bf16[256,4,128]{2,0,1:T(8,128)(2,1)}, u32[]{:S(2)}, u32[]{:S(2)}) async-start(bf16[256,4,128]{2,0,1:T(8,128)(2,1)} %copy.60), calls=%async_computation.3 | async-start | bytes 524288 | tf_op jit(solution)/shard_map/all_to_all | solution.py:66
  25.1 18.9 %copy-start.6 = (f32[8,256]{1,0:T(8,128)S(1)}, f32[8,256]{1,0:T(8,128)}, u32[]{:S(2)}) copy-start(f32[8,256]{1,0:T(8,128)} %param.28) | copy-start | bytes 24580
  31.8 16.6 %all-to-all-start.4 = ((bf16[64,32,128]{2,0,1:T(8,128)(2,1)}), bf16[64,32,128]{2,0,1:T(8,128)(2,1)S(1)}, u32[]{:S(2)}, u32[]{:S(2)}) async-start(bf16[64,32,128]{2,0,1:T(8,128)(2,1)} %copy.61), calls=%async_computation.4 | async-start | bytes 1048576 | tf_op jit(solution)/shard_map/all_to_all | solution.py:58
  37.2 23.3 %collective-permute-start = (bf16[1024,128]{1,0:T(8,128)(2,1)S(1)}, bf16[1024,128]{1,0:T(8,128)(2,1)}, u32[]{:S(2)}, u32[]{:S(2)}) collective-permute-start(bf16[1024,128]{1,0:T(8,128)(2,1)S(1)} %bitcast.168), channel_id=1, source_target_pairs={{0,4},{4,8},{8,12},{12,16},{16,20},{20,24},{24,28},{28,32},{32,36}... | collective-permute-start | bytes 786440 | tf_op jit(solution)/shard_map/ppermute | solution.py:16
  44.7 17.2 %collective-permute-start.1 = (bf16[1024,128]{1,0:T(8,128)(2,1)}, bf16[1024,128]{1,0:T(8,128)(2,1)}, u32[]{:S(2)}, u32[]{:S(2)}) collective-permute-start(bf16[1024,128]{1,0:T(8,128)(2,1)} %bitcast.18), channel_id=1, source_target_pairs={{0,4},{4,8},{8,12},{12,16},{16,20},{20,24},{24,28},{28,32},{32,36}... | collective-permute-start | bytes 786440 | tf_op jit(solution)/shard_map/ppermute | solution.py:16
  48.5 8.5 %all-to-all-start.2 = ((f32[4,2,256]{2,1,0:T(2,128)}), f32[4,2,256]{2,1,0:T(2,128)S(1)}, u32[]{:S(2)}, u32[]{:S(2)}) async-start(f32[4,2,256]{2,1,0:T(2,128)} %all_to_all.161), calls=%async_computation.2 | async-start | bytes 16384 | tf_op jit(solution)/shard_map/all_to_all | solution.py:67
  52.6 7.9 %copy-start.5 = (bf16[256,4,128]{2,0,1:T(8,128)(2,1)S(1)}, bf16[256,4,128]{2,0,1:T(8,128)(2,1)}, u32[]{:S(2)}) copy-start(bf16[256,4,128]{2,0,1:T(8,128)(2,1)} %copy-done.4) | copy-start | bytes 786436
  57.0 12.5 %all-to-all-start.1 = ((bf16[256,8,128]{2,0,1:T(8,128)(2,1)}), bf16[256,8,128]{2,0,1:T(8,128)(2,1)S(1)}, u32[]{:S(2)}, u32[]{:S(2)}) async-start(bf16[256,8,128]{2,0,1:T(8,128)(2,1)} %copy.59), calls=%async_computation.1 | async-start | bytes 1048576 | tf_op jit(solution)/shard_map/all_to_all | solution.py:63
  61.8 17.4 %copy-start = (bf16[1,1280,128]{2,1,0:T(8,128)(2,1)}, bf16[1,1280,128]{2,1,0:T(8,128)(2,1)S(1)}, u32[]{:S(2)}) copy-start(bf16[1,1280,128]{2,1,0:T(8,128)(2,1)S(1)} %get-tuple-element.105) | copy-start | bytes 983044
  61.8 17.4 %copy-start.2 = (bf16[1,1280,128]{2,1,0:T(8,128)(2,1)}, bf16[1,1280,128]{2,1,0:T(8,128)(2,1)S(1)}, u32[]{:S(2)}) copy-start(bf16[1,1280,128]{2,1,0:T(8,128)(2,1)S(1)} %get-tuple-element.106) | copy-start | bytes 983044
  69.5 12.3 %all-to-all-start.5 = ((bf16[256,8,128]{2,0,1:T(8,128)(2,1)}), bf16[256,8,128]{2,0,1:T(8,128)(2,1)}, u32[]{:S(2)}, u32[]{:S(2)}) async-start(bf16[256,8,128]{2,0,1:T(8,128)(2,1)} %bitcast.27), calls=%async_computation.5 | async-start | bytes 1048576 | tf_op jit(solution)/shard_map/all_to_all | solution.py:64
  81.8 17.9 %all-to-all-start.6 = ((f32[4,2,256]{2,1,0:T(2,128)}), f32[4,2,256]{2,1,0:T(2,128)S(1)}, u32[]{:S(2)}, u32[]{:S(2)}) async-start(f32[4,2,256]{2,1,0:T(2,128)} %all_to_all.173), calls=%async_computation.6 | async-start | bytes 16384 | tf_op jit(solution)/shard_map/all_to_all | solution.py:68
  92.0 29.7 %collective-permute-start.3 = (f32[1024,128]{1,0:T(8,128)}, f32[1024,128]{1,0:T(8,128)}, u32[]{:S(2)}, u32[]{:S(2)}) collective-permute-start(f32[1024,128]{1,0:T(8,128)} %slice.261), channel_id=1, source_target_pairs={{4,0},{8,4},{12,8},{16,12},{20,16},{24,20},{28,24},{32,28},{36,32}... | collective-permute-start | bytes 1572872 | tf_op jit(solution)/shard_map/ppermute | solution.py:16
  107.9 4.7 %copy-start.1 = (bf16[1,1280,128]{2,1,0:T(8,128)(2,1)S(1)}, bf16[1,1280,128]{2,1,0:T(8,128)(2,1)}, u32[]{:S(2)}) copy-start(bf16[1,1280,128]{2,1,0:T(8,128)(2,1)} %copy-done) | copy-start | bytes 983044
  107.9 4.7 %copy-start.3 = (bf16[1,1280,128]{2,1,0:T(8,128)(2,1)S(1)}, bf16[1,1280,128]{2,1,0:T(8,128)(2,1)}, u32[]{:S(2)}) copy-start(bf16[1,1280,128]{2,1,0:T(8,128)(2,1)} %copy-done.2) | copy-start | bytes 983044
  108.9 24.3 %collective-permute-start.2 = (f32[1024,128]{1,0:T(8,128)}, f32[1024,128]{1,0:T(8,128)}, u32[]{:S(2)}, u32[]{:S(2)}) collective-permute-start(f32[1024,128]{1,0:T(8,128)} %slice.253), channel_id=1, source_target_pairs={{4,0},{8,4},{12,8},{16,12},{20,16},{24,20},{28,24},{32,28},{36,32}... | collective-permute-start | bytes 1572872 | tf_op jit(solution)/shard_map/ppermute | solution.py:16
  117.0 12.8 %all-to-all-start.7 = ((bf16[1024,2,128]{2,1,0:T(2,128)(2,1)}), bf16[1024,2,128]{2,1,0:T(2,128)(2,1)S(1)}, u32[]{:S(2)}, u32[]{:S(2)}) async-start(bf16[1024,2,128]{2,1,0:T(2,128)(2,1)} %copy.66), calls=%async_computation.7 | async-start | bytes 1048576 | tf_op jit(solution)/shard_map/all_to_all | solution.py:90
  129.8 10.1 %all-to-all-start.11 = ((bf16[4,2,16384]{2,1,0:T(2,128)(2,1)}), bf16[4,2,16384]{2,1,0:T(2,128)(2,1)S(1)}, u32[]{:S(2)}, u32[]{:S(2)}) async-start(bf16[4,2,16384]{2,1,0:T(2,128)(2,1)} %reshape.299), calls=%async_computation.11 | async-start | bytes 524288 | tf_op jit(solution)/shard_map/all_to_all | solution.py:90
  139.9 10.1 %all-to-all-start.9 = ((bf16[4,2,16384]{2,1,0:T(2,128)(2,1)}), bf16[4,2,16384]{2,1,0:T(2,128)(2,1)S(1)}, u32[]{:S(2)}, u32[]{:S(2)}) async-start(bf16[4,2,16384]{2,1,0:T(2,128)(2,1)} %reshape.297), calls=%async_computation.9 | async-start | bytes 524288 | tf_op jit(solution)/shard_map/all_to_all | solution.py:90
  150.0 12.3 %all-to-all-start.8 = ((bf16[256,8,128]{2,1,0:T(8,128)(2,1)}), bf16[256,8,128]{2,1,0:T(8,128)(2,1)S(1)}, u32[]{:S(2)}, u32[]{:S(2)}) async-start(bf16[256,8,128]{2,1,0:T(8,128)(2,1)} %copy.69), calls=%async_computation.8 | async-start | bytes 1048576 | tf_op jit(solution)/shard_map/all_to_all | solution.py:91
  162.3 9.4 %all-to-all-start.12 = ((bf16[256,4,128]{2,1,0:T(4,128)(2,1)}), bf16[256,4,128]{2,1,0:T(4,128)(2,1)S(1)}, u32[]{:S(2)}, u32[]{:S(2)}) async-start(bf16[256,4,128]{2,1,0:T(4,128)(2,1)} %copy.75), calls=%async_computation.12 | async-start | bytes 524288 | tf_op jit(solution)/shard_map/all_to_all | solution.py:91
  171.7 9.4 %all-to-all-start.10 = ((bf16[256,4,128]{2,1,0:T(4,128)(2,1)}), bf16[256,4,128]{2,1,0:T(4,128)(2,1)S(1)}, u32[]{:S(2)}, u32[]{:S(2)}) async-start(bf16[256,4,128]{2,1,0:T(4,128)(2,1)} %copy.72), calls=%async_computation.10 | async-start | bytes 524288 | tf_op jit(solution)/shard_map/all_to_all | solution.py:91

commit v2 on v1

--- a/solution.py
+++ b/solution.py
@@ -60,37 +60,64 @@
         "thd,thd->ht", forward_out, grad_rows, preferred_element_type=jnp.float32
     )
     ring = lax.axis_size("sl")
-    query_g = lax.all_to_all(queries, "sl", split_axis=1, concat_axis=0, tiled=True)
-    grad_g = lax.all_to_all(grad_rows, "sl", split_axis=1, concat_axis=0, tiled=True)
-    key_g = lax.all_to_all(normed_keys, "sl", split_axis=1, concat_axis=0, tiled=True)
-    value_g = lax.all_to_all(value_matrix, "sl", split_axis=1, concat_axis=0, tiled=True)
-    logsum_g = lax.all_to_all(row_log_total, "sl", split_axis=0, concat_axis=1, tiled=True)
-    delta_g = lax.all_to_all(delta_rows, "sl", split_axis=0, concat_axis=1, tiled=True)
-    start_g = lax.all_gather(pair_start, "sl", axis=0, tiled=True)
-    tokens, group, depth = query_g.shape
+    local_tokens, query_heads, depth = queries.shape
+    key_heads = normed_keys.shape[1]
+    group = query_heads // key_heads
+    packed = jnp.concatenate(
+        [
+            queries.reshape(local_tokens, ring, group * key_heads // ring, depth),
+            grad_rows.reshape(local_tokens, ring, group * key_heads // ring, depth),
+            normed_keys.reshape(local_tokens, ring, key_heads // ring, depth),
+            value_matrix.reshape(local_tokens, ring, key_heads // ring, depth),
+        ],
+        axis=2,
+    )
+    packed = lax.all_to_all(packed, "sl", split_axis=1, concat_axis=0, tiled=True)[:, 0]
+    starts = jnp.broadcast_to(pair_start.astype(jnp.float32), (ring, 1, local_tokens))
+    rows = jnp.concatenate(
+        [
+            row_log_total.reshape(ring, query_heads // ring, local_tokens),
+            delta_rows.reshape(ring, query_heads // ring, local_tokens),
+            starts,
+        ],
+        axis=1,
+    )
+    rows = lax.all_to_all(rows, "sl", split_axis=0, concat_axis=2, tiled=True)[0]
+    heads_here = query_heads // ring
+    query_g = packed[:, :heads_here]
+    grad_g = packed[:, heads_here : 2 * heads_here]
+    key_own = packed[:, 2 * heads_here]
+    value_own = packed[:, 2 * heads_here + 1]
+    logsum_g = rows[:heads_here]
+    delta_g = rows[heads_here : 2 * heads_here]
+    start_g = jnp.round(rows[2 * heads_here]).astype(jnp.int32)
+    tokens = query_g.shape[0]
     base = lax.axis_index("sh") * tokens
-    key_own = key_g[:, 0]
-    value_own = value_g[:, 0]
-    key_far = shifted(key_own, "sh", 1)
-    value_far = shifted(value_own, "sh", 1)
-    keys = jnp.concatenate([key_far, key_own], axis=0)
-    values = jnp.concatenate([value_far, value_own], axis=0)
+    far = shifted(jnp.stack([key_own, value_own]), "sh", 1)
+    keys = jnp.concatenate([far[0], key_own], axis=0)
+    values = jnp.concatenate([far[1], value_own], axis=0)
     query_sum, key_sum, value_sum = band_terms(
         query_g, grad_g, logsum_g, delta_g, start_g, base, keys, values
     )
-    key_back = shifted(key_sum[:WINDOW_LENGTH], "sh", -1)
-    value_back = shifted(value_sum[:WINDOW_LENGTH], "sh", -1)
-    key_total = key_sum[WINDOW_LENGTH:] + key_back
-    value_total = value_sum[WINDOW_LENGTH:] + value_back
+    back = shifted(
+        jnp.stack([key_sum[:WINDOW_LENGTH], value_sum[:WINDOW_LENGTH]]), "sh", -1
+    )
+    key_total = key_sum[WINDOW_LENGTH:] + back[0]
+    value_total = value_sum[WINDOW_LENGTH:] + back[1]
     query_grad = (query_sum * score_scale).astype(jnp.bfloat16)
     key_grad = (key_total * score_scale).astype(jnp.bfloat16)[:, None]
     value_grad = value_total.astype(jnp.bfloat16)[:, None]
-
-    def back(x):
-        x = lax.all_to_all(x, "sl", split_axis=0, concat_axis=1, tiled=True)
-        return lax.all_to_all(x, "head", split_axis=0, concat_axis=1, tiled=True)
-
-    return back(query_grad), back(key_grad), back(value_grad)
+    outs = jnp.concatenate([query_grad, key_grad, value_grad], axis=1)
+    items = outs.shape[1]
+    outs = lax.all_to_all(outs, "sl", split_axis=0, concat_axis=1, tiled=True)
+    outs = lax.all_to_all(outs, "head", split_axis=0, concat_axis=1, tiled=True)
+    head_size = lax.axis_size("head")
+    outs = outs.reshape(outs.shape[0], head_size, ring, items, depth)
+    rows_out = outs.shape[0]
+    query_out = outs[:, :, :, :group].reshape(rows_out, -1, depth)
+    key_out = outs[:, :, :, group].reshape(rows_out, -1, depth)
+    value_out = outs[:, :, :, group + 1].reshape(rows_out, -1, depth)
+    return query_out, key_out, value_out
 
 
 def solution(mesh):

time: 183 us -> 144 us (0.79)
  starting transfers between devices: 66.9 us -> 19.3 us
  blocking collectives: 10.4 us -> 31.7 us
  waiting for transfers between devices: 47.6 us -> 64.3 us
  local copies, waits for them, and re-layouts: 22.3 us -> 9.75 us
  matrix products: 20.6 us -> 10.7 us
  other arithmetic: 12.9 us -> 6.81 us
    all_to_all x12 -> x2, starting transfers between devices: 44.5 us -> 8.03 us  [the longest x1 4.46 us: on_device(): lax.all_to_all(rows, 'sl', split_axis=0, concat_axis=2, tiled=True)[0]]
    ppermute x4 -> x2, waiting for transfers between devices: 0.01 us -> 33.6 us  [shifted(): return lax.ppermute(value, axis, pairs)]
    all_to_all x0 -> x2, blocking collectives: none -> 31.7 us  [the longest x1 17.9 us: on_device(): outs = lax.all_to_all(outs, 'head', split_axis=0, concat_axis=1, tiled=True)]
    all_to_all x12 -> x2, waiting for transfers between devices: 47.6 us -> 23.1 us  [the longest x1 19 us: on_device(): lax.all_to_all(packed, 'sl', split_axis=1, concat_axis=0, tiled=True)[:, 0]]
    ppermute x4 -> x2, starting transfers between devices: 19 us -> 7.63 us  [shifted(): return lax.ppermute(value, axis, pairs)]
    all_gather x1 -> x0, blocking collectives: 10.4 us -> none  [on_device(): start_g = lax.all_gather(pair_start, 'sl', axis=0, tiled=True)]
    all_to_all x1, waiting for transfers between devices: 0.01 us -> 7.52 us  [on_device(): lax.all_to_all(output_gradient, 'head', split_axis=1, concat_axis=0, tile...]
    all_to_all x10 -> x5, local copies, waits for them, and re-layouts: 6.75 us -> 1.28 us  [the longest x3 0.91 us: on_device(): outs = lax.all_to_all(outs, 'sl', split_axis=0, concat_axis=1, tiled=True)]
  transfers between devices with their start and end apart: 17 -> 5, of which waited for: 10 -> 5; matrix products, arithmetic and copies ran while one was open for 29% -> 4% of each run, Pallas kernels for 0% -> 0%
where the time goes in v2:
time: 144 us
  waiting for transfers between devices  64.3 us (45%)
  blocking collectives  31.7 us (22%)
  starting transfers between devices  19.3 us (13%)
  matrix products  10.7 us (7%)
  local copies, waits for them, and re-layouts  9.75 us (7%)
  other arithmetic  6.81 us (5%)
    ppermute x2, waiting for transfers between devices, shifted(): return lax.ppermute(value, axis, pairs)  33.6 us
    all_to_all x1, waiting for transfers between devices, on_device(): lax.all_to_all(packed, 'sl', split_axis=1, concat_axis=0, tiled=True)[:, 0]  19 us
    all_to_all x1, blocking collectives, on_device(): outs = lax.all_to_all(outs, 'head', split_axis=0, concat_axis=1, tiled=True)  17.9 us
    all_to_all x1, blocking collectives, on_device(): outs = lax.all_to_all(outs, 'sl', split_axis=0, concat_axis=1, tiled=True)  13.8 us
    ppermute x2, starting transfers between devices, shifted(): return lax.ppermute(value, axis, pairs)  7.63 us
    all_to_all x1, waiting for transfers between devices, on_device(): lax.all_to_all(output_gradient, 'head', split_axis=1, concat_axis=0, tile...  7.52 us
    unnamed x16, local copies, waits for them, and re-layouts  6.12 us
    all_to_all x1, starting transfers between devices, on_device(): lax.all_to_all(rows, 'sl', split_axis=0, concat_axis=2, tiled=True)[0]  4.46 us
  transfers between devices with their start and end apart: 5, of which 5 were waited for; matrix products, arithmetic and copies ran while one was open for 4% of the time, Pallas kernels for 0%

profile of v2, /device:TPU:4, one launch (start us, length us, event | category | flops | bytes accessed | tf_op | source)
XLA Modules:
  0.0 143.6 jit_solution(3560316685536225834)
XLA Ops:
  0.6 0.0 copy-start.3
  0.6 0.0 copy-start.4
  0.7 0.0 copy-start.2
  0.7 0.0 copy-start.1
  0.7 2.1 %copy.76 = bf16[64,32,128]{2,0,1:T(8,128)(2,1)} copy(bf16[64,32,128]{2,1,0:T(8,128)(2,1)} %param.27) | data formatting | bytes 1048576 | tf_op args[4]
  2.8 0.0 copy-start
  2.8 3.6 %all-to-all-start = ((bf16[64,32,128]{2,0,1:T(8,128)(2,1)}), bf16[64,32,128]{2,0,1:T(8,128)(2,1)S(1)}, u32[]{:S(2)}, u32[]{:S(2)}) async-start(bf16[64,32,128]{2,0,1:T(8,128)(2,1)} %copy.76), calls=%async_computation | async-start | bytes 1048576 | tf_op jit(solution)/shard_map/all_to_all | solution.py:58
  6.4 1.1 copy.75
  7.5 0.0 copy-done.3
  7.5 0.0 copy-done.4
  7.5 0.0 copy-done.2
  7.6 0.0 copy-done.1
  7.6 0.1 copy_bitcast_fusion
  7.6 7.5 %all-to-all-done = bf16[64,32,128]{2,0,1:T(8,128)(2,1)S(1)} async-done(((bf16[64,32,128]{2,0,1:T(8,128)(2,1)}), bf16[64,32,128]{2,0,1:T(8,128)(2,1)S(1)}, u32[]{:S(2)}, u32[]{:S(2)}) %all-to-all-start) | async-done | bytes 524320 | tf_op jit(solution)/shard_map/all_to_all | solution.py:58
  15.2 0.3 copy.82
  15.6 0.0 copy-done
  15.6 0.4 fusion.24
  15.9 0.1 copy.104
  16.0 0.6 pad_maximum_fusion.6
  16.6 4.5 %all-to-all-start.2 = ((f32[4,5,256]{2,1,0:T(8,128)}), f32[4,5,256]{2,1,0:T(8,128)S(1)}, u32[]{:S(2)}, u32[]{:S(2)}) async-start(f32[4,5,256]{2,1,0:T(8,128)} %pad_maximum_fusion.6), calls=%async_computation.2 | async-start | bytes 65536 | tf_op jit(solution)/shard_map/all_to_all | solution.py:85
  21.1 1.4 pad_maximum_fusion
  22.5 4.1 %all-to-all-done.2 = f32[4,5,256]{2,1,0:T(8,128)S(1)} async-done(((f32[4,5,256]{2,1,0:T(8,128)}), f32[4,5,256]{2,1,0:T(8,128)S(1)}, u32[]{:S(2)}, u32[]{:S(2)}) %all-to-all-start.2) | async-done | bytes 20512 | tf_op jit(solution)/shard_map/all_to_all | solution.py:85
  26.6 3.6 %all-to-all-start.1 = ((bf16[256,4,6,128]{3,0,2,1:T(8,128)(2,1)}), bf16[256,4,6,128]{3,0,2,1:T(8,128)(2,1)S(1)}, u32[]{:S(2)}, u32[]{:S(2)}) async-start(bf16[256,4,6,128]{3,0,2,1:T(8,128)(2,1)} %pad_maximum_fusion), calls=%async_computation.1 | async-start | bytes 3145728 | tf_op jit(solution)/shard_map/all_to_all | solution.py:75
  30.1 0.1 iota_add_fusion.1
  30.2 0.1 iota_add_fusion
  30.3 19.0 %all-to-all-done.1 = bf16[256,4,6,128]{3,0,2,1:T(8,128)(2,1)S(1)} async-done(((bf16[256,4,6,128]{3,0,2,1:T(8,128)(2,1)}), bf16[256,4,6,128]{3,0,2,1:T(8,128)(2,1)S(1)}, u32[]{:S(2)}, u32[]{:S(2)}) %all-to-all-start.1) | async-done | bytes 1572896 | tf_op jit(solution)/shard_map/all_to_all | solution.py:75
  49.4 0.1 copy.81
  49.5 0.1 slice_bitcast_fusion.14
  49.6 0.1 pad_maximum_fusion.3
  49.7 3.8 %collective-permute-start = (bf16[2,1024,128]{2,1,0:T(8,128)(2,1)S(1)}, bf16[2,1024,128]{2,1,0:T(8,128)(2,1)S(1)}, u32[]{:S(2)}, u32[]{:S(2)}) collective-permute-start(bf16[2,1024,128]{2,1,0:T(8,128)(2,1)S(1)} %pad_maximum_fusion.3), channel_id=1, source_target_pairs={{0,4},{4,8},{8,12},{12,16},{16,20},{20,24},{24,28},{28,32},{32,36}... | collective-permute-start | bytes 1572872 | tf_op jit(solution)/shard_map/ppermute | solution.py:16
  53.5 1.9 %fusion.11 = pred[4,256,1280]{1,2,0:T(8,128)(4,1)S(1)} fusion(s32[4,256]{1,0:T(4,128)S(1)} %bitcast.204, s32[4,1280]{1,0:T(4,128)S(1)} %iota_add_fusion, s32[4,256]{1,0:T(4,128)S(1)} %iota_add_fusion.1), kind=kLoop, calls=%fused_computation.14 | loop fusion | flops 7864320 | bytes 1339392 | tf_op jit(solution)/shard_map/and | solution.py:34
  55.4 0.1 fusion.67
  55.5 14.9 %collective-permute-done = bf16[2,1024,128]{2,1,0:T(8,128)(2,1)S(1)} collective-permute-done((bf16[2,1024,128]{2,1,0:T(8,128)(2,1)S(1)}, bf16[2,1024,128]{2,1,0:T(8,128)(2,1)S(1)}, u32[]{:S(2)}, u32[]{:S(2)}) %collective-permute-start) | collective-permute-done | bytes 524320 | tf_op jit(solution)/shard_map/ppermute | solution.py:16
  70.4 0.2 fusion.54
  70.6 0.2 fusion.48
  70.7 1.5 %fusion.35 = f32[4,1280,256,2]{2,1,3,0:T(8,128)S(1)} fusion(bf16[1,1280,128]{2,1,0:T(8,128)(2,1)S(1)} %get-tuple-element.129, bf16[1,1280,128]{2,1,0:T(8,128)(2,1)S(1)} %get-tuple-element.130, bf16[1,1280,128]{2,1,0:T(8,128)(2,1)S(1)} %get-tuple-element.128, bf16[1,1280,128]{2,1,0:T(8,128)(2,1)S(1)} %get-tuple-element.127, ...), kind=kOutput, calls=%fused_computation.64 | convolution fusion | flops 676331520 | bytes 12320768 | tf_op jit(solution)/shard_map/tigd,tjd->tgij/dot_general | solution.py:36
  72.2 2.6 %fusion.13 = f32[4,1280,128]{2,1,0:T(8,128)S(1)} fusion(f32[4,1280,256,2]{2,1,3,0:T(8,128)S(1)} %fusion.35, f32[4,2,256]{2,1,0:T(2,128)S(1)} %get-tuple-element.132, pred[4,256,1280]{1,2,0:T(8,128)(4,1)S(1)} %fusion.11, bf16[4,256,2,128]{3,1,0,2:T(8,128)(2,1)S(1)} %bitcast.200), kind=kOutput, calls=%fused_computation.16 | convolution fusion | flops 681574400 | bytes 14950400 | tf_op jit(solution)/shard_map/tgij,tigd->tjd/dot_general | solution.py:45
  74.9 4.1 %fusion.1 = bf16[4,2,256,1280]{2,3,1,0:T(8,128)(2,1)S(1)} fusion(f32[4,1280,256,2]{2,1,3,0:T(8,128)S(1)} %fusion.35, f32[4,2,256]{2,1,0:T(2,128)S(1)} %get-tuple-element.131, f32[4,2,256]{2,1,0:T(2,128)S(1)} %get-tuple-element.132, pred[4,256,1280]{1,2,0:T(8,128)(4,1)S(1)} %fusion.11, bf16[1,1280,128]{2,1,0:T(8,128)(2,1)S(1)} %get-tuple-element.123, ...), kind=kOutput, calls=%fused_computation.2 | convolution fusion | flops 692060160 | bytes 18890752 | tf_op jit(solution)/shard_map/tigd,tjd->tgij/dot_general | solution.py:40
  79.0 1.5 %convolution_bitcast_fusion = f32[4,1280,128]{2,1,0:T(8,128)S(1)} fusion(bf16[4,2,256,1280]{2,3,1,0:T(8,128)(2,1)S(1)} %fusion.1, bf16[4,256,2,128]{3,1,0,2:T(8,128)(2,1)S(1)} %bitcast.182), kind=kOutput, calls=%fused_computation.17 | convolution fusion | flops 671088640 | bytes 8388608 | tf_op jit(solution)/shard_map/tgij,tigd->tjd/dot_general | solution.py:44
  80.5 0.1 scatter-add.26
  80.6 0.1 fusion.34
  80.8 0.1 fusion.32
  80.9 0.1 fusion.30
  81.2 0.1 scatter-add.34
  81.2 0.1 fusion.29
  81.4 0.1 fusion.27
  81.5 0.1 fusion.25
  81.7 1.1 pad_maximum_fusion.1
  82.8 3.8 %collective-permute-start.1 = (f32[2,1024,128]{2,1,0:T(8,128)}, f32[2,1024,128]{2,1,0:T(8,128)S(1)}, u32[]{:S(2)}, u32[]{:S(2)}) collective-permute-start(f32[2,1024,128]{2,1,0:T(8,128)} %pad_maximum_fusion.1), channel_id=1, source_target_pairs={{4,0},{8,4},{12,8},{16,12},{20,16},{24,20},{28,24},{32,28},{36,32}... | collective-permute-start | bytes 3145736 | tf_op jit(solution)/shard_map/ppermute | solution.py:16
  86.6 1.0 fusion.23
  87.6 0.3 copy.87
  87.9 18.8 %collective-permute-done.1 = f32[2,1024,128]{2,1,0:T(8,128)S(1)} collective-permute-done((f32[2,1024,128]{2,1,0:T(8,128)}, f32[2,1024,128]{2,1,0:T(8,128)S(1)}, u32[]{:S(2)}, u32[]{:S(2)}) %collective-permute-start.1) | collective-permute-done | bytes 1048608 | tf_op jit(solution)/shard_map/ppermute | solution.py:16
  106.6 0.1 fusion.59
  106.7 0.1 pad_maximum_fusion.2
  106.9 0.8 copy.90
  107.7 13.8 %all_to_all.81 = bf16[1024,4,128]{2,1,0:T(4,128)(2,1)S(1)} all-to-all(bf16[1024,4,128]{2,1,0:T(4,128)(2,1)S(1)} %copy.90), channel_id=1, replica_groups=mesh['head'=4,'sh'=32,'sl'=4] {'sl'}, dimensions={0} | all-to-all | bytes 2097152 | tf_op jit(solution)/shard_map/all_to_all | solution.py:112
  121.5 0.1 copy.91
  121.6 0.1 copy.92
  121.7 0.7 copy.93
  122.4 17.9 %all_to_all.82 = bf16[256,16,128]{2,1,0:T(8,128)(2,1)S(1)} all-to-all(bf16[256,16,128]{2,1,0:T(8,128)(2,1)S(1)} %copy.93), channel_id=1, replica_groups=mesh['head'=4,'sh'=32,'sl'=4] {'head'}, dimensions={0} | all-to-all | bytes 2097152 | tf_op jit(solution)/shard_map/all_to_all | solution.py:113
  140.3 0.3 copy.94
  140.7 1.1 copy.95
  141.9 0.9 copy.96
  142.7 0.9 copy.97
  (18 shorter events, 0.5 us)
Async XLA Ops:
  0.6 6.9 %copy-start.3 = (f32[8,256]{1,0:T(8,128)S(1)}, f32[8,256]{1,0:T(8,128)}, u32[]{:S(2)}) copy-start(f32[8,256]{1,0:T(8,128)} %param.28) | copy-start | bytes 24580
  0.6 6.9 %copy-start.4 = (s32[256]{0:T(256)S(1)}, s32[256]{0:T(256)}, u32[]{:S(2)}) copy-start(s32[256]{0:T(256)} %param.29) | copy-start | bytes 3076
  0.7 6.9 %copy-start.2 = (bf16[256,4,128]{2,1,0:T(4,128)(2,1)S(1)}, bf16[256,4,128]{2,1,0:T(4,128)(2,1)}, u32[]{:S(2)}) copy-start(bf16[256,4,128]{2,1,0:T(4,128)(2,1)} %param.24) | copy-start | bytes 786436
  0.7 6.9 %copy-start.1 = (bf16[256,4,128]{2,1,0:T(4,128)(2,1)S(1)}, bf16[256,4,128]{2,1,0:T(4,128)(2,1)}, u32[]{:S(2)}) copy-start(bf16[256,4,128]{2,1,0:T(4,128)(2,1)} %param.25) | copy-start | bytes 786436
  2.8 12.8 %copy-start = (bf16[256,8,128]{2,1,0:T(8,128)(2,1)S(1)}, bf16[256,8,128]{2,1,0:T(8,128)(2,1)}, u32[]{:S(2)}) copy-start(bf16[256,8,128]{2,1,0:T(8,128)(2,1)} %param.26) | copy-start | bytes 1572868
  2.8 12.4 %all-to-all-start = ((bf16[64,32,128]{2,0,1:T(8,128)(2,1)}), bf16[64,32,128]{2,0,1:T(8,128)(2,1)S(1)}, u32[]{:S(2)}, u32[]{:S(2)}) async-start(bf16[64,32,128]{2,0,1:T(8,128)(2,1)} %copy.76), calls=%async_computation | async-start | bytes 1048576 | tf_op jit(solution)/shard_map/all_to_all | solution.py:58
  16.6 9.9 %all-to-all-start.2 = ((f32[4,5,256]{2,1,0:T(8,128)}), f32[4,5,256]{2,1,0:T(8,128)S(1)}, u32[]{:S(2)}, u32[]{:S(2)}) async-start(f32[4,5,256]{2,1,0:T(8,128)} %pad_maximum_fusion.6), calls=%async_computation.2 | async-start | bytes 65536 | tf_op jit(solution)/shard_map/all_to_all | solution.py:85
  26.6 22.8 %all-to-all-start.1 = ((bf16[256,4,6,128]{3,0,2,1:T(8,128)(2,1)}), bf16[256,4,6,128]{3,0,2,1:T(8,128)(2,1)S(1)}, u32[]{:S(2)}, u32[]{:S(2)}) async-start(bf16[256,4,6,128]{3,0,2,1:T(8,128)(2,1)} %pad_maximum_fusion), calls=%async_computation.1 | async-start | bytes 3145728 | tf_op jit(solution)/shard_map/all_to_all | solution.py:75
  49.7 20.7 %collective-permute-start = (bf16[2,1024,128]{2,1,0:T(8,128)(2,1)S(1)}, bf16[2,1024,128]{2,1,0:T(8,128)(2,1)S(1)}, u32[]{:S(2)}, u32[]{:S(2)}) collective-permute-start(bf16[2,1024,128]{2,1,0:T(8,128)(2,1)S(1)} %pad_maximum_fusion.3), channel_id=1, source_target_pairs={{0,4},{4,8},{8,12},{12,16},{16,20},{20,24},{24,28},{28,32},{32,36}... | collective-permute-start | bytes 1572872 | tf_op jit(solution)/shard_map/ppermute | solution.py:16
  82.8 23.8 %collective-permute-start.1 = (f32[2,1024,128]{2,1,0:T(8,128)}, f32[2,1024,128]{2,1,0:T(8,128)S(1)}, u32[]{:S(2)}, u32[]{:S(2)}) collective-permute-start(f32[2,1024,128]{2,1,0:T(8,128)} %pad_maximum_fusion.1), channel_id=1, source_target_pairs={{4,0},{8,4},{12,8},{16,12},{20,16},{24,20},{28,24},{32,28},{36,32}... | collective-permute-start | bytes 3145736 | tf_op jit(solution)/shard_map/ppermute | solution.py:16

commit v3 on v2

--- a/solution.py
+++ b/solution.py
@@ -63,60 +63,70 @@
     local_tokens, query_heads, depth = queries.shape
     key_heads = normed_keys.shape[1]
     group = query_heads // key_heads
-    packed = jnp.concatenate(
+    heads_here = query_heads // ring
+    kv_packed = jnp.concatenate(
         [
-            queries.reshape(local_tokens, ring, group * key_heads // ring, depth),
-            grad_rows.reshape(local_tokens, ring, group * key_heads // ring, depth),
             normed_keys.reshape(local_tokens, ring, key_heads // ring, depth),
             value_matrix.reshape(local_tokens, ring, key_heads // ring, depth),
         ],
         axis=2,
     )
-    packed = lax.all_to_all(packed, "sl", split_axis=1, concat_axis=0, tiled=True)[:, 0]
+    kv_packed = lax.all_to_all(kv_packed, "sl", split_axis=1, concat_axis=0, tiled=True)[:, 0]
+    key_own = kv_packed[:, 0]
+    value_own = kv_packed[:, 1]
+    far = shifted(kv_packed.transpose(1, 0, 2), "sh", 1)
+    qd_packed = jnp.concatenate(
+        [
+            queries.reshape(local_tokens, ring, heads_here, depth),
+            grad_rows.reshape(local_tokens, ring, heads_here, depth),
+        ],
+        axis=2,
+    )
+    qd_packed = lax.all_to_all(qd_packed, "sl", split_axis=1, concat_axis=0, tiled=True)[:, 0]
     starts = jnp.broadcast_to(pair_start.astype(jnp.float32), (ring, 1, local_tokens))
     rows = jnp.concatenate(
         [
-            row_log_total.reshape(ring, query_heads // ring, local_tokens),
-            delta_rows.reshape(ring, query_heads // ring, local_tokens),
+            row_log_total.reshape(ring, heads_here, local_tokens),
+            delta_rows.reshape(ring, heads_here, local_tokens),
             starts,
         ],
         axis=1,
     )
     rows = lax.all_to_all(rows, "sl", split_axis=0, concat_axis=2, tiled=True)[0]
-    heads_here = query_heads // ring
-    query_g = packed[:, :heads_here]
-    grad_g = packed[:, heads_here : 2 * heads_here]
-    key_own = packed[:, 2 * heads_here]
-    value_own = packed[:, 2 * heads_here + 1]
+    query_g = qd_packed[:, :heads_here]
+    grad_g = qd_packed[:, heads_here:]
     logsum_g = rows[:heads_here]
     delta_g = rows[heads_here : 2 * heads_here]
     start_g = jnp.round(rows[2 * heads_here]).astype(jnp.int32)
     tokens = query_g.shape[0]
     base = lax.axis_index("sh") * tokens
-    far = shifted(jnp.stack([key_own, value_own]), "sh", 1)
     keys = jnp.concatenate([far[0], key_own], axis=0)
     values = jnp.concatenate([far[1], value_own], axis=0)
     query_sum, key_sum, value_sum = band_terms(
         query_g, grad_g, logsum_g, delta_g, start_g, base, keys, values
     )
     back = shifted(
-        jnp.stack([key_sum[:WINDOW_LENGTH], value_sum[:WINDOW_LENGTH]]), "sh", -1
+        jnp.stack([key_sum[:WINDOW_LENGTH], value_sum[:WINDOW_LENGTH]]).astype(jnp.bfloat16),
+        "sh",
+        -1,
     )
-    key_total = key_sum[WINDOW_LENGTH:] + back[0]
-    value_total = value_sum[WINDOW_LENGTH:] + back[1]
-    query_grad = (query_sum * score_scale).astype(jnp.bfloat16)
-    key_grad = (key_total * score_scale).astype(jnp.bfloat16)[:, None]
-    value_grad = value_total.astype(jnp.bfloat16)[:, None]
-    outs = jnp.concatenate([query_grad, key_grad, value_grad], axis=1)
-    items = outs.shape[1]
-    outs = lax.all_to_all(outs, "sl", split_axis=0, concat_axis=1, tiled=True)
-    outs = lax.all_to_all(outs, "head", split_axis=0, concat_axis=1, tiled=True)
+
+    def to_tokens(x):
+        x = lax.all_to_all(x, "sl", split_axis=0, concat_axis=1, tiled=True)
+        return lax.all_to_all(x, "head", split_axis=0, concat_axis=1, tiled=True)
+
     head_size = lax.axis_size("head")
-    outs = outs.reshape(outs.shape[0], head_size, ring, items, depth)
-    rows_out = outs.shape[0]
-    query_out = outs[:, :, :, :group].reshape(rows_out, -1, depth)
-    key_out = outs[:, :, :, group].reshape(rows_out, -1, depth)
-    value_out = outs[:, :, :, group + 1].reshape(rows_out, -1, depth)
+    query_grad = to_tokens((query_sum * score_scale).astype(jnp.bfloat16))
+    rows_out = query_grad.shape[0]
+    query_out = query_grad.reshape(rows_out, -1, depth)
+    key_total = key_sum[WINDOW_LENGTH:] + back[0].astype(jnp.float32)
+    value_total = value_sum[WINDOW_LENGTH:] + back[1].astype(jnp.float32)
+    key_grad = (key_total * score_scale).astype(jnp.bfloat16)
+    value_grad = value_total.astype(jnp.bfloat16)
+    kv_out = to_tokens(jnp.stack([key_grad, value_grad], axis=1))
+    kv_out = kv_out.reshape(rows_out, head_size, ring, 2, depth)
+    key_out = kv_out[:, :, :, 0].reshape(rows_out, -1, depth)
+    value_out = kv_out[:, :, :, 1].reshape(rows_out, -1, depth)
     return query_out, key_out, value_out
 
 

time: 144 us -> 135 us (0.938)
  blocking collectives: 31.7 us -> 0 us
  starting transfers between devices: 19.3 us -> 42.3 us
  waiting for transfers between devices: 64.3 us -> 53 us
  local copies, waits for them, and re-layouts: 9.75 us -> 15.9 us
  other arithmetic: 6.81 us -> 10.7 us
    ppermute x2, waiting for transfers between devices: 33.6 us -> 1.01 us  [shifted(): return lax.ppermute(value, axis, pairs)]
    all_to_all x2 -> x0, blocking collectives: 31.7 us -> none  [the longest x1 17.9 us: on_device(): outs = lax.all_to_all(outs, 'head', split_axis=0, concat_axis=1, tiled=True)]
    all_to_all x1 -> x6, waiting for transfers between devices: 19 us -> 41.1 us  [the longest x2 15.4 us: to_tokens(): return lax.all_to_all(x, 'head', split_axis=0, concat_axis=1, tiled=True)]
    all_to_all x1 -> x6, starting transfers between devices: 3.56 us -> 22 us  [the longest x2 7.12 us: to_tokens(): x = lax.all_to_all(x, 'sl', split_axis=0, concat_axis=1, tiled=True)]
    ppermute x2, starting transfers between devices: 7.63 us -> 13.5 us  [shifted(): return lax.ppermute(value, axis, pairs)]
    all_to_all x5 -> x10, local copies, waits for them, and re-layouts: 1.28 us -> 3.58 us  [the longest x6 2.48 us: to_tokens(): x = lax.all_to_all(x, 'sl', split_axis=0, concat_axis=1, tiled=True)]
    another operation x1, other arithmetic: 0.16 us -> 2.05 us  [band_terms(): key_w = jnp.stack([keys[t * BLOCK:t * BLOCK + span] for t in range(tiles)])]
    unnamed x16 -> x33, local copies, waits for them, and re-layouts: 6.12 us -> 4.78 us
  transfers between devices with their start and end apart: 5 -> 10, of which waited for: 5 -> 10; matrix products, arithmetic and copies ran while one was open for 4% -> 16% of each run, Pallas kernels for 0% -> 0%
where the time goes in v3:
time: 135 us; the launch traced here: 134 us
  waiting for transfers between devices  53 us (39%)
  starting transfers between devices  42.3 us (31%)
  local copies, waits for them, and re-layouts  15.9 us (12%)
  other arithmetic  10.7 us (8%)
  matrix products  10.7 us (8%)
    all_to_all x2, waiting for transfers between devices, to_tokens(): return lax.all_to_all(x, 'head', split_axis=0, concat_axis=1, tiled=True)  15.4 us
    ppermute x2, starting transfers between devices, shifted(): return lax.ppermute(value, axis, pairs)  13.5 us
    all_to_all x2, waiting for transfers between devices, to_tokens(): x = lax.all_to_all(x, 'sl', split_axis=0, concat_axis=1, tiled=True)  12.3 us
    all_to_all x1, waiting for transfers between devices, on_device(): lax.all_to_all(kv_packed, 'sl', split_axis=1, concat_axis=0, tiled=True)  8.12 us
    all_to_all x2, starting transfers between devices, to_tokens(): x = lax.all_to_all(x, 'sl', split_axis=0, concat_axis=1, tiled=True)  7.12 us
    all_to_all x2, starting transfers between devices, to_tokens(): return lax.all_to_all(x, 'head', split_axis=0, concat_axis=1, tiled=True)  6.94 us
    all_to_all x1, waiting for transfers between devices, on_device(): lax.all_to_all(output_gradient, 'head', split_axis=1, concat_axis=0, tile...  6.61 us
    all_to_all x1, waiting for transfers between devices, on_device(): lax.all_to_all(qd_packed, 'sl', split_axis=1, concat_axis=0, tiled=True)  5.25 us
  transfers between devices with their start and end apart: 10, of which 10 were waited for; matrix products, arithmetic and copies ran while one was open for 16% of the time, Pallas kernels for 0%

profile of v3, /device:TPU:4, one launch (start us, length us, event | category | flops | bytes accessed | tf_op | source)
XLA Modules:
  0.0 133.9 jit_solution(10667146032963447479)
XLA Ops:
  0.7 2.1 %copy.75 = bf16[64,32,128]{2,0,1:T(8,128)(2,1)} copy(bf16[64,32,128]{2,1,0:T(8,128)(2,1)} %param.27) | data formatting | bytes 1048576 | tf_op args[4]
  2.8 3.5 %all-to-all-start.1 = ((bf16[64,32,128]{2,0,1:T(8,128)(2,1)}), bf16[64,32,128]{2,0,1:T(8,128)(2,1)S(1)}, u32[]{:S(2)}, u32[]{:S(2)}) async-start(bf16[64,32,128]{2,0,1:T(8,128)(2,1)} %copy.75), calls=%async_computation.1 | async-start | bytes 1048576 | tf_op jit(solution)/shard_map/all_to_all | solution.py:58
  6.2 1.1 copy_bitcast_fusion.1
  7.4 0.1 copy.78
  7.5 0.8 pad_maximum_fusion.1
  8.3 0.1 iota_add_fusion.1
  8.4 6.6 %all-to-all-done.1 = bf16[64,32,128]{2,0,1:T(8,128)(2,1)S(1)} async-done(((bf16[64,32,128]{2,0,1:T(8,128)(2,1)}), bf16[64,32,128]{2,0,1:T(8,128)(2,1)S(1)}, u32[]{:S(2)}, u32[]{:S(2)}) %all-to-all-start.1) | async-done | bytes 524320 | tf_op jit(solution)/shard_map/all_to_all | solution.py:58
  15.0 4.5 %all-to-all-start = ((bf16[256,4,2,128]{3,0,2,1:T(8,128)(2,1)}), bf16[256,4,2,128]{3,0,2,1:T(8,128)(2,1)S(1)}, u32[]{:S(2)}, u32[]{:S(2)}) async-start(bf16[256,4,2,128]{3,0,2,1:T(8,128)(2,1)} %pad_maximum_fusion.1), calls=%async_computation | async-start | bytes 1048576 | tf_op jit(solution)/shard_map/all_to_all | solution.py:74
  19.5 0.7 iota_add_fusion
  20.2 0.3 copy.77
  20.5 8.1 %all-to-all-done = bf16[256,4,2,128]{3,0,2,1:T(8,128)(2,1)S(1)} async-done(((bf16[256,4,2,128]{3,0,2,1:T(8,128)(2,1)}), bf16[256,4,2,128]{3,0,2,1:T(8,128)(2,1)S(1)}, u32[]{:S(2)}, u32[]{:S(2)}) %all-to-all-start) | async-done | bytes 524320 | tf_op jit(solution)/shard_map/all_to_all | solution.py:74
  28.7 3.8 %collective-permute-start = (bf16[2,1024,128]{2,1,0:T(8,128)(2,1)S(1)}, bf16[2,1024,128]{2,1,0:T(8,128)(2,1)}, u32[]{:S(2)}, u32[]{:S(2)}) collective-permute-start(bf16[2,1024,128]{2,1,0:T(8,128)(2,1)S(1)} %bitcast.190), channel_id=1, source_target_pairs={{0,4},{4,8},{8,12},{12,16},{16,20},{20,24},{24,28},{28,32},{32,36}... | collective-permute-start | bytes 1572872 | tf_op jit(solution)/shard_map/ppermute | solution.py:16
  32.5 0.8 slice_bitcast_fusion.10
  33.4 1.4 %fusion.24 = f32[8,256]{0,1:T(8,128)S(1)} fusion(bf16[8,256,128]{2,0,1:T(8,128)(2,1)S(1)} %bitcast.194, bf16[256,8,128]{2,1,0:T(8,128)(2,1)} %param.26), kind=kLoop, calls=%fused_computation.31 | loop fusion | flops 1046528 | bytes 1056768
  34.8 0.6 pad_maximum_fusion.6
  35.5 3.3 %all-to-all-start.2 = ((f32[4,5,256]{2,1,0:T(8,128)}), f32[4,5,256]{2,1,0:T(8,128)S(1)}, u32[]{:S(2)}, u32[]{:S(2)}) async-start(f32[4,5,256]{2,1,0:T(8,128)} %pad_maximum_fusion.6), calls=%async_computation.2 | async-start | bytes 65536 | tf_op jit(solution)/shard_map/all_to_all | solution.py:95
  38.7 1.1 pad_maximum_fusion
  39.8 4.3 %all-to-all-done.2 = f32[4,5,256]{2,1,0:T(8,128)S(1)} async-done(((f32[4,5,256]{2,1,0:T(8,128)}), f32[4,5,256]{2,1,0:T(8,128)S(1)}, u32[]{:S(2)}, u32[]{:S(2)}) %all-to-all-start.2) | async-done | bytes 20512 | tf_op jit(solution)/shard_map/all_to_all | solution.py:95
  44.2 3.5 %all-to-all-start.3 = ((bf16[256,4,4,128]{3,0,2,1:T(8,128)(2,1)}), bf16[256,4,4,128]{3,0,2,1:T(8,128)(2,1)S(1)}, u32[]{:S(2)}, u32[]{:S(2)}) async-start(bf16[256,4,4,128]{3,0,2,1:T(8,128)(2,1)} %pad_maximum_fusion), calls=%async_computation.3 | async-start | bytes 2097152 | tf_op jit(solution)/shard_map/all_to_all | solution.py:85
  47.7 0.6 slice_bitcast_fusion.15
  48.3 1.9 %fusion.11 = pred[4,256,1280]{1,2,0:T(8,128)(4,1)S(1)} fusion(s32[4,256]{1,0:T(4,128)S(1)} %bitcast.211, s32[4,1280]{1,0:T(4,128)S(1)} %copy-done.9, s32[4,256]{1,0:T(4,128)S(1)} %iota_add_fusion.1), kind=kLoop, calls=%fused_computation.14 | loop fusion | flops 7864320 | bytes 1339392 | tf_op jit(solution)/shard_map/and | solution.py:34
  50.2 0.1 collective-permute-done
  50.3 1.1 slice_bitcast_fusion.11
  51.4 2.1 %fusion.52 = (bf16[1,1280,128]{2,1,0:T(8,128)(2,1)S(1)}, bf16[1,1280,128]{2,1,0:T(8,128)(2,1)S(1)}, bf16[1,1280,128]{2,1,0:T(8,128)(2,1)S(1)}, bf16[1,1280,128]{2,1,0:T(8,128)(2,1)}) fusion(bf16[1024,128]{1,0:T(8,128)(2,1)S(1)} %get-tuple-element.122, bf16[1024,128]{1,0:T(8,128)(2,1)} %get-tuple-element.124), kind=kLoop, calls=%fused_computation.87 | loop fusion | flops 2621440 | bytes 1835008 | tf_op jit(solution)/shard_map/stack | solution.py:28
  53.5 1.2 fusion.46
  54.6 5.2 %all-to-all-done.3 = bf16[256,4,4,128]{3,0,2,1:T(8,128)(2,1)S(1)} async-done(((bf16[256,4,4,128]{3,0,2,1:T(8,128)(2,1)}), bf16[256,4,4,128]{3,0,2,1:T(8,128)(2,1)S(1)}, u32[]{:S(2)}, u32[]{:S(2)}) %all-to-all-start.3) | async-done | bytes 1048608 | tf_op jit(solution)/shard_map/all_to_all | solution.py:85
  59.9 0.1 copy.80
  59.9 0.1 fusion.67
  60.0 0.8 copy-done.2
  60.8 1.5 %fusion.35 = f32[4,1280,256,2]{2,1,3,0:T(8,128)S(1)} fusion(bf16[1,1280,128]{2,1,0:T(8,128)(2,1)S(1)} %get-tuple-element.127, bf16[1,1280,128]{2,1,0:T(8,128)(2,1)S(1)} %copy-done.2, bf16[1,1280,128]{2,1,0:T(8,128)(2,1)S(1)} %get-tuple-element.126, bf16[1,1280,128]{2,1,0:T(8,128)(2,1)S(1)} %get-tuple-element.125, bf16[4,256,2,128]{3,1,0,2:T(8,128)(2,1)S(1)} %bitcast.184), kind=kOutput, calls=%fused_computation.62 | convolution fusion | flops 676331520 | bytes 12320768 | tf_op jit(solution)/shard_map/tigd,tjd->tgij/dot_general | solution.py:36
  62.4 2.6 %fusion.13 = f32[4,1280,128]{2,1,0:T(8,128)S(1)} fusion(f32[4,1280,256,2]{2,1,3,0:T(8,128)S(1)} %fusion.35, f32[4,2,256]{2,1,0:T(2,128)S(1)} %copy-done.11, pred[4,256,1280]{1,2,0:T(8,128)(4,1)S(1)} %fusion.11, bf16[4,256,2,128]{3,1,0,2:T(8,128)(2,1)S(1)} %bitcast.207), kind=kOutput, calls=%fused_computation.16 | convolution fusion | flops 681574400 | bytes 14950400 | tf_op jit(solution)/shard_map/tgij,tigd->tjd/dot_general | solution.py:45
  65.1 4.1 %fusion.1 = bf16[4,2,256,1280]{2,3,1,0:T(8,128)(2,1)S(1)} fusion(f32[4,1280,256,2]{2,1,3,0:T(8,128)S(1)} %fusion.35, f32[4,2,256]{2,1,0:T(2,128)S(1)} %copy-done.12, f32[4,2,256]{2,1,0:T(2,128)S(1)} %copy-done.11, pred[4,256,1280]{1,2,0:T(8,128)(4,1)S(1)} %fusion.11, bf16[1,1280,128]{2,1,0:T(8,128)(2,1)S(1)} %copy-done.7, ...), kind=kOutput, calls=%fused_computation.2 | convolution fusion | flops 692060160 | bytes 18890752 | tf_op jit(solution)/shard_map/tigd,tjd->tgij/dot_general | solution.py:40
  69.2 1.5 %convolution_bitcast_fusion = f32[4,1280,128]{2,1,0:T(8,128)S(1)} fusion(bf16[4,2,256,1280]{2,3,1,0:T(8,128)(2,1)S(1)} %fusion.1, bf16[4,256,2,128]{3,1,0,2:T(8,128)(2,1)S(1)} %bitcast.185), kind=kOutput, calls=%fused_computation.17 | convolution fusion | flops 671088640 | bytes 8388608 | tf_op jit(solution)/shard_map/tgij,tigd->tjd/dot_general | solution.py:44
  70.8 0.1 scatter-add.26
  70.9 0.1 fusion.34
  71.0 0.1 fusion.32
  71.2 0.1 fusion.30
  71.3 0.1 scatter-add.34
  71.4 0.1 fusion.29
  71.5 0.1 fusion.27
  71.7 0.1 fusion.25
  72.0 9.7 %collective-permute-start.1 = (bf16[2,1024,128]{2,1,0:T(8,128)(2,1)S(1)}, bf16[2,1024,128]{2,1,0:T(8,128)(2,1)S(1)}, u32[]{:S(2)}, u32[]{:S(2)}) collective-permute-start(bf16[2,1024,128]{2,1,0:T(8,128)(2,1)S(1)} %pad_maximum_fusion.2), channel_id=1, source_target_pairs={{4,0},{8,4},{12,8},{16,12},{20,16},{24,20},{28,24},{32,28},{36,32}... | collective-permute-start | bytes 1572872 | tf_op jit(solution)/shard_map/ppermute | solution.py:16
  81.8 1.0 fusion.23
  82.7 0.3 copy.85
  83.0 1.3 copy.86
  84.4 3.7 %all-to-all-start.4 = ((bf16[1024,2,128]{2,1,0:T(2,128)(2,1)}), bf16[1024,2,128]{2,1,0:T(2,128)(2,1)S(1)}, u32[]{:S(2)}, u32[]{:S(2)}) async-start(bf16[1024,2,128]{2,1,0:T(2,128)(2,1)} %copy.86), calls=%async_computation.4 | async-start | bytes 1048576 | tf_op jit(solution)/shard_map/all_to_all | solution.py:115
  88.0 0.9 collective-permute-done.1
  88.9 0.1 fusion.57
  89.1 1.3 copy.93
  90.4 5.5 %all-to-all-done.4 = bf16[1024,2,128]{2,1,0:T(2,128)(2,1)S(1)} async-done(((bf16[1024,2,128]{2,1,0:T(2,128)(2,1)}), bf16[1024,2,128]{2,1,0:T(2,128)(2,1)S(1)}, u32[]{:S(2)}, u32[]{:S(2)}) %all-to-all-start.4) | async-done | bytes 524320 | tf_op jit(solution)/shard_map/all_to_all | solution.py:115
  95.9 3.5 %all-to-all-start.6 = ((bf16[1024,2,128]{2,1,0:T(2,128)(2,1)}), bf16[1024,2,128]{2,1,0:T(2,128)(2,1)S(1)}, u32[]{:S(2)}, u32[]{:S(2)}) async-start(bf16[1024,2,128]{2,1,0:T(2,128)(2,1)} %copy.93), calls=%async_computation.6 | async-start | bytes 1048576 | tf_op jit(solution)/shard_map/all_to_all | solution.py:115
  99.4 0.1 copy.87
  99.5 1.1 copy.89
  100.6 6.8 %all-to-all-done.6 = bf16[1024,2,128]{2,1,0:T(2,128)(2,1)S(1)} async-done(((bf16[1024,2,128]{2,1,0:T(2,128)(2,1)}), bf16[1024,2,128]{2,1,0:T(2,128)(2,1)S(1)}, u32[]{:S(2)}, u32[]{:S(2)}) %all-to-all-start.6) | async-done | bytes 524320 | tf_op jit(solution)/shard_map/all_to_all | solution.py:115
  107.4 3.5 %all-to-all-start.5 = ((bf16[256,8,128]{2,1,0:T(8,128)(2,1)}), bf16[256,8,128]{2,1,0:T(8,128)(2,1)S(1)}, u32[]{:S(2)}, u32[]{:S(2)}) async-start(bf16[256,8,128]{2,1,0:T(8,128)(2,1)} %copy.89), calls=%async_computation.5 | async-start | bytes 1048576 | tf_op jit(solution)/shard_map/all_to_all | solution.py:116
  110.9 0.1 copy.94
  111.0 1.1 copy.96
  112.1 7.5 %all-to-all-done.5 = bf16[256,8,128]{2,1,0:T(8,128)(2,1)S(1)} async-done(((bf16[256,8,128]{2,1,0:T(8,128)(2,1)}), bf16[256,8,128]{2,1,0:T(8,128)(2,1)S(1)}, u32[]{:S(2)}, u32[]{:S(2)}) %all-to-all-start.5) | async-done | bytes 524320 | tf_op jit(solution)/shard_map/all_to_all | solution.py:116
  119.7 3.5 %all-to-all-start.7 = ((bf16[256,8,128]{2,1,0:T(8,128)(2,1)}), bf16[256,8,128]{2,1,0:T(8,128)(2,1)S(1)}, u32[]{:S(2)}, u32[]{:S(2)}) async-start(bf16[256,8,128]{2,1,0:T(8,128)(2,1)} %copy.96), calls=%async_computation.7 | async-start | bytes 1048576 | tf_op jit(solution)/shard_map/all_to_all | solution.py:116
  123.1 0.9 copy.131
  124.0 7.9 %all-to-all-done.7 = bf16[256,8,128]{2,1,0:T(8,128)(2,1)S(1)} async-done(((bf16[256,8,128]{2,1,0:T(8,128)(2,1)}), bf16[256,8,128]{2,1,0:T(8,128)(2,1)S(1)}, u32[]{:S(2)}, u32[]{:S(2)}) %all-to-all-start.7) | async-done | bytes 524320 | tf_op jit(solution)/shard_map/all_to_all | solution.py:116
  131.9 0.1 copy.97
  132.1 0.9 copy.98
  133.0 0.9 copy.99
  (48 shorter events, 0.7 us)
Async XLA Ops:
  0.6 6.7 %copy-start.4 = (bf16[256,8,128]{2,1,0:T(8,128)(2,1)S(1)}, bf16[256,8,128]{2,1,0:T(8,128)(2,1)}, u32[]{:S(2)}) copy-start(bf16[256,8,128]{2,1,0:T(8,128)(2,1)} %param.23) | copy-start | bytes 1572868
  0.6 6.8 %copy-start.13 = (s32[256]{0:T(256)S(1)}, s32[256]{0:T(256)}, u32[]{:S(2)}) copy-start(s32[256]{0:T(256)} %param.29) | copy-start | bytes 3076
  0.7 6.8 %copy-start.10 = (f32[8,256]{1,0:T(8,128)S(1)}, f32[8,256]{1,0:T(8,128)}, u32[]{:S(2)}) copy-start(f32[8,256]{1,0:T(8,128)} %param.28) | copy-start | bytes 24580
  2.8 12.3 %all-to-all-start.1 = ((bf16[64,32,128]{2,0,1:T(8,128)(2,1)}), bf16[64,32,128]{2,0,1:T(8,128)(2,1)S(1)}, u32[]{:S(2)}, u32[]{:S(2)}) async-start(bf16[64,32,128]{2,0,1:T(8,128)(2,1)} %copy.75), calls=%async_computation.1 | async-start | bytes 1048576 | tf_op jit(solution)/shard_map/all_to_all | solution.py:58
  15.0 13.6 %all-to-all-start = ((bf16[256,4,2,128]{3,0,2,1:T(8,128)(2,1)}), bf16[256,4,2,128]{3,0,2,1:T(8,128)(2,1)S(1)}, u32[]{:S(2)}, u32[]{:S(2)}) async-start(bf16[256,4,2,128]{3,0,2,1:T(8,128)(2,1)} %pad_maximum_fusion.1), calls=%async_computation | async-start | bytes 1048576 | tf_op jit(solution)/shard_map/all_to_all | solution.py:74
  28.7 21.6 %collective-permute-start = (bf16[2,1024,128]{2,1,0:T(8,128)(2,1)S(1)}, bf16[2,1024,128]{2,1,0:T(8,128)(2,1)}, u32[]{:S(2)}, u32[]{:S(2)}) collective-permute-start(bf16[2,1024,128]{2,1,0:T(8,128)(2,1)S(1)} %bitcast.190), channel_id=1, source_target_pairs={{0,4},{4,8},{8,12},{12,16},{16,20},{20,24},{24,28},{28,32},{32,36}... | collective-permute-start | bytes 1572872 | tf_op jit(solution)/shard_map/ppermute | solution.py:16
  33.4 15.0 %copy-start.9 = (s32[4,1280]{1,0:T(4,128)S(1)}, s32[4,1280]{1,0:T(4,128)}, u32[]{:S(2)}) copy-start(s32[4,1280]{1,0:T(4,128)} %iota_add_fusion) | copy-start | bytes 61444
  35.5 8.7 %all-to-all-start.2 = ((f32[4,5,256]{2,1,0:T(8,128)}), f32[4,5,256]{2,1,0:T(8,128)S(1)}, u32[]{:S(2)}, u32[]{:S(2)}) async-start(f32[4,5,256]{2,1,0:T(8,128)} %pad_maximum_fusion.6), calls=%async_computation.2 | async-start | bytes 65536 | tf_op jit(solution)/shard_map/all_to_all | solution.py:95
  44.2 15.7 %all-to-all-start.3 = ((bf16[256,4,4,128]{3,0,2,1:T(8,128)(2,1)}), bf16[256,4,4,128]{3,0,2,1:T(8,128)(2,1)S(1)}, u32[]{:S(2)}, u32[]{:S(2)}) async-start(bf16[256,4,4,128]{3,0,2,1:T(8,128)(2,1)} %pad_maximum_fusion), calls=%async_computation.3 | async-start | bytes 2097152 | tf_op jit(solution)/shard_map/all_to_all | solution.py:85
  47.7 5.8 %copy-start.3 = (bf16[1024,128]{1,0:T(8,128)(2,1)S(1)}, bf16[1024,128]{1,0:T(8,128)(2,1)}, u32[]{:S(2)}) copy-start(bf16[1024,128]{1,0:T(8,128)(2,1)} %get-tuple-element.123) | copy-start | bytes 786436
  53.5 6.6 %copy-start = (bf16[1,1280,128]{2,1,0:T(8,128)(2,1)}, bf16[1,1280,128]{2,1,0:T(8,128)(2,1)S(1)}, u32[]{:S(2)}) copy-start(bf16[1,1280,128]{2,1,0:T(8,128)(2,1)S(1)} %get-tuple-element.127) | copy-start | bytes 983044
  59.9 1.0 copy-start.2
  60.8 1.5 %copy-start.11 = (f32[4,2,256]{2,1,0:T(2,128)S(1)}, f32[4,2,256]{2,1,0:T(2,128)}, u32[]{:S(2)}) copy-start(f32[4,2,256]{2,1,0:T(2,128)} %get-tuple-element.129) | copy-start | bytes 24580
  62.4 2.7 %copy-start.5 = (bf16[1,1280,128]{2,1,0:T(8,128)(2,1)S(1)}, bf16[1,1280,128]{2,1,0:T(8,128)(2,1)}, u32[]{:S(2)}) copy-start(bf16[1,1280,128]{2,1,0:T(8,128)(2,1)} %get-tuple-element.117) | copy-start | bytes 983044
  62.4 2.7 %copy-start.6 = (bf16[1,1280,128]{2,1,0:T(8,128)(2,1)S(1)}, bf16[1,1280,128]{2,1,0:T(8,128)(2,1)}, u32[]{:S(2)}) copy-start(bf16[1,1280,128]{2,1,0:T(8,128)(2,1)} %get-tuple-element.118) | copy-start | bytes 983044
  62.4 2.7 %copy-start.7 = (bf16[1,1280,128]{2,1,0:T(8,128)(2,1)S(1)}, bf16[1,1280,128]{2,1,0:T(8,128)(2,1)}, u32[]{:S(2)}) copy-start(bf16[1,1280,128]{2,1,0:T(8,128)(2,1)} %get-tuple-element.119) | copy-start | bytes 983044
  62.4 2.7 %copy-start.8 = (bf16[1,1280,128]{2,1,0:T(8,128)(2,1)S(1)}, bf16[1,1280,128]{2,1,0:T(8,128)(2,1)}, u32[]{:S(2)}) copy-start(bf16[1,1280,128]{2,1,0:T(8,128)(2,1)} %get-tuple-element.120) | copy-start | bytes 983044
  62.4 2.7 %copy-start.12 = (f32[4,2,256]{2,1,0:T(2,128)S(1)}, f32[4,2,256]{2,1,0:T(2,128)}, u32[]{:S(2)}) copy-start(f32[4,2,256]{2,1,0:T(2,128)} %get-tuple-element.130) | copy-start | bytes 24580
  71.8 10.0 %copy-start.1 = (bf16[1,1280,128]{2,1,0:T(8,128)(2,1)S(1)}, bf16[1,1280,128]{2,1,0:T(8,128)(2,1)}, u32[]{:S(2)}) copy-start(bf16[1,1280,128]{2,1,0:T(8,128)(2,1)} %copy-done) | copy-start | bytes 983044
  72.0 16.9 %collective-permute-start.1 = (bf16[2,1024,128]{2,1,0:T(8,128)(2,1)S(1)}, bf16[2,1024,128]{2,1,0:T(8,128)(2,1)S(1)}, u32[]{:S(2)}, u32[]{:S(2)}) collective-permute-start(bf16[2,1024,128]{2,1,0:T(8,128)(2,1)S(1)} %pad_maximum_fusion.2), channel_id=1, source_target_pairs={{4,0},{8,4},{12,8},{16,12},{20,16},{24,20},{28,24},{32,28},{36,32}... | collective-permute-start | bytes 1572872 | tf_op jit(solution)/shard_map/ppermute | solution.py:16
  84.4 11.5 %all-to-all-start.4 = ((bf16[1024,2,128]{2,1,0:T(2,128)(2,1)}), bf16[1024,2,128]{2,1,0:T(2,128)(2,1)S(1)}, u32[]{:S(2)}, u32[]{:S(2)}) async-start(bf16[1024,2,128]{2,1,0:T(2,128)(2,1)} %copy.86), calls=%async_computation.4 | async-start | bytes 1048576 | tf_op jit(solution)/shard_map/all_to_all | solution.py:115
  95.9 11.5 %all-to-all-start.6 = ((bf16[1024,2,128]{2,1,0:T(2,128)(2,1)}), bf16[1024,2,128]{2,1,0:T(2,128)(2,1)S(1)}, u32[]{:S(2)}, u32[]{:S(2)}) async-start(bf16[1024,2,128]{2,1,0:T(2,128)(2,1)} %copy.93), calls=%async_computation.6 | async-start | bytes 1048576 | tf_op jit(solution)/shard_map/all_to_all | solution.py:115
  107.4 12.3 %all-to-all-start.5 = ((bf16[256,8,128]{2,1,0:T(8,128)(2,1)}), bf16[256,8,128]{2,1,0:T(8,128)(2,1)S(1)}, u32[]{:S(2)}, u32[]{:S(2)}) async-start(bf16[256,8,128]{2,1,0:T(8,128)(2,1)} %copy.89), calls=%async_computation.5 | async-start | bytes 1048576 | tf_op jit(solution)/shard_map/all_to_all | solution.py:116
  119.7 12.3 %all-to-all-start.7 = ((bf16[256,8,128]{2,1,0:T(8,128)(2,1)}), bf16[256,8,128]{2,1,0:T(8,128)(2,1)S(1)}, u32[]{:S(2)}, u32[]{:S(2)}) async-start(bf16[256,8,128]{2,1,0:T(8,128)(2,1)} %copy.96), calls=%async_computation.7 | async-start | bytes 1048576 | tf_op jit(solution)/shard_map/all_to_all | solution.py:116

commit v4 on v2

--- a/solution.py
+++ b/solution.py
@@ -52,46 +52,68 @@
     return query_term.reshape(tokens, group, depth), key_term, value_term
 
 
+def split_three(x):
+    hi = lax.reduce_precision(x, exponent_bits=8, mantissa_bits=7)
+    rest = x - hi
+    mid = lax.reduce_precision(rest, exponent_bits=8, mantissa_bits=7)
+    lo = rest - mid
+    return jnp.stack([hi, mid, lo], axis=-1).astype(jnp.bfloat16)
+
+
+def join_three(parts):
+    parts = parts.astype(jnp.float32)
+    return (parts[..., 0] + parts[..., 1]) + parts[..., 2]
+
+
 def on_device(
     queries, normed_keys, value_matrix, forward_out, output_gradient, row_log_total, pair_start
 ):
-    grad_rows = lax.all_to_all(output_gradient, "head", split_axis=1, concat_axis=0, tiled=True)
-    delta_rows = jnp.einsum(
-        "thd,thd->ht", forward_out, grad_rows, preferred_element_type=jnp.float32
+    ring = lax.axis_size("sl")
+    head_size = lax.axis_size("head")
+    local_tokens, heads_local, depth = queries.shape
+    kv_local = normed_keys.shape[1]
+    heads_here = heads_local // ring
+    kv_here = kv_local // ring
+    grad_rows = output_gradient.reshape(
+        output_gradient.shape[0], head_size, ring, heads_here, depth
+    ).transpose(0, 2, 1, 3, 4)
+    grad_rows = grad_rows.reshape(output_gradient.shape[0], ring * head_size, heads_here, depth)
+    grad_g = lax.all_to_all(
+        grad_rows, ("sl", "head"), split_axis=1, concat_axis=0, tiled=True
+    )[:, 0]
+    logsum = row_log_total.reshape(ring, heads_here, local_tokens).transpose(2, 0, 1)
+    side = jnp.concatenate(
+        [
+            split_three(logsum).reshape(local_tokens, ring, heads_here * 3),
+            jnp.broadcast_to(
+                split_three(pair_start.astype(jnp.float32))[:, None], (local_tokens, ring, 3)
+            ),
+        ],
+        axis=2,
     )
-    ring = lax.axis_size("sl")
-    local_tokens, query_heads, depth = queries.shape
-    key_heads = normed_keys.shape[1]
-    group = query_heads // key_heads
+    side = jnp.pad(side, ((0, 0), (0, 0), (0, depth - side.shape[2])))
     packed = jnp.concatenate(
         [
-            queries.reshape(local_tokens, ring, group * key_heads // ring, depth),
-            grad_rows.reshape(local_tokens, ring, group * key_heads // ring, depth),
-            normed_keys.reshape(local_tokens, ring, key_heads // ring, depth),
-            value_matrix.reshape(local_tokens, ring, key_heads // ring, depth),
+            queries.reshape(local_tokens, ring, heads_here, depth),
+            forward_out.reshape(local_tokens, ring, heads_here, depth),
+            normed_keys.reshape(local_tokens, ring, kv_here, depth),
+            value_matrix.reshape(local_tokens, ring, kv_here, depth),
+            side[:, :, None],
         ],
         axis=2,
     )
     packed = lax.all_to_all(packed, "sl", split_axis=1, concat_axis=0, tiled=True)[:, 0]
-    starts = jnp.broadcast_to(pair_start.astype(jnp.float32), (ring, 1, local_tokens))
-    rows = jnp.concatenate(
-        [
-            row_log_total.reshape(ring, query_heads // ring, local_tokens),
-            delta_rows.reshape(ring, query_heads // ring, local_tokens),
-            starts,
-        ],
-        axis=1,
-    )
-    rows = lax.all_to_all(rows, "sl", split_axis=0, concat_axis=2, tiled=True)[0]
-    heads_here = query_heads // ring
     query_g = packed[:, :heads_here]
-    grad_g = packed[:, heads_here : 2 * heads_here]
+    forward_g = packed[:, heads_here : 2 * heads_here]
     key_own = packed[:, 2 * heads_here]
     value_own = packed[:, 2 * heads_here + 1]
-    logsum_g = rows[:heads_here]
-    delta_g = rows[heads_here : 2 * heads_here]
-    start_g = jnp.round(rows[2 * heads_here]).astype(jnp.int32)
+    side_g = packed[:, 2 * heads_here + 2]
     tokens = query_g.shape[0]
+    logsum_g = join_three(side_g[:, : 3 * heads_here].reshape(tokens, heads_here, 3)).T
+    start_g = jnp.round(join_three(side_g[:, 3 * heads_here : 3 * heads_here + 3])).astype(
+        jnp.int32
+    )
+    delta_g = jnp.einsum("tgd,tgd->gt", forward_g, grad_g, preferred_element_type=jnp.float32)
     base = lax.axis_index("sh") * tokens
     far = shifted(jnp.stack([key_own, value_own]), "sh", 1)
     keys = jnp.concatenate([far[0], key_own], axis=0)
@@ -100,23 +122,23 @@
         query_g, grad_g, logsum_g, delta_g, start_g, base, keys, values
     )
     back = shifted(
-        jnp.stack([key_sum[:WINDOW_LENGTH], value_sum[:WINDOW_LENGTH]]), "sh", -1
+        jnp.stack([key_sum[:WINDOW_LENGTH], value_sum[:WINDOW_LENGTH]]).astype(jnp.bfloat16),
+        "sh",
+        -1,
     )
-    key_total = key_sum[WINDOW_LENGTH:] + back[0]
-    value_total = value_sum[WINDOW_LENGTH:] + back[1]
+    key_total = key_sum[WINDOW_LENGTH:] + back[0].astype(jnp.float32)
+    value_total = value_sum[WINDOW_LENGTH:] + back[1].astype(jnp.float32)
     query_grad = (query_sum * score_scale).astype(jnp.bfloat16)
     key_grad = (key_total * score_scale).astype(jnp.bfloat16)[:, None]
     value_grad = value_total.astype(jnp.bfloat16)[:, None]
     outs = jnp.concatenate([query_grad, key_grad, value_grad], axis=1)
     items = outs.shape[1]
-    outs = lax.all_to_all(outs, "sl", split_axis=0, concat_axis=1, tiled=True)
-    outs = lax.all_to_all(outs, "head", split_axis=0, concat_axis=1, tiled=True)
-    head_size = lax.axis_size("head")
-    outs = outs.reshape(outs.shape[0], head_size, ring, items, depth)
+    outs = lax.all_to_all(outs, ("sl", "head"), split_axis=0, concat_axis=1, tiled=True)
     rows_out = outs.shape[0]
-    query_out = outs[:, :, :, :group].reshape(rows_out, -1, depth)
-    key_out = outs[:, :, :, group].reshape(rows_out, -1, depth)
-    value_out = outs[:, :, :, group + 1].reshape(rows_out, -1, depth)
+    outs = outs.reshape(rows_out, ring, head_size, items, depth).transpose(0, 2, 1, 3, 4)
+    query_out = outs[:, :, :, :heads_here].reshape(rows_out, -1, depth)
+    key_out = outs[:, :, :, heads_here].reshape(rows_out, -1, depth)
+    value_out = outs[:, :, :, heads_here + 1].reshape(rows_out, -1, depth)
     return query_out, key_out, value_out
 
 

time: 144 us -> 131 us (0.910)
  waiting for transfers between devices: 64.3 us -> 53.4 us
  local copies, waits for them, and re-layouts: 9.75 us -> 20 us
  blocking collectives: 31.7 us -> 22.2 us
  starting transfers between devices: 19.3 us -> 16.4 us
    ppermute x2, waiting for transfers between devices: 33.6 us -> 23.2 us  [shifted(): return lax.ppermute(value, axis, pairs)]
    all_to_all x2 -> x1, blocking collectives: 31.7 us -> 22.2 us  [on_device(): lax.all_to_all(outs, ('sl', 'head'), split_axis=0, concat_axis=1, tiled=T...]
    all_to_all x2 -> x1, waiting for transfers between devices: 11.6 us -> 8 us  [on_device(): lax.all_to_all(grad_rows, ('sl', 'head'), split_axis=1, concat_axis=0, ti...]
    squeeze x0 -> x1, local copies, waits for them, and re-layouts: none -> 3.38 us  [on_device(): lax.all_to_all(packed, 'sl', split_axis=1, concat_axis=0, tiled=True)[:, 0]]
    all_to_all x1, waiting for transfers between devices: 19 us -> 22.2 us  [on_device(): lax.all_to_all(packed, 'sl', split_axis=1, concat_axis=0, tiled=True)[:, 0]]
    all_to_all x2 -> x1, starting transfers between devices: 8.07 us -> 5.21 us  [on_device(): lax.all_to_all(grad_rows, ('sl', 'head'), split_axis=1, concat_axis=0, ti...]
    all_to_all x1, local copies, waits for them, and re-layouts: 0.1 us -> 2.7 us  [on_device(): lax.all_to_all(packed, 'sl', split_axis=1, concat_axis=0, tiled=True)[:, 0]]
    concatenate x2 -> x0, other arithmetic: 2.03 us -> none  [the longest x1 1.39 us: on_device(): jnp.concatenate([queries.reshape(local_tokens, ring, group * key_heads //...]
  transfers between devices with their start and end apart: 5 -> 4, of which waited for: 5 -> 4; matrix products, arithmetic and copies ran while one was open for 4% -> 5% of each run, Pallas kernels for 0% -> 0%
where the time goes in v4:
time: 131 us
  waiting for transfers between devices  53.4 us (41%)
  blocking collectives  22.2 us (17%)
  local copies, waits for them, and re-layouts  20 us (15%)
  starting transfers between devices  16.4 us (13%)
  matrix products  10.9 us (8%)
  other arithmetic  6.56 us (5%)
    ppermute x2, waiting for transfers between devices, shifted(): return lax.ppermute(value, axis, pairs)  23.2 us
    all_to_all x1, blocking collectives, on_device(): lax.all_to_all(outs, ('sl', 'head'), split_axis=0, concat_axis=1, tiled=T...  22.2 us
    all_to_all x1, waiting for transfers between devices, on_device(): lax.all_to_all(packed, 'sl', split_axis=1, concat_axis=0, tiled=True)[:, 0]  22.2 us
    all_to_all x1, waiting for transfers between devices, on_device(): lax.all_to_all(grad_rows, ('sl', 'head'), split_axis=1, concat_axis=0, ti...  8 us
    ppermute x2, starting transfers between devices, shifted(): return lax.ppermute(value, axis, pairs)  7.63 us
    unnamed x32, local copies, waits for them, and re-layouts  6.8 us
    all_to_all x1, starting transfers between devices, on_device(): lax.all_to_all(grad_rows, ('sl', 'head'), split_axis=1, concat_axis=0, ti...  5.21 us
    dot_general x1, matrix products, band_terms(): jnp.einsum('tigd,tjd->tgij', grad_t, value_w, preferred_element_type=jnp....  4.29 us
  transfers between devices with their start and end apart: 4, of which 4 were waited for; matrix products, arithmetic and copies ran while one was open for 5% of the time, Pallas kernels for 0%

profile of v4, /device:TPU:4, one launch (start us, length us, event | category | flops | bytes accessed | tf_op | source)
XLA Modules:
  0.0 130.8 jit_solution(18021831941188493789)
XLA Ops:
  0.7 1.3 copy.142
  2.0 0.0 copy-start.5
  2.0 0.8 copy.143
  2.8 5.2 %all-to-all-start.1 = ((bf16[64,16,2,128]{3,0,2,1:T(8,128)(2,1)}), bf16[64,16,2,128]{3,0,2,1:T(8,128)(2,1)S(1)}, u32[]{:S(2)}, u32[]{:S(2)}) async-start(bf16[64,16,2,128]{3,0,2,1:T(8,128)(2,1)} %bitcast.42), calls=%async_computation.1 | async-start | bytes 1048576 | tf_op jit(solution)/shard_map/all_to_all | solution.py:81
  8.0 0.0 copy-start.6
  8.2 0.1 fusion.60
  8.3 0.2 copy.136
  8.5 0.0 copy-start.7
  8.5 0.1 copy.129
  8.7 0.1 copy.130
  8.7 0.1 constant_dynamic-update-slice_fusion.1
  8.8 0.2 copy-done.6
  9.0 0.1 bitcast_dynamic-update-slice_fusion.1
  9.1 0.4 copy-done.7
  9.5 0.1 bitcast_dynamic-update-slice_fusion
  9.6 1.2 copy-done
  10.9 8.0 %all-to-all-done.1 = bf16[64,16,2,128]{3,0,2,1:T(8,128)(2,1)S(1)} async-done(((bf16[64,16,2,128]{3,0,2,1:T(8,128)(2,1)}), bf16[64,16,2,128]{3,0,2,1:T(8,128)(2,1)S(1)}, u32[]{:S(2)}, u32[]{:S(2)}) %all-to-all-start.1) | async-done | bytes 524320 | tf_op jit(solution)/shard_map/all_to_all | solution.py:81
  18.9 3.6 %all-to-all-start = ((bf16[256,4,7,128]{3,0,2,1:T(8,128)(2,1)}), bf16[256,4,7,128]{3,0,2,1:T(8,128)(2,1)S(1)}, u32[]{:S(2)}, u32[]{:S(2)}) async-start(bf16[256,4,7,128]{3,0,2,1:T(8,128)(2,1)} %copy-done), calls=%async_computation | async-start | bytes 3670016 | tf_op jit(solution)/shard_map/all_to_all | solution.py:105
  22.5 0.1 iota_add_fusion.1
  22.5 0.1 iota_add_fusion
  22.6 0.8 copy.144
  23.5 22.2 %all-to-all-done = bf16[256,4,7,128]{3,0,2,1:T(8,128)(2,1)S(1)} async-done(((bf16[256,4,7,128]{3,0,2,1:T(8,128)(2,1)}), bf16[256,4,7,128]{3,0,2,1:T(8,128)(2,1)S(1)}, u32[]{:S(2)}, u32[]{:S(2)}) %all-to-all-start) | async-done | bytes 1835040 | tf_op jit(solution)/shard_map/all_to_all | solution.py:105
  45.6 2.7 %copy.137 = bf16[4,256,1,7,128]{1,0,4,3,2:T(4,128)(2,1)} copy(bf16[4,256,1,7,128]{4,1,3,0,2:T(8,128)(2,1)S(1)} %bitcast.202) | data formatting | bytes 3670016 | tf_op jit(solution)/shard_map/all_to_all | solution.py:105
  48.3 3.4 %squeeze.14 = bf16[1024,7,128]{0,2,1:T(8,128)(2,1)S(1)} reshape(bf16[4,256,1,7,128]{1,0,4,3,2:T(4,128)(2,1)} %copy.137) | data formatting | bytes 3670016 | tf_op jit(solution)/shard_map/squeeze | solution.py:105
  51.7 1.0 slice_bitcast_fusion.14
  52.7 0.9 fusion.38
  53.6 0.8 pad_maximum_fusion.1
  54.5 3.8 %collective-permute-start = (bf16[2,1024,128]{1,2,0:T(8,128)(2,1)}, bf16[2,1024,128]{1,2,0:T(8,128)(2,1)}, u32[]{:S(2)}, u32[]{:S(2)}) collective-permute-start(bf16[2,1024,128]{1,2,0:T(8,128)(2,1)} %pad_maximum_fusion.1), channel_id=1, source_target_pairs={{0,4},{4,8},{8,12},{12,16},{16,20},{20,24},{24,28},{28,32},{32,36}... | collective-permute-start | bytes 1572872 | tf_op jit(solution)/shard_map/ppermute | solution.py:16
  58.3 1.3 %copy.138 = bf16[1024,2,128]{2,0,1:T(8,128)(2,1)S(1)} copy(bf16[1024,2,128]{0,2,1:T(8,128)(2,1)} %get-tuple-element.117) | data formatting | bytes 1048576 | tf_op jit(solution)/shard_map/slice | solution.py:106
  59.7 0.0 copy-start.3
  59.7 0.3 copy.168
  60.1 0.0 copy-start.2
  60.1 0.4 multiply_reduce_fusion
  60.5 1.9 %fusion.11 = pred[4,256,1280]{1,2,0:T(8,128)(4,1)S(1)} fusion(s32[4,256]{1,0:T(4,128)S(1)} %convert_element_type.72, s32[4,1280]{1,0:T(4,128)S(1)} %iota_add_fusion, s32[4,256]{1,0:T(4,128)S(1)} %iota_add_fusion.1), kind=kLoop, calls=%fused_computation.14 | loop fusion | flops 7864320 | bytes 1339392 | tf_op jit(solution)/shard_map/and | solution.py:34
  62.3 14.6 %collective-permute-done = bf16[2,1024,128]{1,2,0:T(8,128)(2,1)} collective-permute-done((bf16[2,1024,128]{1,2,0:T(8,128)(2,1)}, bf16[2,1024,128]{1,2,0:T(8,128)(2,1)}, u32[]{:S(2)}, u32[]{:S(2)}) %collective-permute-start) | collective-permute-done | bytes 524320 | tf_op jit(solution)/shard_map/ppermute | solution.py:16
  76.9 1.1 slice_bitcast_fusion.11
  78.0 0.1 fusion.54
  78.1 0.1 fusion.48
  78.2 1.6 %fusion.34 = f32[4,1280,256,2]{2,1,3,0:T(8,128)S(1)} fusion(bf16[1,1280,128]{1,2,0:T(8,128)(2,1)S(1)} %get-tuple-element.130, bf16[1,1280,128]{1,2,0:T(8,128)(2,1)S(1)} %get-tuple-element.131, bf16[1,1280,128]{1,2,0:T(8,128)(2,1)S(1)} %get-tuple-element.129, bf16[1,1280,128]{1,2,0:T(8,128)(2,1)S(1)} %get-tuple-element.128, ...), kind=kOutput, calls=%fused_computation.61 | convolution fusion | flops 676331520 | bytes 12320768 | tf_op jit(solution)/shard_map/tigd,tjd->tgij/dot_general | solution.py:36
  79.7 2.7 %fusion.13 = f32[4,1280,128]{2,1,0:T(8,128)S(1)} fusion(f32[4,1280,256,2]{2,1,3,0:T(8,128)S(1)} %fusion.34, f32[4,2,256]{2,1,0:T(2,128)S(1)} %bitcast.221, pred[4,256,1280]{1,2,0:T(8,128)(4,1)S(1)} %fusion.11, bf16[4,256,2,128]{3,1,0,2:T(8,128)(2,1)S(1)} %bitcast.209), kind=kOutput, calls=%fused_computation.16 | convolution fusion | flops 681574400 | bytes 14950400 | tf_op jit(solution)/shard_map/tgij,tigd->tjd/dot_general | solution.py:45
  82.4 4.3 %fusion.1 = bf16[4,2,256,1280]{2,3,1,0:T(8,128)(2,1)S(1)} fusion(f32[4,1280,256,2]{2,1,3,0:T(8,128)S(1)} %fusion.34, f32[4,2,256]{2,1,0:T(2,128)S(1)} %bitcast.220, f32[4,2,256]{2,1,0:T(2,128)S(1)} %bitcast.222, pred[4,256,1280]{1,2,0:T(8,128)(4,1)S(1)} %fusion.11, bf16[1,1280,128]{1,2,0:T(8,128)(2,1)S(1)} %get-tuple-element.124, ...), kind=kOutput, calls=%fused_computation.2 | convolution fusion | flops 692060160 | bytes 18890752 | tf_op jit(solution)/shard_map/tigd,tjd->tgij/dot_general | solution.py:40
  86.7 1.5 %convolution_bitcast_fusion = f32[4,1280,128]{2,1,0:T(8,128)S(1)} fusion(bf16[4,2,256,1280]{2,3,1,0:T(8,128)(2,1)S(1)} %fusion.1, bf16[4,256,2,128]{3,1,0,2:T(8,128)(2,1)S(1)} %bitcast.204), kind=kOutput, calls=%fused_computation.17 | convolution fusion | flops 671088640 | bytes 8388608 | tf_op jit(solution)/shard_map/tgij,tigd->tjd/dot_general | solution.py:44
  88.3 0.1 scatter-add.26
  88.4 0.1 fusion.33
  88.5 0.1 fusion.31
  88.7 0.1 fusion.29
  88.9 0.1 scatter-add.34
  89.0 0.1 fusion.28
  89.1 0.1 fusion.26
  89.3 0.1 fusion.24
  89.5 0.1 pad_maximum_fusion.2
  89.5 3.8 %collective-permute-start.1 = (bf16[2,1024,128]{2,1,0:T(8,128)(2,1)S(1)}, bf16[2,1024,128]{2,1,0:T(8,128)(2,1)}, u32[]{:S(2)}, u32[]{:S(2)}) collective-permute-start(bf16[2,1024,128]{2,1,0:T(8,128)(2,1)S(1)} %pad_maximum_fusion.2), channel_id=1, source_target_pairs={{4,0},{8,4},{12,8},{16,12},{20,16},{24,20},{28,24},{32,28},{36,32}... | collective-permute-start | bytes 1572872 | tf_op jit(solution)/shard_map/ppermute | solution.py:16
  93.3 0.9 fusion.23
  94.2 0.3 copy.149
  94.5 8.7 %collective-permute-done.1 = bf16[2,1024,128]{2,1,0:T(8,128)(2,1)} collective-permute-done((bf16[2,1024,128]{2,1,0:T(8,128)(2,1)S(1)}, bf16[2,1024,128]{2,1,0:T(8,128)(2,1)}, u32[]{:S(2)}, u32[]{:S(2)}) %collective-permute-start.1) | collective-permute-done | bytes 524320 | tf_op jit(solution)/shard_map/ppermute | solution.py:16
  103.1 1.2 fusion.61
  104.3 0.1 pad_maximum_fusion
  104.4 0.8 copy.152
  105.3 22.2 %all_to_all.45 = bf16[1024,4,128]{2,1,0:T(4,128)(2,1)S(1)} all-to-all(bf16[1024,4,128]{2,1,0:T(4,128)(2,1)S(1)} %copy.152), channel_id=1, replica_groups=mesh['head'=4,'sh'=32,'sl'=4] {'sl','head'}, dimensions={0} | all-to-all | bytes 2097152 | tf_op jit(solution)/shard_map/all_to_all | solution.py:136
  127.5 0.1 copy.153
  127.6 0.1 copy.154
  127.9 1.1 copy.158
  129.0 0.9 copy.159
  129.9 0.9 copy.160
  (42 shorter events, 0.7 us)
Async XLA Ops:
  0.6 7.4 %copy-start.8 = (f32[8,256]{1,0:T(8,128)S(1)}, f32[8,256]{1,0:T(8,128)}, u32[]{:S(2)}) copy-start(f32[8,256]{1,0:T(8,128)} %param.28) | copy-start | bytes 24580
  0.6 7.5 %copy-start.9 = (s32[256]{0:T(256)S(1)}, s32[256]{0:T(256)}, u32[]{:S(2)}) copy-start(s32[256]{0:T(256)} %param.29) | copy-start | bytes 3076
  0.7 7.9 %copy-start.4 = (bf16[256,8,128]{2,1,0:T(8,128)(2,1)S(1)}, bf16[256,8,128]{2,1,0:T(8,128)(2,1)}, u32[]{:S(2)}) copy-start(bf16[256,8,128]{2,1,0:T(8,128)(2,1)} %param.23) | copy-start | bytes 1572868
  2.0 6.7 %copy-start.5 = (bf16[256,8,128]{2,1,0:T(8,128)(2,1)S(1)}, bf16[256,8,128]{2,1,0:T(8,128)(2,1)}, u32[]{:S(2)}) copy-start(bf16[256,8,128]{2,1,0:T(8,128)(2,1)} %param.26) | copy-start | bytes 1572868
  2.8 16.0 %all-to-all-start.1 = ((bf16[64,16,2,128]{3,0,2,1:T(8,128)(2,1)}), bf16[64,16,2,128]{3,0,2,1:T(8,128)(2,1)S(1)}, u32[]{:S(2)}, u32[]{:S(2)}) async-start(bf16[64,16,2,128]{3,0,2,1:T(8,128)(2,1)} %bitcast.42), calls=%async_computation.1 | async-start | bytes 1048576 | tf_op jit(solution)/shard_map/all_to_all | solution.py:81
  8.0 1.0 copy-start.6
  8.5 1.0 copy-start.7
  9.6 1.2 copy-start
  18.9 26.8 %all-to-all-start = ((bf16[256,4,7,128]{3,0,2,1:T(8,128)(2,1)}), bf16[256,4,7,128]{3,0,2,1:T(8,128)(2,1)S(1)}, u32[]{:S(2)}, u32[]{:S(2)}) async-start(bf16[256,4,7,128]{3,0,2,1:T(8,128)(2,1)} %copy-done), calls=%async_computation | async-start | bytes 3670016 | tf_op jit(solution)/shard_map/all_to_all | solution.py:105
  53.6 6.5 %copy-start.1 = (bf16[16,64,1,2,128]{4,1,0,3,2:T(8,128)(2,1)S(1)}, bf16[16,64,1,2,128]{4,1,0,3,2:T(8,128)(2,1)}, u32[]{:S(2)}) copy-start(bf16[16,64,1,2,128]{4,1,0,3,2:T(8,128)(2,1)} %copy.144) | copy-start | bytes 1572868
  54.5 22.4 %collective-permute-start = (bf16[2,1024,128]{1,2,0:T(8,128)(2,1)}, bf16[2,1024,128]{1,2,0:T(8,128)(2,1)}, u32[]{:S(2)}, u32[]{:S(2)}) collective-permute-start(bf16[2,1024,128]{1,2,0:T(8,128)(2,1)} %pad_maximum_fusion.1), channel_id=1, source_target_pairs={{0,4},{4,8},{8,12},{12,16},{16,20},{20,24},{24,28},{28,32},{32,36}... | collective-permute-start | bytes 1572872 | tf_op jit(solution)/shard_map/ppermute | solution.py:16
  59.7 18.2 %copy-start.3 = (bf16[1024,128]{0,1:T(8,128)(2,1)S(1)}, bf16[1024,128]{0,1:T(8,128)(2,1)}, u32[]{:S(2)}) copy-start(bf16[1024,128]{0,1:T(8,128)(2,1)} %get-tuple-element.112) | copy-start | bytes 786436
  60.1 18.0 %copy-start.2 = (bf16[1024,128]{0,1:T(8,128)(2,1)S(1)}, bf16[1024,128]{0,1:T(8,128)(2,1)}, u32[]{:S(2)}) copy-start(bf16[1024,128]{0,1:T(8,128)(2,1)} %get-tuple-element.111) | copy-start | bytes 786436
  89.5 13.6 %collective-permute-start.1 = (bf16[2,1024,128]{2,1,0:T(8,128)(2,1)S(1)}, bf16[2,1024,128]{2,1,0:T(8,128)(2,1)}, u32[]{:S(2)}, u32[]{:S(2)}) collective-permute-start(bf16[2,1024,128]{2,1,0:T(8,128)(2,1)S(1)} %pad_maximum_fusion.2), channel_id=1, source_target_pairs={{4,0},{8,4},{12,8},{16,12},{20,16},{24,20},{28,24},{32,28},{36,32}... | collective-permute-start | bytes 1572872 | tf_op jit(solution)/shard_map/ppermute | solution.py:16

commit v5 on v4

v5 whole, which is shorter than its diff:
```python
import jax
import jax.numpy as jnp
from jax import lax
from jax.sharding import Mesh
from jax.sharding import PartitionSpec as P

WINDOW_LENGTH = 1024
BLOCK = 256

score_scale = 168.0 ** (-0.5)


def shifted(value, axis, by):
    size = lax.axis_size(axis)
    pairs = [(i, i + by) for i in range(size) if 0 <= i + by < size]
    return lax.ppermute(value, axis, pairs)


def band_terms(query, grad, logsum, delta, start, base, keys, values):
    group, tokens, depth = query.shape
    tiles = tokens // BLOCK
    span = WINDOW_LENGTH + BLOCK
    query_t = query.reshape(group, tiles, BLOCK, depth)
    grad_t = grad.reshape(group, tiles, BLOCK, depth)
    logsum_t = logsum.reshape(group, tiles, BLOCK).transpose(1, 0, 2)
    delta_t = delta.reshape(group, tiles, BLOCK).transpose(1, 0, 2)
    start_t = start.reshape(tiles, BLOCK)
    key_w = jnp.stack([keys[t * BLOCK : t * BLOCK + span] for t in range(tiles)])
    value_w = jnp.stack([values[t * BLOCK : t * BLOCK + span] for t in range(tiles)])
    tile_base = base + BLOCK * jnp.arange(tiles, dtype=jnp.int32)
    query_place = tile_base[:, None] + jnp.arange(BLOCK, dtype=jnp.int32)[None, :]
    key_place = tile_base[:, None] - WINDOW_LENGTH + jnp.arange(span, dtype=jnp.int32)[None, :]
    gap = query_place[:, :, None] - key_place[:, None, :]
    visible = (gap >= 0) & (gap < WINDOW_LENGTH) & (key_place[:, None, :] >= start_t[:, :, None])
    scores = (
        jnp.einsum("gtid,tjd->tgij", query_t, key_w, preferred_element_type=jnp.float32)
        * score_scale
    )
    probs = jnp.where(visible[:, None], jnp.exp(scores - logsum_t[..., None]), 0.0)
    dprobs = jnp.einsum("gtid,tjd->tgij", grad_t, value_w, preferred_element_type=jnp.float32)
    low_scores = (probs * (dprobs - delta_t[..., None])).astype(jnp.bfloat16)
    low_probs = probs.astype(jnp.bfloat16)
    query_term = jnp.einsum("tgij,tjd->tigd", low_scores, key_w, preferred_element_type=jnp.float32)
    key_w_term = jnp.einsum("tgij,gtid->tjd", low_scores, query_t, preferred_element_type=jnp.float32)
    value_w_term = jnp.einsum("tgij,gtid->tjd", low_probs, grad_t, preferred_element_type=jnp.float32)
    total = WINDOW_LENGTH + tokens
    key_term = jnp.zeros((total, depth), jnp.float32)
    value_term = jnp.zeros((total, depth), jnp.float32)
    for t in range(tiles):
        key_term = key_term.at[t * BLOCK : t * BLOCK + span].add(key_w_term[t])
        value_term = value_term.at[t * BLOCK : t * BLOCK + span].add(value_w_term[t])
    return query_term.reshape(tokens, group, depth), key_term, value_term


def split_three(x):
    hi = lax.reduce_precision(x, exponent_bits=8, mantissa_bits=7)
    rest = x - hi
    mid = lax.reduce_precision(rest, exponent_bits=8, mantissa_bits=7)
    lo = rest - mid
    return jnp.stack([hi, mid, lo], axis=-1).astype(jnp.bfloat16)


def join_three(parts):
    parts = parts.astype(jnp.float32)
    return (parts[..., 0] + parts[..., 1]) + parts[..., 2]


def on_device(
    queries, normed_keys, value_matrix, forward_out, output_gradient, row_log_total, pair_start
):
    ring = lax.axis_size("sl")
    head_size = lax.axis_size("head")
    local_tokens, heads_local, depth = queries.shape
    kv_local = normed_keys.shape[1]
    heads_here = heads_local // ring
    kv_here = kv_local // ring
    grad_rows = output_gradient.shape[0]
    grad_g = output_gradient.reshape(grad_rows, head_size, ring, heads_here, depth)
    grad_g = grad_g.transpose(2, 1, 3, 0, 4).reshape(ring * head_size, heads_here, grad_rows, depth)
    grad_g = lax.all_to_all(grad_g, ("sl", "head"), split_axis=0, concat_axis=2, tiled=True)[0]
    logsum = row_log_total.reshape(ring, heads_here, local_tokens).transpose(0, 2, 1)
    side = jnp.concatenate(
        [
            split_three(logsum).reshape(ring, local_tokens, heads_here * 3),
            jnp.broadcast_to(
                split_three(pair_start.astype(jnp.float32))[None], (ring, local_tokens, 3)
            ),
        ],
        axis=2,
    )
    side = jnp.pad(side, ((0, 0), (0, 0), (0, depth - side.shape[2])))
    kv_packed = jnp.concatenate(
        [
            normed_keys.reshape(local_tokens, ring * kv_here, depth).transpose(1, 0, 2)[:, None],
            value_matrix.reshape(local_tokens, ring * kv_here, depth).transpose(1, 0, 2)[:, None],
            side[:, None],
        ],
        axis=1,
    )
    kv_packed = lax.all_to_all(kv_packed, "sl", split_axis=0, concat_axis=2, tiled=True)[0]
    far = shifted(kv_packed[:2], "sh", 1)
    key_own = kv_packed[0]
    value_own = kv_packed[1]
    side_g = kv_packed[2]
    tokens = key_own.shape[0]
    logsum_g = join_three(side_g[:, : 3 * heads_here].reshape(tokens, heads_here, 3)).T
    start_g = jnp.round(join_three(side_g[:, 3 * heads_here : 3 * heads_here + 3])).astype(
        jnp.int32
    )
    qf_packed = jnp.concatenate(
        [
            queries.reshape(local_tokens, ring, heads_here, depth).transpose(1, 2, 0, 3),
            forward_out.reshape(local_tokens, ring, heads_here, depth).transpose(1, 2, 0, 3),
        ],
        axis=1,
    )
    qf_packed = lax.all_to_all(qf_packed, "sl", split_axis=0, concat_axis=2, tiled=True)[0]
    query_g = qf_packed[:heads_here]
    forward_g = qf_packed[heads_here:]
    delta_g = jnp.einsum("gtd,gtd->gt", forward_g, grad_g, preferred_element_type=jnp.float32)
    base = lax.axis_index("sh") * tokens
    keys = jnp.concatenate([far[0], key_own], axis=0)
    values = jnp.concatenate([far[1], value_own], axis=0)
    query_sum, key_sum, value_sum = band_terms(
        query_g, grad_g, logsum_g, delta_g, start_g, base, keys, values
    )
    back = shifted(
        jnp.stack([key_sum[:WINDOW_LENGTH], value_sum[:WINDOW_LENGTH]]).astype(jnp.bfloat16),
        "sh",
        -1,
    )

    def to_tokens(x):
        items = x.shape[1]
        x = lax.all_to_all(x, ("sl", "head"), split_axis=0, concat_axis=1, tiled=True)
        rows_out = x.shape[0]
        return x.reshape(rows_out, ring, head_size, items, depth).transpose(0, 2, 1, 3, 4)

    query_out = to_tokens((query_sum * score_scale).astype(jnp.bfloat16))
    query_out = query_out.reshape(query_out.shape[0], -1, depth)
    key_total = key_sum[WINDOW_LENGTH:] + back[0].astype(jnp.float32)
    value_total = value_sum[WINDOW_LENGTH:] + back[1].astype(jnp.float32)
    key_grad = (key_total * score_scale).astype(jnp.bfloat16)
    value_grad = value_total.astype(jnp.bfloat16)
    kv_out = to_tokens(jnp.stack([key_grad, value_grad], axis=1))
    rows_out = kv_out.shape[0]
    key_out = kv_out[:, :, :, 0].reshape(rows_out, -1, depth)
    value_out = kv_out[:, :, :, 1].reshape(rows_out, -1, depth)
    return query_out, key_out, value_out


def solution(mesh):
    head, seq = mesh.devices.shape
    ring = WINDOW_LENGTH // BLOCK
    grouped = Mesh(mesh.devices.reshape(head, seq // ring, ring), ("head", "sh", "sl"))
    seq_axes = ("sh", "sl")
    placed = (
        P(seq_axes, "head", None),
        P(seq_axes, "head", None),
        P(seq_axes, "head", None),
        P(seq_axes, "head", None),
        P(seq_axes + ("head",), None, None),
        P("head", seq_axes),
        P(seq_axes),
    )
    out = P(seq_axes + ("head",), None, None)
    return jax.shard_map(
        on_device,
        mesh=grouped,
        in_specs=placed,
        out_specs=(out, out, out),
        check_vma=False,
    )
```

time: 131 us -> 127 us (0.969)
  blocking collectives: 22.2 us -> 0 us
  starting transfers between devices: 16.4 us -> 30.8 us
  matrix products: 10.9 us -> 18.2 us
  local copies, waits for them, and re-layouts: 20 us -> 15.6 us
  other arithmetic: 6.56 us -> 9.15 us
  waiting for transfers between devices: 53.4 us -> 51.1 us
    all_to_all x1 -> x0, blocking collectives: 22.2 us -> none  [on_device(): lax.all_to_all(outs, ('sl', 'head'), split_axis=0, concat_axis=1, tiled=T...]
    all_to_all x2 -> x5, starting transfers between devices: 8.79 us -> 23 us  [the longest x2 10.8 us: to_tokens(): lax.all_to_all(x, ('sl', 'head'), split_axis=0, concat_axis=1, tiled=True)]
    ppermute x2, waiting for transfers between devices: 23.2 us -> 10.1 us  [shifted(): return lax.ppermute(value, axis, pairs)]
    all_to_all x2 -> x5, waiting for transfers between devices: 30.2 us -> 40.9 us  [the longest x2 17.8 us: to_tokens(): lax.all_to_all(x, ('sl', 'head'), split_axis=0, concat_axis=1, tiled=True)]
    dot_general x4, matrix products: 10 us -> 15.5 us  [the longest x1 6.1 us: band_terms(): jnp.einsum('tgij,gtid->tjd', low_probs, grad_t, preferred_element_type=jn...]
    squeeze x2 -> x0, local copies, waits for them, and re-layouts: 4.33 us -> none  [the longest x1 3.38 us: on_device(): lax.all_to_all(packed, 'sl', split_axis=1, concat_axis=0, tiled=True)[:, 0]]
    all_to_all x4 -> x3, local copies, waits for them, and re-layouts: 3.76 us -> 0.48 us  [the longest x1 0.37 us: on_device(): lax.all_to_all(kv_packed, 'sl', split_axis=0, concat_axis=2, tiled=True)[0]]
    convert_element_type x1 -> x2, local copies, waits for them, and re-layouts: 0.27 us -> 2.65 us  [on_device(): query_out = to_tokens((query_sum * score_scale).astype(jnp.bfloat16))]
  transfers between devices with their start and end apart: 4 -> 7, of which waited for: 4 -> 6; matrix products, arithmetic and copies ran while one was open for 5% -> 15% of each run, Pallas kernels for 0% -> 0%
where the time goes in v5:
time: 127 us; the launch traced here: 126 us
  waiting for transfers between devices  51.1 us (40%)
  starting transfers between devices  30.8 us (24%)
  matrix products  18.2 us (14%)
  local copies, waits for them, and re-layouts  15.6 us (12%)
  other arithmetic  9.15 us (7%)
    all_to_all x2, waiting for transfers between devices, to_tokens(): lax.all_to_all(x, ('sl', 'head'), split_axis=0, concat_axis=1, tiled=True)  17.8 us
    all_to_all x2, starting transfers between devices, to_tokens(): lax.all_to_all(x, ('sl', 'head'), split_axis=0, concat_axis=1, tiled=True)  10.8 us
    all_to_all x1, waiting for transfers between devices, on_device(): lax.all_to_all(kv_packed, 'sl', split_axis=0, concat_axis=2, tiled=True)[0]  10.5 us
    ppermute x2, waiting for transfers between devices, shifted(): return lax.ppermute(value, axis, pairs)  10.1 us
    all_to_all x1, waiting for transfers between devices, on_device(): lax.all_to_all(grad_g, ('sl', 'head'), split_axis=0, concat_axis=2, tiled...  8.41 us
    ppermute x2, starting transfers between devices, shifted(): return lax.ppermute(value, axis, pairs)  7.85 us
    dot_general x1, matrix products, band_terms(): jnp.einsum('tgij,gtid->tjd', low_probs, grad_t, preferred_element_type=jn...  6.1 us
    dot_general x1, matrix products, band_terms(): jnp.einsum('gtid,tjd->tgij', grad_t, value_w, preferred_element_type=jnp....  5.91 us
  transfers between devices with their start and end apart: 7, of which 6 were waited for; matrix products, arithmetic and copies ran while one was open for 15% of the time, Pallas kernels for 0%

profile of v5, /device:TPU:4, one launch (start us, length us, event | category | flops | bytes accessed | tf_op | source)
XLA Modules:
  0.0 126.0 jit_solution(8916972195658639818)
XLA Ops:
  0.7 1.3 %copy.144 = bf16[64,32,128]{2,0,1:T(8,128)(2,1)S(1)} copy(bf16[64,32,128]{2,1,0:T(8,128)(2,1)} %param.27) | data formatting | bytes 1048576 | tf_op args[4]
  2.0 0.8 copy.145
  2.8 5.2 %all-to-all-start.2 = ((bf16[16,2,64,128]{3,2,1,0:T(8,128)(2,1)}), bf16[16,2,64,128]{3,2,1,0:T(8,128)(2,1)S(1)}, u32[]{:S(2)}, u32[]{:S(2)}) async-start(bf16[16,2,64,128]{3,2,1,0:T(8,128)(2,1)} %bitcast.46), calls=%async_computation.2 | async-start | bytes 1048576 | tf_op jit(solution)/shard_map/all_to_all | solution.py:80
  8.2 0.2 copy.134
  8.4 0.2 copy.133
  8.6 0.0 copy-start.7
  8.7 0.1 fusion.58
  8.8 0.0 copy-start.8
  8.8 0.7 pad_maximum_fusion.1
  9.4 1.0 copy.138
  10.4 8.4 %all-to-all-done.2 = bf16[16,2,64,128]{3,2,1,0:T(8,128)(2,1)S(1)} async-done(((bf16[16,2,64,128]{3,2,1,0:T(8,128)(2,1)}), bf16[16,2,64,128]{3,2,1,0:T(8,128)(2,1)S(1)}, u32[]{:S(2)}, u32[]{:S(2)}) %all-to-all-start.2) | async-done | bytes 524320 | tf_op jit(solution)/shard_map/all_to_all | solution.py:80
  18.9 3.5 %all-to-all-start = ((bf16[4,3,256,128]{2,3,1,0:T(8,128)(2,1)}), bf16[4,3,256,128]{2,3,1,0:T(8,128)(2,1)S(1)}, u32[]{:S(2)}, u32[]{:S(2)}) async-start(bf16[4,3,256,128]{2,3,1,0:T(8,128)(2,1)} %copy.138), calls=%async_computation | async-start | bytes 1572864 | tf_op jit(solution)/shard_map/all_to_all | solution.py:100
  22.4 0.1 iota_add_fusion.1
  22.4 0.1 copy.141
  22.5 0.1 copy.140
  22.6 1.1 pad_maximum_fusion
  23.7 0.1 iota_add_fusion
  23.8 10.5 %all-to-all-done = bf16[4,3,256,128]{2,3,1,0:T(8,128)(2,1)S(1)} async-done(((bf16[4,3,256,128]{2,3,1,0:T(8,128)(2,1)}), bf16[4,3,256,128]{2,3,1,0:T(8,128)(2,1)S(1)}, u32[]{:S(2)}, u32[]{:S(2)}) %all-to-all-start) | async-done | bytes 786464 | tf_op jit(solution)/shard_map/all_to_all | solution.py:100
  34.3 3.5 %all-to-all-start.1 = ((bf16[4,4,256,128]{3,2,1,0:T(8,128)(2,1)}), bf16[4,4,256,128]{3,2,1,0:T(8,128)(2,1)S(1)}, u32[]{:S(2)}, u32[]{:S(2)}) async-start(bf16[4,4,256,128]{3,2,1,0:T(8,128)(2,1)} %pad_maximum_fusion), calls=%async_computation.1 | async-start | bytes 2097152 | tf_op jit(solution)/shard_map/all_to_all | solution.py:117
  37.8 0.4 copy.139
  38.2 0.8 slice.328
  39.0 0.8 fusion.73
  39.9 4.0 %collective-permute-start = (bf16[2,1024,128]{2,1,0:T(8,128)(2,1)}, bf16[2,1024,128]{2,1,0:T(8,128)(2,1)}, u32[]{:S(2)}, u32[]{:S(2)}) collective-permute-start(bf16[2,1024,128]{2,1,0:T(8,128)(2,1)} %bitcast.14), channel_id=1, source_target_pairs={{0,4},{4,8},{8,12},{12,16},{16,20},{20,24},{24,28},{28,32},{32,36}... | collective-permute-start | bytes 1572872 | tf_op jit(solution)/shard_map/ppermute | solution.py:16
  43.9 0.1 slice_convert_fusion.2
  44.0 0.1 copy.180
  44.2 0.5 fusion.38
  44.8 0.0 copy-start.6
  44.8 2.7 %fusion.8 = pred[4,256,1280]{2,1,0:T(8,128)(4,1)} fusion(s32[4,256]{1,0:T(4,128)S(1)} %convert_element_type.72, s32[4,1280]{1,0:T(4,128)S(1)} %iota_add_fusion, s32[4,256]{1,0:T(4,128)S(1)} %iota_add_fusion.1), kind=kLoop, calls=%fused_computation.11 | loop fusion | flops 7864320 | bytes 1339392 | tf_op jit(solution)/shard_map/and | solution.py:34
  47.5 4.3 %all-to-all-done.1 = bf16[4,4,256,128]{3,2,1,0:T(8,128)(2,1)S(1)} async-done(((bf16[4,4,256,128]{3,2,1,0:T(8,128)(2,1)}), bf16[4,4,256,128]{3,2,1,0:T(8,128)(2,1)S(1)}, u32[]{:S(2)}, u32[]{:S(2)}) %all-to-all-start.1) | async-done | bytes 1048608 | tf_op jit(solution)/shard_map/all_to_all | solution.py:117
  51.8 0.0 copy-start.5
  51.8 0.4 fusion.21
  52.2 10.1 %collective-permute-done = bf16[2,1024,128]{2,1,0:T(8,128)(2,1)} collective-permute-done((bf16[2,1024,128]{2,1,0:T(8,128)(2,1)}, bf16[2,1024,128]{2,1,0:T(8,128)(2,1)}, u32[]{:S(2)}, u32[]{:S(2)}) %collective-permute-start) | collective-permute-done | bytes 524320 | tf_op jit(solution)/shard_map/ppermute | solution.py:16
  62.3 1.1 slice_bitcast_fusion.13
  63.4 0.2 fusion.52
  63.6 1.3 %fusion.46 = (bf16[1,1280,128]{2,1,0:T(8,128)(2,1)}, bf16[1,1280,128]{2,1,0:T(8,128)(2,1)}, bf16[1,1280,128]{2,1,0:T(8,128)(2,1)}, bf16[1,1280,128]{2,1,0:T(8,128)(2,1)}) fusion(bf16[1024,128]{1,0:T(8,128)(2,1)S(1)} %get-tuple-element.122, bf16[1024,128]{1,0:T(8,128)(2,1)S(1)} %bitcast.216), kind=kLoop, calls=%fused_computation.85 | loop fusion | flops 2621440 | bytes 1835008 | tf_op jit(solution)/shard_map/stack | solution.py:29
  64.8 1.5 %fusion.32 = f32[4,2,256,1280]{3,2,1,0:T(8,128)S(1)} fusion(bf16[1,1280,128]{2,1,0:T(8,128)(2,1)S(1)} %get-tuple-element.126, bf16[1,1280,128]{2,1,0:T(8,128)(2,1)S(1)} %get-tuple-element.127, bf16[1,1280,128]{2,1,0:T(8,128)(2,1)S(1)} %get-tuple-element.125, bf16[1,1280,128]{2,1,0:T(8,128)(2,1)S(1)} %get-tuple-element.124, ...), kind=kOutput, calls=%fused_computation.60 | convolution fusion | flops 673054720 | bytes 12320768 | tf_op jit(solution)/shard_map/gtid,tjd->tgij/dot_general | solution.py:36
  66.4 6.1 %fusion.10 = f32[4,1280,128]{2,1,0:T(8,128)} fusion(f32[4,2,256,1280]{3,2,1,0:T(8,128)S(1)} %fusion.32, f32[4,2,256]{2,1,0:T(2,128)S(1)} %bitcast.224, pred[4,256,1280]{2,1,0:T(8,128)(4,1)} %fusion.8, bf16[2,4,256,128]{3,2,1,0:T(8,128)(2,1)S(1)} %bitcast.205), kind=kOutput, calls=%fused_computation.13 | convolution fusion | flops 681574400 | bytes 14950400 | tf_op jit(solution)/shard_map/tgij,gtid->tjd/dot_general | solution.py:45
  72.5 5.9 %fusion = bf16[4,2,256,1280]{3,2,1,0:T(8,128)(2,1)S(1)} fusion(f32[4,2,256,1280]{3,2,1,0:T(8,128)S(1)} %fusion.32, f32[4,2,256]{2,1,0:T(2,128)S(1)} %bitcast.223, f32[4,2,256]{2,1,0:T(2,128)S(1)} %bitcast.225, pred[4,256,1280]{2,1,0:T(8,128)(4,1)} %fusion.8, bf16[1,1280,128]{2,1,0:T(8,128)(2,1)} %get-tuple-element.120, ...), kind=kOutput, calls=%fused_computation.1 | convolution fusion | flops 692060160 | bytes 18890752 | tf_op jit(solution)/shard_map/gtid,tjd->tgij/dot_general | solution.py:40
  78.4 2.0 %convolution_bitcast_fusion = f32[4,1280,128]{2,1,0:T(8,128)S(1)} fusion(bf16[4,2,256,1280]{3,2,1,0:T(8,128)(2,1)S(1)} %fusion, bf16[1,4,4,256,128]{4,3,1,2,0:T(8,128)(2,1)S(1)} %bitcast.198), kind=kOutput, calls=%fused_computation.14 | convolution fusion | flops 671088640 | bytes 8388608 | tf_op jit(solution)/shard_map/tgij,gtid->tjd/dot_general | solution.py:44
  80.5 0.1 scatter-add.26
  80.6 0.1 fusion.31
  80.7 0.1 fusion.29
  80.9 0.1 fusion.27
  80.9 1.3 %copy-done = f32[4,1280,128]{2,1,0:T(8,128)S(1)} copy-done((f32[4,1280,128]{2,1,0:T(8,128)S(1)}, f32[4,1280,128]{2,1,0:T(8,128)}, u32[]{:S(2)}) %copy-start) | copy-done | bytes 2621464
  82.3 0.1 scatter-add.34
  82.4 0.1 fusion.26
  82.6 0.1 fusion.24
  82.7 0.1 fusion.22
  83.0 0.1 pad_maximum_fusion.2
  83.1 3.9 %collective-permute-start.1 = (bf16[2,1024,128]{2,1,0:T(8,128)(2,1)S(1)}, bf16[2,1024,128]{2,1,0:T(8,128)(2,1)}, u32[]{:S(2)}, u32[]{:S(2)}) collective-permute-start(bf16[2,1024,128]{2,1,0:T(8,128)(2,1)S(1)} %pad_maximum_fusion.2), channel_id=1, source_target_pairs={{4,0},{8,4},{12,8},{16,12},{20,16},{24,20},{28,24},{32,28},{36,32}... | collective-permute-start | bytes 1572872 | tf_op jit(solution)/shard_map/ppermute | solution.py:16
  86.9 2.7 %fusion.20 = bf16[4,256,2,128]{1,3,2,0:T(8,128)(2,1)} fusion(bf16[4,2,256,1280]{3,2,1,0:T(8,128)(2,1)S(1)} %fusion, bf16[1,1280,128]{2,1,0:T(8,128)(2,1)S(1)} %copy-done.2, bf16[1,1280,128]{2,1,0:T(8,128)(2,1)S(1)} %copy-done.4, bf16[1,1280,128]{2,1,0:T(8,128)(2,1)S(1)} %get-tuple-element.125, bf16[1,1280,128]{2,1,0:T(8,128)(2,1)S(1)} %get-tuple-element.124), kind=kOutput, calls=%fused_computation.25 | convolution fusion | flops 676855808 | bytes 7077888 | tf_op jit(solution)/shard_map/tgij,tjd->tigd/dot_general | solution.py:43
  89.6 1.3 %copy.152 = bf16[4,256,2,128]{3,1,0,2:T(8,128)(2,1)S(1)} copy(bf16[4,256,2,128]{1,3,2,0:T(8,128)(2,1)} %fusion.20) | data formatting | bytes 1048576 | tf_op jit(solution)/shard_map/convert_element_type | solution.py:139
  90.9 1.3 %copy.153 = bf16[1024,2,128]{2,1,0:T(2,128)(2,1)} copy(bf16[1024,2,128]{2,0,1:T(8,128)(2,1)S(1)} %bitcast.210) | data formatting | bytes 1048576 | tf_op jit(solution)/shard_map/convert_element_type | solution.py:139
  92.3 7.2 %all-to-all-start.3 = ((bf16[1024,2,128]{2,1,0:T(2,128)(2,1)}), bf16[1024,2,128]{2,1,0:T(2,128)(2,1)S(1)}, u32[]{:S(2)}, u32[]{:S(2)}) async-start(bf16[1024,2,128]{2,1,0:T(2,128)(2,1)} %copy.153), calls=%async_computation.3 | async-start | bytes 1048576 | tf_op jit(solution)/shard_map/all_to_all | solution.py:135
  99.5 1.2 fusion.59
  100.6 0.1 pad_maximum_fusion.3
  100.7 1.4 %copy.160 = bf16[1024,2,128]{2,1,0:T(2,128)(2,1)} copy(bf16[1024,2,128]{2,0,1:T(8,128)(2,1)S(1)} %pad_maximum_fusion.3) | data formatting | bytes 1048576 | tf_op jit(solution)/shard_map/stack | solution.py:145
  102.0 8.2 %all-to-all-done.3 = bf16[1024,2,128]{2,1,0:T(2,128)(2,1)S(1)} async-done(((bf16[1024,2,128]{2,1,0:T(2,128)(2,1)}), bf16[1024,2,128]{2,1,0:T(2,128)(2,1)S(1)}, u32[]{:S(2)}, u32[]{:S(2)}) %all-to-all-start.3) | async-done | bytes 524320 | tf_op jit(solution)/shard_map/all_to_all | solution.py:135
  110.3 3.6 %all-to-all-start.4 = ((bf16[1024,2,128]{2,1,0:T(2,128)(2,1)}), bf16[1024,2,128]{2,1,0:T(2,128)(2,1)S(1)}, u32[]{:S(2)}, u32[]{:S(2)}) async-start(bf16[1024,2,128]{2,1,0:T(2,128)(2,1)} %copy.160), calls=%async_computation.4 | async-start | bytes 1048576 | tf_op jit(solution)/shard_map/all_to_all | solution.py:135
  113.9 0.1 copy.154
  114.0 1.1 copy.162
  115.1 9.5 %all-to-all-done.4 = bf16[1024,2,128]{2,1,0:T(2,128)(2,1)S(1)} async-done(((bf16[1024,2,128]{2,1,0:T(2,128)(2,1)}), bf16[1024,2,128]{2,1,0:T(2,128)(2,1)S(1)}, u32[]{:S(2)}, u32[]{:S(2)}) %all-to-all-start.4) | async-done | bytes 524320 | tf_op jit(solution)/shard_map/all_to_all | solution.py:135
  124.7 0.4 copy.198
  125.1 1.0 fusion.74
  (46 shorter events, 0.6 us)
Async XLA Ops:
  0.6 7.4 %copy-start.12 = (s32[256]{0:T(256)S(1)}, s32[256]{0:T(256)}, u32[]{:S(2)}) copy-start(s32[256]{0:T(256)} %param.29) | copy-start | bytes 3076
  0.6 7.5 %copy-start.11 = (f32[8,256]{1,0:T(8,128)S(1)}, f32[8,256]{1,0:T(8,128)}, u32[]{:S(2)}) copy-start(f32[8,256]{1,0:T(8,128)} %param.28) | copy-start | bytes 24580
  0.7 7.5 %copy-start.9 = (bf16[256,4,128]{2,1,0:T(4,128)(2,1)S(1)}, bf16[256,4,128]{2,1,0:T(4,128)(2,1)}, u32[]{:S(2)}) copy-start(bf16[256,4,128]{2,1,0:T(4,128)(2,1)} %param.25) | copy-start | bytes 786436
  0.7 7.7 %copy-start.10 = (bf16[256,4,128]{2,1,0:T(4,128)(2,1)S(1)}, bf16[256,4,128]{2,1,0:T(4,128)(2,1)}, u32[]{:S(2)}) copy-start(bf16[256,4,128]{2,1,0:T(4,128)(2,1)} %param.24) | copy-start | bytes 786436
  2.8 16.0 %all-to-all-start.2 = ((bf16[16,2,64,128]{3,2,1,0:T(8,128)(2,1)}), bf16[16,2,64,128]{3,2,1,0:T(8,128)(2,1)S(1)}, u32[]{:S(2)}, u32[]{:S(2)}) async-start(bf16[16,2,64,128]{3,2,1,0:T(8,128)(2,1)} %bitcast.46), calls=%async_computation.2 | async-start | bytes 1048576 | tf_op jit(solution)/shard_map/all_to_all | solution.py:80
  8.6 13.8 %copy-start.7 = (bf16[256,8,128]{2,1,0:T(8,128)(2,1)S(1)}, bf16[256,8,128]{2,1,0:T(8,128)(2,1)}, u32[]{:S(2)}) copy-start(bf16[256,8,128]{2,1,0:T(8,128)(2,1)} %param.26) | copy-start | bytes 1572868
  8.8 13.8 %copy-start.8 = (bf16[256,8,128]{2,1,0:T(8,128)(2,1)S(1)}, bf16[256,8,128]{2,1,0:T(8,128)(2,1)}, u32[]{:S(2)}) copy-start(bf16[256,8,128]{2,1,0:T(8,128)(2,1)} %param.23) | copy-start | bytes 1572868
  18.9 15.4 %all-to-all-start = ((bf16[4,3,256,128]{2,3,1,0:T(8,128)(2,1)}), bf16[4,3,256,128]{2,3,1,0:T(8,128)(2,1)S(1)}, u32[]{:S(2)}, u32[]{:S(2)}) async-start(bf16[4,3,256,128]{2,3,1,0:T(8,128)(2,1)} %copy.138), calls=%async_computation | async-start | bytes 1572864 | tf_op jit(solution)/shard_map/all_to_all | solution.py:100
  34.3 17.4 %all-to-all-start.1 = ((bf16[4,4,256,128]{3,2,1,0:T(8,128)(2,1)}), bf16[4,4,256,128]{3,2,1,0:T(8,128)(2,1)S(1)}, u32[]{:S(2)}, u32[]{:S(2)}) async-start(bf16[4,4,256,128]{3,2,1,0:T(8,128)(2,1)} %pad_maximum_fusion), calls=%async_computation.1 | async-start | bytes 2097152 | tf_op jit(solution)/shard_map/all_to_all | solution.py:117
  39.9 22.4 %collective-permute-start = (bf16[2,1024,128]{2,1,0:T(8,128)(2,1)}, bf16[2,1024,128]{2,1,0:T(8,128)(2,1)}, u32[]{:S(2)}, u32[]{:S(2)}) collective-permute-start(bf16[2,1024,128]{2,1,0:T(8,128)(2,1)} %bitcast.14), channel_id=1, source_target_pairs={{0,4},{4,8},{8,12},{12,16},{16,20},{20,24},{24,28},{28,32},{32,36}... | collective-permute-start | bytes 1572872 | tf_op jit(solution)/shard_map/ppermute | solution.py:16
  44.8 18.6 %copy-start.6 = (bf16[1,1,4,256,128]{4,3,2,1,0:T(8,128)(2,1)S(1)}, bf16[1,1,4,256,128]{4,3,2,1,0:T(8,128)(2,1)}, u32[]{:S(2)}) copy-start(bf16[1,1,4,256,128]{4,3,2,1,0:T(8,128)(2,1)} %get-tuple-element.113) | copy-start | bytes 786436
  51.8 11.8 %copy-start.5 = (bf16[1,1,4,256,128]{4,3,2,1,0:T(8,128)(2,1)S(1)}, bf16[1,1,4,256,128]{4,3,2,1,0:T(8,128)(2,1)}, u32[]{:S(2)}) copy-start(bf16[1,1,4,256,128]{4,3,2,1,0:T(8,128)(2,1)} %get-tuple-element.111) | copy-start | bytes 786436
  63.5 2.8 %copy-start.1 = (bf16[1,1280,128]{2,1,0:T(8,128)(2,1)}, bf16[1,1280,128]{2,1,0:T(8,128)(2,1)S(1)}, u32[]{:S(2)}) copy-start(bf16[1,1280,128]{2,1,0:T(8,128)(2,1)S(1)} %get-tuple-element.126) | copy-start | bytes 983044
  63.5 2.8 %copy-start.3 = (bf16[1,1280,128]{2,1,0:T(8,128)(2,1)}, bf16[1,1280,128]{2,1,0:T(8,128)(2,1)S(1)}, u32[]{:S(2)}) copy-start(bf16[1,1280,128]{2,1,0:T(8,128)(2,1)S(1)} %get-tuple-element.127) | copy-start | bytes 983044
  80.6 1.7 %copy-start = (f32[4,1280,128]{2,1,0:T(8,128)S(1)}, f32[4,1280,128]{2,1,0:T(8,128)}, u32[]{:S(2)}) copy-start(f32[4,1280,128]{2,1,0:T(8,128)} %fusion.10) | copy-start | bytes 7864324
  82.8 4.1 %copy-start.2 = (bf16[1,1280,128]{2,1,0:T(8,128)(2,1)S(1)}, bf16[1,1280,128]{2,1,0:T(8,128)(2,1)}, u32[]{:S(2)}) copy-start(bf16[1,1280,128]{2,1,0:T(8,128)(2,1)} %copy-done.1) | copy-start | bytes 983044
  82.8 4.1 %copy-start.4 = (bf16[1,1280,128]{2,1,0:T(8,128)(2,1)S(1)}, bf16[1,1280,128]{2,1,0:T(8,128)(2,1)}, u32[]{:S(2)}) copy-start(bf16[1,1280,128]{2,1,0:T(8,128)(2,1)} %copy-done.3) | copy-start | bytes 983044
  83.1 16.4 %collective-permute-start.1 = (bf16[2,1024,128]{2,1,0:T(8,128)(2,1)S(1)}, bf16[2,1024,128]{2,1,0:T(8,128)(2,1)}, u32[]{:S(2)}, u32[]{:S(2)}) collective-permute-start(bf16[2,1024,128]{2,1,0:T(8,128)(2,1)S(1)} %pad_maximum_fusion.2), channel_id=1, source_target_pairs={{4,0},{8,4},{12,8},{16,12},{20,16},{24,20},{28,24},{32,28},{36,32}... | collective-permute-start | bytes 1572872 | tf_op jit(solution)/shard_map/ppermute | solution.py:16
  92.3 18.0 %all-to-all-start.3 = ((bf16[1024,2,128]{2,1,0:T(2,128)(2,1)}), bf16[1024,2,128]{2,1,0:T(2,128)(2,1)S(1)}, u32[]{:S(2)}, u32[]{:S(2)}) async-start(bf16[1024,2,128]{2,1,0:T(2,128)(2,1)} %copy.153), calls=%async_computation.3 | async-start | bytes 1048576 | tf_op jit(solution)/shard_map/all_to_all | solution.py:135
  110.3 14.4 %all-to-all-start.4 = ((bf16[1024,2,128]{2,1,0:T(2,128)(2,1)}), bf16[1024,2,128]{2,1,0:T(2,128)(2,1)S(1)}, u32[]{:S(2)}, u32[]{:S(2)}) async-start(bf16[1024,2,128]{2,1,0:T(2,128)(2,1)} %copy.160), calls=%async_computation.4 | async-start | bytes 1048576 | tf_op jit(solution)/shard_map/all_to_all | solution.py:135

commit v6 on v5

--- a/solution.py
+++ b/solution.py
@@ -77,7 +77,6 @@
     grad_rows = output_gradient.shape[0]
     grad_g = output_gradient.reshape(grad_rows, head_size, ring, heads_here, depth)
     grad_g = grad_g.transpose(2, 1, 3, 0, 4).reshape(ring * head_size, heads_here, grad_rows, depth)
-    grad_g = lax.all_to_all(grad_g, ("sl", "head"), split_axis=0, concat_axis=2, tiled=True)[0]
     logsum = row_log_total.reshape(ring, heads_here, local_tokens).transpose(0, 2, 1)
     side = jnp.concatenate(
         [
@@ -99,6 +98,8 @@
     )
     kv_packed = lax.all_to_all(kv_packed, "sl", split_axis=0, concat_axis=2, tiled=True)[0]
     far = shifted(kv_packed[:2], "sh", 1)
+    grad_g, kv_packed = lax.optimization_barrier((grad_g, kv_packed))
+    grad_g = lax.all_to_all(grad_g, ("sl", "head"), split_axis=0, concat_axis=2, tiled=True)[0]
     key_own = kv_packed[0]
     value_own = kv_packed[1]
     side_g = kv_packed[2]

time: 127 us -> 124 us (0.976)
  waiting for transfers between devices: 51.1 us -> 42 us
  starting transfers between devices: 30.8 us -> 34.4 us
  local copies, waits for them, and re-layouts: 15.6 us -> 17.5 us
  other arithmetic: 9.15 us -> 11 us
    ppermute x2, starting transfers between devices: 7.85 us -> 15.4 us  [shifted(): return lax.ppermute(value, axis, pairs)]
    ppermute x2, waiting for transfers between devices: 10.1 us -> 3.67 us  [shifted(): return lax.ppermute(value, axis, pairs)]
    all_to_all x2, waiting for transfers between devices: 17.8 us -> 14.1 us  [to_tokens(): lax.all_to_all(x, ('sl', 'head'), split_axis=0, concat_axis=1, tiled=True)]
    all_to_all x2, starting transfers between devices: 10.8 us -> 7.15 us  [to_tokens(): lax.all_to_all(x, ('sl', 'head'), split_axis=0, concat_axis=1, tiled=True)]
    all_to_all x1, waiting for transfers between devices: 4.25 us -> 6.62 us  [on_device(): lax.all_to_all(qf_packed, 'sl', split_axis=0, concat_axis=2, tiled=True)[0]]
    all_to_all x1, starting transfers between devices: 5.21 us -> 3.75 us  [on_device(): lax.all_to_all(grad_g, ('sl', 'head'), split_axis=0, concat_axis=2, tiled...]
    squeeze x0 -> x2, local copies, waits for them, and re-layouts: none -> 1.4 us  [the longest x1 0.84 us: on_device(): value_own = kv_packed[1]]
    unnamed x34 -> x21, local copies, waits for them, and re-layouts: 4.58 us -> 5.28 us
  transfers between devices with their start and end apart: 7 -> 7, of which waited for: 6 -> 6; matrix products, arithmetic and copies ran while one was open for 15% -> 13% of each run, Pallas kernels for 0% -> 0%
where the time goes in v6:
time: 124 us; the launch traced here: 123 us
  waiting for transfers between devices  42 us (34%)
  starting transfers between devices  34.4 us (28%)
  local copies, waits for them, and re-layouts  17.5 us (14%)
  matrix products  17.4 us (14%)
  other arithmetic  11 us (9%)
    ppermute x2, starting transfers between devices, shifted(): return lax.ppermute(value, axis, pairs)  15.4 us
    all_to_all x2, waiting for transfers between devices, to_tokens(): lax.all_to_all(x, ('sl', 'head'), split_axis=0, concat_axis=1, tiled=True)  14.1 us
    all_to_all x1, waiting for transfers between devices, on_device(): lax.all_to_all(kv_packed, 'sl', split_axis=0, concat_axis=2, tiled=True)[0]  9.81 us
    all_to_all x1, waiting for transfers between devices, on_device(): lax.all_to_all(grad_g, ('sl', 'head'), split_axis=0, concat_axis=2, tiled...  7.84 us
    all_to_all x2, starting transfers between devices, to_tokens(): lax.all_to_all(x, ('sl', 'head'), split_axis=0, concat_axis=1, tiled=True)  7.15 us
    all_to_all x1, waiting for transfers between devices, on_device(): lax.all_to_all(qf_packed, 'sl', split_axis=0, concat_axis=2, tiled=True)[0]  6.62 us
    dot_general x1, matrix products, band_terms(): jnp.einsum('tgij,gtid->tjd', low_probs, grad_t, preferred_element_type=jn...  6.09 us
    dot_general x1, matrix products, band_terms(): jnp.einsum('gtid,tjd->tgij', grad_t, value_w, preferred_element_type=jnp....  5.99 us
  transfers between devices with their start and end apart: 7, of which 6 were waited for; matrix products, arithmetic and copies ran while one was open for 13% of the time, Pallas kernels for 0%

profile of v6, /device:TPU:4, one launch (start us, length us, event | category | flops | bytes accessed | tf_op | source)
XLA Modules:
  0.0 123.4 jit_solution(17974167256727717836)
XLA Ops:
  0.6 0.7 reduce-precision_convert_fusion.3
  1.3 0.7 reshape.366
  2.1 1.2 copy.127
  3.3 1.2 copy.126
  4.5 0.0 copy-start.4
  4.6 0.1 fusion.54
  4.6 0.7 pad_maximum_fusion.1
  5.3 0.0 copy-start.5
  5.3 1.0 copy.131
  6.3 4.6 %all-to-all-start = ((bf16[4,3,256,128]{2,3,1,0:T(8,128)(2,1)}), bf16[4,3,256,128]{2,3,1,0:T(8,128)(2,1)S(1)}, u32[]{:S(2)}, u32[]{:S(2)}) async-start(bf16[4,3,256,128]{2,3,1,0:T(8,128)(2,1)} %copy.131), calls=%async_computation | async-start | bytes 1572864 | tf_op jit(solution)/shard_map/all_to_all | solution.py:99
  10.9 0.1 iota_add_fusion.1
  11.0 0.2 copy.133
  11.2 0.8 copy.134
  12.1 0.1 copy.137
  12.2 0.1 copy.136
  12.2 1.1 pad_maximum_fusion
  13.3 0.1 iota_add_fusion
  13.4 9.8 %all-to-all-done = bf16[4,3,256,128]{2,3,1,0:T(8,128)(2,1)S(1)} async-done(((bf16[4,3,256,128]{2,3,1,0:T(8,128)(2,1)}), bf16[4,3,256,128]{2,3,1,0:T(8,128)(2,1)S(1)}, u32[]{:S(2)}, u32[]{:S(2)}) %all-to-all-start) | async-done | bytes 786464 | tf_op jit(solution)/shard_map/all_to_all | solution.py:99
  23.2 3.5 %all-to-all-start.1 = ((bf16[4,4,256,128]{3,2,1,0:T(8,128)(2,1)}), bf16[4,4,256,128]{3,2,1,0:T(8,128)(2,1)S(1)}, u32[]{:S(2)}, u32[]{:S(2)}) async-start(bf16[4,4,256,128]{3,2,1,0:T(8,128)(2,1)} %pad_maximum_fusion), calls=%async_computation.1 | async-start | bytes 2097152 | tf_op jit(solution)/shard_map/all_to_all | solution.py:118
  26.8 0.6 copy.135
  27.4 0.4 copy.132
  27.8 1.2 slice.278
  29.0 3.8 %collective-permute-start = (bf16[2,1024,128]{1,2,0:T(8,128)(2,1)}, bf16[2,1024,128]{1,2,0:T(8,128)(2,1)}, u32[]{:S(2)}, u32[]{:S(2)}) collective-permute-start(bf16[2,1024,128]{1,2,0:T(8,128)(2,1)} %slice.278), channel_id=1, source_target_pairs={{0,4},{4,8},{8,12},{12,16},{16,20},{20,24},{24,28},{28,32},{32,36}... | collective-permute-start | bytes 1572872 | tf_op jit(solution)/shard_map/ppermute | solution.py:16
  32.8 0.6 squeeze.15
  33.4 0.8 slice_bitcast_fusion.15
  34.3 6.6 %all-to-all-done.1 = bf16[4,4,256,128]{3,2,1,0:T(8,128)(2,1)S(1)} async-done(((bf16[4,4,256,128]{3,2,1,0:T(8,128)(2,1)}), bf16[4,4,256,128]{3,2,1,0:T(8,128)(2,1)S(1)}, u32[]{:S(2)}, u32[]{:S(2)}) %all-to-all-start.1) | async-done | bytes 1048608 | tf_op jit(solution)/shard_map/all_to_all | solution.py:118
  41.0 3.8 %all-to-all-start.2 = ((bf16[16,2,64,128]{3,2,1,0:T(8,128)(2,1)}), bf16[16,2,64,128]{3,2,1,0:T(8,128)(2,1)S(1)}, u32[]{:S(2)}, u32[]{:S(2)}) async-start(bf16[16,2,64,128]{3,2,1,0:T(8,128)(2,1)} %bitcast.17), calls=%async_computation.2 | async-start | bytes 1048576 | tf_op jit(solution)/shard_map/all_to_all | solution.py:102
  44.7 2.7 %fusion.7 = pred[4,256,1280]{2,1,0:T(8,128)(4,1)} fusion(s32[4,256]{1,0:T(4,128)S(1)} %convert_element_type.72, s32[4,1280]{1,0:T(4,128)S(1)} %iota_add_fusion, s32[4,256]{1,0:T(4,128)S(1)} %iota_add_fusion.1), kind=kLoop, calls=%fused_computation.10 | loop fusion | flops 7864320 | bytes 1339392 | tf_op jit(solution)/shard_map/and | solution.py:34
  47.5 0.0 copy-start.3
  47.5 7.8 %all-to-all-done.2 = bf16[16,2,64,128]{3,2,1,0:T(8,128)(2,1)S(1)} async-done(((bf16[16,2,64,128]{3,2,1,0:T(8,128)(2,1)}), bf16[16,2,64,128]{3,2,1,0:T(8,128)(2,1)S(1)}, u32[]{:S(2)}, u32[]{:S(2)}) %all-to-all-start.2) | async-done | bytes 524320 | tf_op jit(solution)/shard_map/all_to_all | solution.py:102
  55.4 0.4 fusion.20
  55.7 1.1 slice_bitcast_fusion.13
  56.8 1.2 %fusion.48 = (bf16[1,1280,128]{1,2,0:T(8,128)(2,1)S(1)}, bf16[1,1280,128]{1,2,0:T(8,128)(2,1)S(1)}, bf16[1,1280,128]{1,2,0:T(8,128)(2,1)S(1)}, bf16[1,1280,128]{1,2,0:T(8,128)(2,1)S(1)}) fusion(bf16[1024,128]{0,1:T(8,128)(2,1)S(1)} %get-tuple-element.127, bf16[1024,128]{0,1:T(8,128)(2,1)} %get-tuple-element.117), kind=kLoop, calls=%fused_computation.85 | loop fusion | flops 2621440 | bytes 1835008 | tf_op jit(solution)/shard_map/stack | solution.py:28
  58.1 1.2 fusion.42
  59.2 1.5 %fusion.31 = f32[4,2,256,1280]{3,2,1,0:T(8,128)S(1)} fusion(bf16[1,1280,128]{1,2,0:T(8,128)(2,1)S(1)} %get-tuple-element.130, bf16[1,1280,128]{1,2,0:T(8,128)(2,1)S(1)} %get-tuple-element.131, bf16[1,1280,128]{1,2,0:T(8,128)(2,1)S(1)} %get-tuple-element.129, bf16[1,1280,128]{1,2,0:T(8,128)(2,1)S(1)} %get-tuple-element.128, ...), kind=kOutput, calls=%fused_computation.59 | convolution fusion | flops 673054720 | bytes 12320768 | tf_op jit(solution)/shard_map/gtid,tjd->tgij/dot_general | solution.py:36
  60.8 6.1 %fusion.9 = f32[4,1280,128]{2,1,0:T(8,128)} fusion(f32[4,2,256,1280]{3,2,1,0:T(8,128)S(1)} %fusion.31, f32[4,2,256]{2,1,0:T(2,128)S(1)} %bitcast.221, pred[4,256,1280]{2,1,0:T(8,128)(4,1)} %fusion.7, bf16[2,4,256,128]{3,2,1,0:T(8,128)(2,1)S(1)} %bitcast.203), kind=kOutput, calls=%fused_computation.12 | convolution fusion | flops 681574400 | bytes 14950400 | tf_op jit(solution)/shard_map/tgij,gtid->tjd/dot_general | solution.py:45
  66.9 6.0 %multiply_convert_fusion = bf16[4,2,256,1280]{3,2,1,0:T(8,128)(2,1)S(1)} fusion(f32[4,2,256,1280]{3,2,1,0:T(8,128)S(1)} %fusion.31, f32[4,2,256]{2,1,0:T(2,128)S(1)} %bitcast.220, f32[4,2,256]{2,1,0:T(2,128)S(1)} %bitcast.222, pred[4,256,1280]{2,1,0:T(8,128)(4,1)} %fusion.7, bf16[1,1280,128]{1,2,0:T(8,128)(2,1)} %get-tuple-element.124, ...), kind=kOutput, calls=%fused_computation | convolution fusion | flops 688783360 | bytes 18890752 | tf_op jit(solution)/shard_map/gtid,tjd->tgij/dot_general | solution.py:40
  72.9 1.9 %convolution_bitcast_fusion = f32[4,1280,128]{2,1,0:T(8,128)S(1)} fusion(bf16[4,2,256,1280]{3,2,1,0:T(8,128)(2,1)S(1)} %multiply_convert_fusion, bf16[1,4,4,256,128]{4,3,1,2,0:T(8,128)(2,1)S(1)} %bitcast.199), kind=kOutput, calls=%fused_computation.13 | convolution fusion | flops 671088640 | bytes 8388608 | tf_op jit(solution)/shard_map/tgij,gtid->tjd/dot_general | solution.py:44
  74.9 0.1 scatter-add.26
  74.9 0.1 fusion.30
  75.1 0.1 fusion.28
  75.2 0.1 fusion.26
  75.3 1.3 %copy-done = f32[4,1280,128]{2,1,0:T(8,128)S(1)} copy-done((f32[4,1280,128]{2,1,0:T(8,128)S(1)}, f32[4,1280,128]{2,1,0:T(8,128)}, u32[]{:S(2)}) %copy-start) | copy-done | bytes 2621464
  76.7 0.1 scatter-add.34
  76.8 0.1 fusion.25
  77.0 0.1 fusion.23
  77.1 0.1 fusion.21
  77.4 0.9 pad_maximum_fusion.2
  78.2 11.6 %collective-permute-start.1 = (bf16[2,1024,128]{2,1,0:T(8,128)(2,1)}, bf16[2,1024,128]{2,1,0:T(8,128)(2,1)}, u32[]{:S(2)}, u32[]{:S(2)}) collective-permute-start(bf16[2,1024,128]{2,1,0:T(8,128)(2,1)} %pad_maximum_fusion.2), channel_id=1, source_target_pairs={{4,0},{8,4},{12,8},{16,12},{20,16},{24,20},{28,24},{32,28},{36,32}... | collective-permute-start | bytes 1572872 | tf_op jit(solution)/shard_map/ppermute | solution.py:16
  89.8 1.8 %fusion.19 = bf16[4,256,2,128]{1,3,2,0:T(8,128)(2,1)S(1)} fusion(bf16[4,2,256,1280]{3,2,1,0:T(8,128)(2,1)S(1)} %multiply_convert_fusion, bf16[1,1280,128]{1,2,0:T(8,128)(2,1)S(1)} %get-tuple-element.130, bf16[1,1280,128]{1,2,0:T(8,128)(2,1)S(1)} %copy-done.2, bf16[1,1280,128]{1,2,0:T(8,128)(2,1)S(1)} %get-tuple-element.129, ...), kind=kOutput, calls=%fused_computation.24 | convolution fusion | flops 676855808 | bytes 7077888 | tf_op jit(solution)/shard_map/tgij,tjd->tigd/dot_general | solution.py:43
  91.6 0.3 copy.145
  91.9 1.3 %copy.146 = bf16[1024,2,128]{2,1,0:T(2,128)(2,1)} copy(bf16[1024,2,128]{2,0,1:T(8,128)(2,1)S(1)} %bitcast.209) | data formatting | bytes 1048576 | tf_op jit(solution)/shard_map/convert_element_type | solution.py:140
  93.2 3.6 %all-to-all-start.3 = ((bf16[1024,2,128]{2,1,0:T(2,128)(2,1)}), bf16[1024,2,128]{2,1,0:T(2,128)(2,1)S(1)}, u32[]{:S(2)}, u32[]{:S(2)}) async-start(bf16[1024,2,128]{2,1,0:T(2,128)(2,1)} %copy.146), calls=%async_computation.3 | async-start | bytes 1048576 | tf_op jit(solution)/shard_map/all_to_all | solution.py:136
  96.8 3.7 %collective-permute-done.1 = bf16[2,1024,128]{2,1,0:T(8,128)(2,1)} collective-permute-done((bf16[2,1024,128]{2,1,0:T(8,128)(2,1)}, bf16[2,1024,128]{2,1,0:T(8,128)(2,1)}, u32[]{:S(2)}, u32[]{:S(2)}) %collective-permute-start.1) | collective-permute-done | bytes 524320 | tf_op jit(solution)/shard_map/ppermute | solution.py:16
  100.5 1.2 fusion.55
  101.7 0.1 pad_maximum_fusion.3
  101.7 1.3 %copy.153 = bf16[1024,2,128]{2,1,0:T(2,128)(2,1)} copy(bf16[1024,2,128]{2,0,1:T(8,128)(2,1)S(1)} %pad_maximum_fusion.3) | data formatting | bytes 1048576 | tf_op jit(solution)/shard_map/stack | solution.py:146
  103.1 4.6 %all-to-all-done.3 = bf16[1024,2,128]{2,1,0:T(2,128)(2,1)S(1)} async-done(((bf16[1024,2,128]{2,1,0:T(2,128)(2,1)}), bf16[1024,2,128]{2,1,0:T(2,128)(2,1)S(1)}, u32[]{:S(2)}, u32[]{:S(2)}) %all-to-all-start.3) | async-done | bytes 524320 | tf_op jit(solution)/shard_map/all_to_all | solution.py:136
  107.6 3.6 %all-to-all-start.4 = ((bf16[1024,2,128]{2,1,0:T(2,128)(2,1)}), bf16[1024,2,128]{2,1,0:T(2,128)(2,1)S(1)}, u32[]{:S(2)}, u32[]{:S(2)}) async-start(bf16[1024,2,128]{2,1,0:T(2,128)(2,1)} %copy.153), calls=%async_computation.4 | async-start | bytes 1048576 | tf_op jit(solution)/shard_map/all_to_all | solution.py:136
  111.2 0.1 copy.147
  111.3 1.1 copy.155
  112.5 9.5 %all-to-all-done.4 = bf16[1024,2,128]{2,1,0:T(2,128)(2,1)S(1)} async-done(((bf16[1024,2,128]{2,1,0:T(2,128)(2,1)}), bf16[1024,2,128]{2,1,0:T(2,128)(2,1)S(1)}, u32[]{:S(2)}, u32[]{:S(2)}) %all-to-all-start.4) | async-done | bytes 524320 | tf_op jit(solution)/shard_map/all_to_all | solution.py:136
  122.0 0.4 copy.191
  122.4 1.0 fusion.70
  (37 shorter events, 0.6 us)
Async XLA Ops:
  4.5 6.5 %copy-start.4 = (bf16[64,32,128]{2,1,0:T(8,128)(2,1)S(1)}, bf16[64,32,128]{2,1,0:T(8,128)(2,1)}, u32[]{:S(2)}) copy-start(bf16[64,32,128]{2,1,0:T(8,128)(2,1)} %param.27) | copy-start | bytes 1572868
  5.3 6.8 %copy-start.5 = (bf16[256,8,128]{2,1,0:T(8,128)(2,1)S(1)}, bf16[256,8,128]{2,1,0:T(8,128)(2,1)}, u32[]{:S(2)}) copy-start(bf16[256,8,128]{2,1,0:T(8,128)(2,1)} %param.26) | copy-start | bytes 1572868
  6.3 5.8 %copy-start.6 = (bf16[256,8,128]{2,1,0:T(8,128)(2,1)S(1)}, bf16[256,8,128]{2,1,0:T(8,128)(2,1)}, u32[]{:S(2)}) copy-start(bf16[256,8,128]{2,1,0:T(8,128)(2,1)} %param.23) | copy-start | bytes 1572868
  6.3 16.9 %all-to-all-start = ((bf16[4,3,256,128]{2,3,1,0:T(8,128)(2,1)}), bf16[4,3,256,128]{2,3,1,0:T(8,128)(2,1)S(1)}, u32[]{:S(2)}, u32[]{:S(2)}) async-start(bf16[4,3,256,128]{2,3,1,0:T(8,128)(2,1)} %copy.131), calls=%async_computation | async-start | bytes 1572864 | tf_op jit(solution)/shard_map/all_to_all | solution.py:99
  23.2 17.7 %all-to-all-start.1 = ((bf16[4,4,256,128]{3,2,1,0:T(8,128)(2,1)}), bf16[4,4,256,128]{3,2,1,0:T(8,128)(2,1)S(1)}, u32[]{:S(2)}, u32[]{:S(2)}) async-start(bf16[4,4,256,128]{3,2,1,0:T(8,128)(2,1)} %pad_maximum_fusion), calls=%async_computation.1 | async-start | bytes 2097152 | tf_op jit(solution)/shard_map/all_to_all | solution.py:118
  29.0 26.7 %collective-permute-start = (bf16[2,1024,128]{1,2,0:T(8,128)(2,1)}, bf16[2,1024,128]{1,2,0:T(8,128)(2,1)}, u32[]{:S(2)}, u32[]{:S(2)}) collective-permute-start(bf16[2,1024,128]{1,2,0:T(8,128)(2,1)} %slice.278), channel_id=1, source_target_pairs={{0,4},{4,8},{8,12},{12,16},{16,20},{20,24},{24,28},{28,32},{32,36}... | collective-permute-start | bytes 1572872 | tf_op jit(solution)/shard_map/ppermute | solution.py:16
  41.0 14.4 %all-to-all-start.2 = ((bf16[16,2,64,128]{3,2,1,0:T(8,128)(2,1)}), bf16[16,2,64,128]{3,2,1,0:T(8,128)(2,1)S(1)}, u32[]{:S(2)}, u32[]{:S(2)}) async-start(bf16[16,2,64,128]{3,2,1,0:T(8,128)(2,1)} %bitcast.17), calls=%async_computation.2 | async-start | bytes 1048576 | tf_op jit(solution)/shard_map/all_to_all | solution.py:102
  47.5 10.6 %copy-start.3 = (bf16[1024,128]{0,1:T(8,128)(2,1)S(1)}, bf16[1024,128]{0,1:T(8,128)(2,1)}, u32[]{:S(2)}) copy-start(bf16[1024,128]{0,1:T(8,128)(2,1)} %get-tuple-element.115) | copy-start | bytes 786436
  58.1 2.7 %copy-start.1 = (bf16[1,1280,128]{1,2,0:T(8,128)(2,1)}, bf16[1,1280,128]{1,2,0:T(8,128)(2,1)S(1)}, u32[]{:S(2)}) copy-start(bf16[1,1280,128]{1,2,0:T(8,128)(2,1)S(1)} %get-tuple-element.131) | copy-start | bytes 983044
  74.9 1.7 %copy-start = (f32[4,1280,128]{2,1,0:T(8,128)S(1)}, f32[4,1280,128]{2,1,0:T(8,128)}, u32[]{:S(2)}) copy-start(f32[4,1280,128]{2,1,0:T(8,128)} %fusion.9) | copy-start | bytes 7864324
  77.2 12.6 %copy-start.2 = (bf16[1,1280,128]{1,2,0:T(8,128)(2,1)S(1)}, bf16[1,1280,128]{1,2,0:T(8,128)(2,1)}, u32[]{:S(2)}) copy-start(bf16[1,1280,128]{1,2,0:T(8,128)(2,1)} %copy-done.1) | copy-start | bytes 983044
  78.2 22.3 %collective-permute-start.1 = (bf16[2,1024,128]{2,1,0:T(8,128)(2,1)}, bf16[2,1024,128]{2,1,0:T(8,128)(2,1)}, u32[]{:S(2)}, u32[]{:S(2)}) collective-permute-start(bf16[2,1024,128]{2,1,0:T(8,128)(2,1)} %pad_maximum_fusion.2), channel_id=1, source_target_pairs={{4,0},{8,4},{12,8},{16,12},{20,16},{24,20},{28,24},{32,28},{36,32}... | collective-permute-start | bytes 1572872 | tf_op jit(solution)/shard_map/ppermute | solution.py:16
  93.2 14.4 %all-to-all-start.3 = ((bf16[1024,2,128]{2,1,0:T(2,128)(2,1)}), bf16[1024,2,128]{2,1,0:T(2,128)(2,1)S(1)}, u32[]{:S(2)}, u32[]{:S(2)}) async-start(bf16[1024,2,128]{2,1,0:T(2,128)(2,1)} %copy.146), calls=%async_computation.3 | async-start | bytes 1048576 | tf_op jit(solution)/shard_map/all_to_all | solution.py:136
  107.6 14.4 %all-to-all-start.4 = ((bf16[1024,2,128]{2,1,0:T(2,128)(2,1)}), bf16[1024,2,128]{2,1,0:T(2,128)(2,1)S(1)}, u32[]{:S(2)}, u32[]{:S(2)}) async-start(bf16[1024,2,128]{2,1,0:T(2,128)(2,1)} %copy.153), calls=%async_computation.4 | async-start | bytes 1048576 | tf_op jit(solution)/shard_map/all_to_all | solution.py:136

commit v7 on v6

--- a/solution.py
+++ b/solution.py
@@ -1,6 +1,7 @@
 import jax
 import jax.numpy as jnp
 from jax import lax
+from jax.experimental import pallas as pl
 from jax.sharding import Mesh
 from jax.sharding import PartitionSpec as P
 
@@ -50,6 +51,69 @@
         key_term = key_term.at[t * BLOCK : t * BLOCK + span].add(key_w_term[t])
         value_term = value_term.at[t * BLOCK : t * BLOCK + span].add(value_w_term[t])
     return query_term.reshape(tokens, group, depth), key_term, value_term
+
+
+def band_kernel(q_ref, g_ref, lse_ref, dl_ref, ps_ref, k_ref, v_ref, dq_ref, dk_ref, dv_ref):
+    heads, tokens, depth = q_ref.shape
+    tiles = tokens // BLOCK
+    reach = WINDOW_LENGTH // BLOCK + 1
+    dk_ref[...] = jnp.zeros(dk_ref.shape, jnp.float32)
+    dv_ref[...] = jnp.zeros(dv_ref.shape, jnp.float32)
+    last = (((0,), (0,)), ((), ()))
+    cross = (((1,), (1,)), ((), ()))
+    row = lax.broadcasted_iota(jnp.int32, (BLOCK, BLOCK), 0)
+    col = lax.broadcasted_iota(jnp.int32, (BLOCK, BLOCK), 1)
+
+    def one_tile(t, carry):
+        first = pl.multiple_of(t * BLOCK, BLOCK)
+        starts = ps_ref[pl.ds(first, BLOCK), :]
+        for h in range(heads):
+            query = q_ref[h, pl.ds(first, BLOCK), :]
+            grad = g_ref[h, pl.ds(first, BLOCK), :]
+            logsum = lse_ref[h, pl.ds(first, BLOCK), :]
+            delta = dl_ref[h, pl.ds(first, BLOCK), :]
+            query_acc = jnp.zeros((BLOCK, depth), jnp.float32)
+            for b in range(reach):
+                key_first = pl.multiple_of((t + b) * BLOCK, BLOCK)
+                key = k_ref[pl.ds(key_first, BLOCK), :]
+                value = v_ref[pl.ds(key_first, BLOCK), :]
+                scores = (
+                    lax.dot_general(query, key, cross, preferred_element_type=jnp.float32)
+                    * score_scale
+                )
+                gap = row - col + (WINDOW_LENGTH - b * BLOCK)
+                visible = (gap >= 0) & (gap < WINDOW_LENGTH) & (col + key_first >= starts)
+                probs = jnp.where(visible, jnp.exp(scores - logsum), 0.0)
+                dprobs = lax.dot_general(grad, value, cross, preferred_element_type=jnp.float32)
+                low_scores = (probs * (dprobs - delta)).astype(jnp.bfloat16)
+                query_acc = query_acc + jnp.dot(
+                    low_scores, key, preferred_element_type=jnp.float32
+                )
+                dk_ref[pl.ds(key_first, BLOCK), :] += lax.dot_general(
+                    low_scores, query, last, preferred_element_type=jnp.float32
+                )
+                dv_ref[pl.ds(key_first, BLOCK), :] += lax.dot_general(
+                    probs.astype(jnp.bfloat16), grad, last, preferred_element_type=jnp.float32
+                )
+            dq_ref[h, pl.ds(first, BLOCK), :] = query_acc
+        return carry
+
+    lax.fori_loop(0, tiles, one_tile, 0)
+
+
+def band_pallas(query, grad, logsum, delta, start, base, keys, values):
+    group, tokens, depth = query.shape
+    total = keys.shape[0]
+    start_rel = (start - base + WINDOW_LENGTH)[:, None]
+    dq, dk, dv = pl.pallas_call(
+        band_kernel,
+        out_shape=(
+            jax.ShapeDtypeStruct((group, tokens, depth), jnp.float32),
+            jax.ShapeDtypeStruct((total, depth), jnp.float32),
+            jax.ShapeDtypeStruct((total, depth), jnp.float32),
+        ),
+    )(query, grad, logsum[..., None], delta[..., None], start_rel, keys, values)
+    return dq.transpose(1, 0, 2), dk, dv
 
 
 def split_three(x):
@@ -122,7 +186,7 @@
     base = lax.axis_index("sh") * tokens
     keys = jnp.concatenate([far[0], key_own], axis=0)
     values = jnp.concatenate([far[1], value_own], axis=0)
-    query_sum, key_sum, value_sum = band_terms(
+    query_sum, key_sum, value_sum = band_pallas(
         query_g, grad_g, logsum_g, delta_g, start_g, base, keys, values
     )
     back = shifted(

time: 124 us -> 122 us (0.984)
  Pallas kernels: 0 us -> 17.9 us
  matrix products: 17.4 us -> 0 us
  other arithmetic: 11 us -> 6.66 us
  local copies, waits for them, and re-layouts: 17.5 us -> 19 us
    pallas_call x0 -> x1, Pallas kernels: none -> 17.9 us  [band_pallas(): pl.pallas_call(band_kernel, out_shape=(jax.ShapeDtypeStruct((group, token...]
    dot_general x5 -> x0, matrix products: 17.4 us -> none  [the longest x1 6.09 us: band_terms(): jnp.einsum('tgij,gtid->tjd', low_probs, grad_t, preferred_element_type=jn...]
    broadcast_in_dim x0 -> x2, local copies, waits for them, and re-layouts: none -> 2.71 us  [the longest x1 1.39 us: band_pallas(): logsum[..., None]]
    and x1 -> x0, other arithmetic: 2.68 us -> none  [band_terms(): (gap >= 0) & (gap < WINDOW_LENGTH)]
    another operation x3 -> x1, other arithmetic: 3.09 us -> 0.69 us  [the longest x1 1.25 us: band_terms(): key_w = jnp.stack([keys[t * BLOCK:t * BLOCK + span] for t in range(tiles)])]
    unnamed x21 -> x23, local copies, waits for them, and re-layouts: 5.28 us -> 3.05 us
    another operation x2, local copies, waits for them, and re-layouts: 0.06 us -> 2.23 us  [on_device(): jnp.stack([key_sum[:WINDOW_LENGTH], value_sum[:WINDOW_LENGTH]])]
    ppermute x2, waiting for transfers between devices: 3.67 us -> 5.56 us  [shifted(): return lax.ppermute(value, axis, pairs)]
  transfers between devices with their start and end apart: 7 -> 7, of which waited for: 6 -> 6; matrix products, arithmetic and copies ran while one was open for 13% -> 12% of each run, Pallas kernels for 0% -> 0%
where the time goes in v7:
time: 122 us; the launch traced here: 121 us
  waiting for transfers between devices  42.6 us (35%)
  starting transfers between devices  34 us (28%)
  local copies, waits for them, and re-layouts  19 us (16%)
  Pallas kernels  17.9 us (15%)
  other arithmetic  6.66 us (5%)
    pallas_call x1, Pallas kernels, band_pallas(): pl.pallas_call(band_kernel, out_shape=(jax.ShapeDtypeStruct((group, token...  17.9 us
    ppermute x2, starting transfers between devices, shifted(): return lax.ppermute(value, axis, pairs)  15.2 us
    all_to_all x2, waiting for transfers between devices, to_tokens(): lax.all_to_all(x, ('sl', 'head'), split_axis=0, concat_axis=1, tiled=True)  12.3 us
    all_to_all x1, waiting for transfers between devices, on_device(): lax.all_to_all(kv_packed, 'sl', split_axis=0, concat_axis=2, tiled=True)[0]  10.1 us
    all_to_all x1, waiting for transfers between devices, on_device(): lax.all_to_all(grad_g, ('sl', 'head'), split_axis=0, concat_axis=2, tiled...  8.13 us
    all_to_all x2, starting transfers between devices, to_tokens(): lax.all_to_all(x, ('sl', 'head'), split_axis=0, concat_axis=1, tiled=True)  7.15 us
    all_to_all x1, waiting for transfers between devices, on_device(): lax.all_to_all(qf_packed, 'sl', split_axis=0, concat_axis=2, tiled=True)[0]  6.58 us
    ppermute x2, waiting for transfers between devices, shifted(): return lax.ppermute(value, axis, pairs)  5.56 us
  transfers between devices with their start and end apart: 7, of which 6 were waited for; matrix products, arithmetic and copies ran while one was open for 12% of the time, Pallas kernels for 0%

profile of v7, /device:TPU:4, one launch (start us, length us, event | category | flops | bytes accessed | tf_op | source)
XLA Modules:
  0.0 121.1 jit_solution(3124172722637026225)
XLA Ops:
  0.6 0.0 copy-start.8
  0.6 0.7 reduce-precision_convert_fusion.3
  1.4 0.0 copy-done.8
  1.4 0.0 copy-start.7
  1.4 1.3 %copy.80 = bf16[256,4,128]{0,1,2:T(4,128)(2,1)S(1)} copy(bf16[256,4,128]{2,1,0:T(4,128)(2,1)} %param.8) | data formatting | bytes 524288 | tf_op args[1]
  2.7 0.0 copy-done.7
  2.7 0.2 copy.81
  3.0 0.1 fusion.14
  3.0 0.7 pad_maximum_fusion.1
  3.7 1.0 copy.85
  4.7 0.0 copy-start.4
  4.7 4.6 %all-to-all-start.1 = ((bf16[4,3,256,128]{2,3,1,0:T(8,128)(2,1)}), bf16[4,3,256,128]{2,3,1,0:T(8,128)(2,1)S(1)}, u32[]{:S(2)}, u32[]{:S(2)}) async-start(bf16[4,3,256,128]{2,3,1,0:T(8,128)(2,1)} %copy.85), calls=%async_computation.1 | async-start | bytes 1572864 | tf_op jit(solution)/shard_map/all_to_all | solution.py:163
  9.3 0.0 copy-done.4
  9.3 0.1 copy.76
  9.4 1.0 copy-done.5
  10.3 0.1 copy.77
  10.4 1.1 pad_maximum_fusion
  11.5 10.1 %all-to-all-done.1 = bf16[4,3,256,128]{2,3,1,0:T(8,128)(2,1)S(1)} async-done(((bf16[4,3,256,128]{2,3,1,0:T(8,128)(2,1)}), bf16[4,3,256,128]{2,3,1,0:T(8,128)(2,1)S(1)}, u32[]{:S(2)}, u32[]{:S(2)}) %all-to-all-start.1) | async-done | bytes 786464 | tf_op jit(solution)/shard_map/all_to_all | solution.py:163
  21.6 3.5 %all-to-all-start = ((bf16[4,4,256,128]{3,2,1,0:T(8,128)(2,1)}), bf16[4,4,256,128]{3,2,1,0:T(8,128)(2,1)S(1)}, u32[]{:S(2)}, u32[]{:S(2)}) async-start(bf16[4,4,256,128]{3,2,1,0:T(8,128)(2,1)} %pad_maximum_fusion), calls=%async_computation | async-start | bytes 2097152 | tf_op jit(solution)/shard_map/all_to_all | solution.py:182
  25.1 0.0 copy-done.6
  25.1 1.0 copy.79
  26.2 0.4 copy.86
  26.5 1.0 copy.89
  27.6 3.8 %collective-permute-start = (bf16[2,1024,128]{2,1,0:T(8,128)(2,1)}, bf16[2,1024,128]{2,1,0:T(8,128)(2,1)}, u32[]{:S(2)}, u32[]{:S(2)}) collective-permute-start(bf16[2,1024,128]{2,1,0:T(8,128)(2,1)} %bitcast.35), channel_id=1, source_target_pairs={{0,4},{4,8},{8,12},{12,16},{16,20},{20,24},{24,28},{28,32},{32,36}... | collective-permute-start | bytes 1572872 | tf_op jit(solution)/shard_map/ppermute | solution.py:17
  31.4 0.1 slice_bitcast_fusion.4
  31.4 0.1 slice_convert_fusion.2
  31.6 1.1 fusion.5.ps_ref
  32.7 6.6 %all-to-all-done = bf16[4,4,256,128]{3,2,1,0:T(8,128)(2,1)S(1)} async-done(((bf16[4,4,256,128]{3,2,1,0:T(8,128)(2,1)}), bf16[4,4,256,128]{3,2,1,0:T(8,128)(2,1)S(1)}, u32[]{:S(2)}, u32[]{:S(2)}) %all-to-all-start) | async-done | bytes 1048608 | tf_op jit(solution)/shard_map/all_to_all | solution.py:182
  39.3 3.6 %all-to-all-start.2 = ((bf16[16,2,64,128]{3,2,1,0:T(8,128)(2,1)}), bf16[16,2,64,128]{3,2,1,0:T(8,128)(2,1)S(1)}, u32[]{:S(2)}, u32[]{:S(2)}) async-start(bf16[16,2,64,128]{3,2,1,0:T(8,128)(2,1)} %bitcast.9), calls=%async_computation.2 | async-start | bytes 1048576 | tf_op jit(solution)/shard_map/all_to_all | solution.py:166
  42.9 0.2 copy.88
  43.2 1.4 %copy.90.lse_ref = f32[2,1024,1]{2,1,0:T(8,128)} copy(f32[2,1024,1]{1,0,2:T(2,128)S(1)} %bitcast.138) | data formatting | bytes 16384 | tf_op jit(solution)/shard_map/broadcast_in_dim | solution.py:115
  44.6 0.1 copy.117
  44.7 0.9 fusion.22
  45.6 8.1 %all-to-all-done.2 = bf16[16,2,64,128]{3,2,1,0:T(8,128)(2,1)S(1)} async-done(((bf16[16,2,64,128]{3,2,1,0:T(8,128)(2,1)}), bf16[16,2,64,128]{3,2,1,0:T(8,128)(2,1)S(1)}, u32[]{:S(2)}, u32[]{:S(2)}) %all-to-all-start.2) | async-done | bytes 524320 | tf_op jit(solution)/shard_map/all_to_all | solution.py:166
  53.7 0.0 copy-start
  53.7 0.4 fusion
  54.1 0.4 copy-done
  54.5 1.3 %copy.91.dl_ref = f32[2,1024,1]{2,1,0:T(8,128)} copy(f32[2,1024,1]{1,0,2:T(2,128)S(1)} %bitcast.137) | data formatting | bytes 16384 | tf_op jit(solution)/shard_map/broadcast_in_dim | solution.py:115
  55.8 0.0 collective-permute-done
  55.9 1.1 slice_bitcast_fusion.2
  56.9 1.0 pad_maximum_fusion.2
  58.0 17.9 %shard_map.94 = (f32[2,1024,128]{2,1,0:T(8,128)}, f32[2048,128]{1,0:T(8,128)}, f32[2048,128]{1,0:T(8,128)}) custom-call(bf16[2,1024,128]{2,1,0:T(8,128)(2,1)} %bitcast.122, bf16[2,1024,128]{2,1,0:T(8,128)(2,1)} %bitcast.119, f32[2,1024,1]{2,1,0:T(8,128)} %copy.90.lse_ref, f32[2,1024,1]{2,1,0:T(8,128)} %copy.91.dl_ref, s32[1024,1]{1,0:T(8,128)} %fusion.5.ps_ref, ...), custom_call_target="tpu_custom_call" | custom-call | tf_op jit(solution)/shard_map/pallas_call | solution.py:108
  75.8 1.2 fusion.15
  77.0 1.1 fusion.16
  78.1 0.1 pad_maximum_fusion.4
  78.1 11.3 %collective-permute-start.1 = (bf16[2,1024,128]{2,1,0:T(8,128)(2,1)S(1)}, bf16[2,1024,128]{2,1,0:T(8,128)(2,1)}, u32[]{:S(2)}, u32[]{:S(2)}) collective-permute-start(bf16[2,1024,128]{2,1,0:T(8,128)(2,1)S(1)} %pad_maximum_fusion.4), channel_id=1, source_target_pairs={{4,0},{8,4},{12,8},{16,12},{20,16},{24,20},{28,24},{32,28},{36,32}... | collective-permute-start | bytes 1572872 | tf_op jit(solution)/shard_map/ppermute | solution.py:17
  89.5 0.0 copy-done.1
  89.5 0.1 fusion.1
  89.6 0.0 copy-start.2
  89.6 0.0 copy-start.3
  89.6 1.3 %copy.92 = bf16[1024,2,128]{2,1,0:T(2,128)(2,1)} copy(bf16[1024,2,128]{2,0,1:T(8,128)(2,1)S(1)} %fusion.1) | data formatting | bytes 1048576 | tf_op jit(solution)/shard_map/convert_element_type | solution.py:204
  91.0 3.6 %all-to-all-start.3 = ((bf16[1024,2,128]{2,1,0:T(2,128)(2,1)}), bf16[1024,2,128]{2,1,0:T(2,128)(2,1)S(1)}, u32[]{:S(2)}, u32[]{:S(2)}) async-start(bf16[1024,2,128]{2,1,0:T(2,128)(2,1)} %copy.92), calls=%async_computation.3 | async-start | bytes 1048576 | tf_op jit(solution)/shard_map/all_to_all | solution.py:200
  94.5 5.6 %collective-permute-done.1 = bf16[2,1024,128]{2,1,0:T(8,128)(2,1)} collective-permute-done((bf16[2,1024,128]{2,1,0:T(8,128)(2,1)S(1)}, bf16[2,1024,128]{2,1,0:T(8,128)(2,1)}, u32[]{:S(2)}, u32[]{:S(2)}) %collective-permute-start.1) | collective-permute-done | bytes 524320 | tf_op jit(solution)/shard_map/ppermute | solution.py:17
  100.1 0.0 copy-done.2
  100.1 0.0 copy-done.3
  100.1 1.2 fusion.11
  101.3 0.1 pad_maximum_fusion.5
  101.3 1.4 %copy.94 = bf16[1024,2,128]{2,1,0:T(2,128)(2,1)} copy(bf16[1024,2,128]{2,0,1:T(8,128)(2,1)S(1)} %pad_maximum_fusion.5) | data formatting | bytes 1048576 | tf_op jit(solution)/shard_map/stack | solution.py:210
  102.7 2.7 %all-to-all-done.3 = bf16[1024,2,128]{2,1,0:T(2,128)(2,1)S(1)} async-done(((bf16[1024,2,128]{2,1,0:T(2,128)(2,1)}), bf16[1024,2,128]{2,1,0:T(2,128)(2,1)S(1)}, u32[]{:S(2)}, u32[]{:S(2)}) %all-to-all-start.3) | async-done | bytes 524320 | tf_op jit(solution)/shard_map/all_to_all | solution.py:200
  105.3 3.6 %all-to-all-start.4 = ((bf16[1024,2,128]{2,1,0:T(2,128)(2,1)}), bf16[1024,2,128]{2,1,0:T(2,128)(2,1)S(1)}, u32[]{:S(2)}, u32[]{:S(2)}) async-start(bf16[1024,2,128]{2,1,0:T(2,128)(2,1)} %copy.94), calls=%async_computation.4 | async-start | bytes 1048576 | tf_op jit(solution)/shard_map/all_to_all | solution.py:200
  108.9 1.2 copy.93
  110.1 9.6 %all-to-all-done.4 = bf16[1024,2,128]{2,1,0:T(2,128)(2,1)S(1)} async-done(((bf16[1024,2,128]{2,1,0:T(2,128)(2,1)}), bf16[1024,2,128]{2,1,0:T(2,128)(2,1)S(1)}, u32[]{:S(2)}, u32[]{:S(2)}) %all-to-all-start.4) | async-done | bytes 524320 | tf_op jit(solution)/shard_map/all_to_all | solution.py:200
  119.7 0.4 copy.118
  120.1 1.0 fusion.23
  (17 shorter events, 0.2 us)
Async XLA Ops:
  0.6 0.7 copy-start.8
  1.4 1.3 %copy-start.7 = (bf16[256,4,128]{2,1,0:T(4,128)(2,1)S(1)}, bf16[256,4,128]{2,1,0:T(4,128)(2,1)}, u32[]{:S(2)}) copy-start(bf16[256,4,128]{2,1,0:T(4,128)(2,1)} %param.9) | copy-start | bytes 786436
  4.7 4.6 %copy-start.4 = (bf16[256,8,128]{2,1,0:T(8,128)(2,1)S(1)}, bf16[256,8,128]{2,1,0:T(8,128)(2,1)}, u32[]{:S(2)}) copy-start(bf16[256,8,128]{2,1,0:T(8,128)(2,1)} %param.7) | copy-start | bytes 1572868
  4.7 16.9 %all-to-all-start.1 = ((bf16[4,3,256,128]{2,3,1,0:T(8,128)(2,1)}), bf16[4,3,256,128]{2,3,1,0:T(8,128)(2,1)S(1)}, u32[]{:S(2)}, u32[]{:S(2)}) async-start(bf16[4,3,256,128]{2,3,1,0:T(8,128)(2,1)} %copy.85), calls=%async_computation.1 | async-start | bytes 1572864 | tf_op jit(solution)/shard_map/all_to_all | solution.py:163
  9.3 1.0 copy-start.5
  11.5 13.6 %copy-start.6 = (bf16[64,32,128]{2,1,0:T(8,128)(2,1)S(1)}, bf16[64,32,128]{2,1,0:T(8,128)(2,1)}, u32[]{:S(2)}) copy-start(bf16[64,32,128]{2,1,0:T(8,128)(2,1)} %param.11) | copy-start | bytes 1572868
  21.6 17.7 %all-to-all-start = ((bf16[4,4,256,128]{3,2,1,0:T(8,128)(2,1)}), bf16[4,4,256,128]{3,2,1,0:T(8,128)(2,1)S(1)}, u32[]{:S(2)}, u32[]{:S(2)}) async-start(bf16[4,4,256,128]{3,2,1,0:T(8,128)(2,1)} %pad_maximum_fusion), calls=%async_computation | async-start | bytes 2097152 | tf_op jit(solution)/shard_map/all_to_all | solution.py:182
  27.6 28.3 %collective-permute-start = (bf16[2,1024,128]{2,1,0:T(8,128)(2,1)}, bf16[2,1024,128]{2,1,0:T(8,128)(2,1)}, u32[]{:S(2)}, u32[]{:S(2)}) collective-permute-start(bf16[2,1024,128]{2,1,0:T(8,128)(2,1)} %bitcast.35), channel_id=1, source_target_pairs={{0,4},{4,8},{8,12},{12,16},{16,20},{20,24},{24,28},{28,32},{32,36}... | collective-permute-start | bytes 1572872 | tf_op jit(solution)/shard_map/ppermute | solution.py:17
  39.3 14.4 %all-to-all-start.2 = ((bf16[16,2,64,128]{3,2,1,0:T(8,128)(2,1)}), bf16[16,2,64,128]{3,2,1,0:T(8,128)(2,1)S(1)}, u32[]{:S(2)}, u32[]{:S(2)}) async-start(bf16[16,2,64,128]{3,2,1,0:T(8,128)(2,1)} %bitcast.9), calls=%async_computation.2 | async-start | bytes 1048576 | tf_op jit(solution)/shard_map/all_to_all | solution.py:166
  53.7 0.8 copy-start
  75.8 13.7 %copy-start.1 = (f32[2,1024,128]{2,1,0:T(8,128)S(1)}, f32[2,1024,128]{2,1,0:T(8,128)}, u32[]{:S(2)}) copy-start(f32[2,1024,128]{2,1,0:T(8,128)} %get-tuple-element.10) | copy-start | bytes 3145732
  78.1 22.0 %collective-permute-start.1 = (bf16[2,1024,128]{2,1,0:T(8,128)(2,1)S(1)}, bf16[2,1024,128]{2,1,0:T(8,128)(2,1)}, u32[]{:S(2)}, u32[]{:S(2)}) collective-permute-start(bf16[2,1024,128]{2,1,0:T(8,128)(2,1)S(1)} %pad_maximum_fusion.4), channel_id=1, source_target_pairs={{4,0},{8,4},{12,8},{16,12},{20,16},{24,20},{28,24},{32,28},{36,32}... | collective-permute-start | bytes 1572872 | tf_op jit(solution)/shard_map/ppermute | solution.py:17
  89.6 10.5 %copy-start.2 = (f32[2048,128]{1,0:T(8,128)S(1)}, f32[2048,128]{1,0:T(8,128)}, u32[]{:S(2)}) copy-start(f32[2048,128]{1,0:T(8,128)} %get-tuple-element.11) | copy-start | bytes 3145732
  89.6 10.5 %copy-start.3 = (f32[2048,128]{1,0:T(8,128)S(1)}, f32[2048,128]{1,0:T(8,128)}, u32[]{:S(2)}) copy-start(f32[2048,128]{1,0:T(8,128)} %get-tuple-element.12) | copy-start | bytes 3145732
  91.0 14.4 %all-to-all-start.3 = ((bf16[1024,2,128]{2,1,0:T(2,128)(2,1)}), bf16[1024,2,128]{2,1,0:T(2,128)(2,1)S(1)}, u32[]{:S(2)}, u32[]{:S(2)}) async-start(bf16[1024,2,128]{2,1,0:T(2,128)(2,1)} %copy.92), calls=%async_computation.3 | async-start | bytes 1048576 | tf_op jit(solution)/shard_map/all_to_all | solution.py:200
  105.3 14.4 %all-to-all-start.4 = ((bf16[1024,2,128]{2,1,0:T(2,128)(2,1)}), bf16[1024,2,128]{2,1,0:T(2,128)(2,1)S(1)}, u32[]{:S(2)}, u32[]{:S(2)}) async-start(bf16[1024,2,128]{2,1,0:T(2,128)(2,1)} %copy.94), calls=%async_computation.4 | async-start | bytes 1048576 | tf_op jit(solution)/shard_map/all_to_all | solution.py:200

commit v8 on v7

--- a/solution.py
+++ b/solution.py
@@ -1,3 +1,5 @@
+from functools import partial
+
 import jax
 import jax.numpy as jnp
 from jax import lax
@@ -53,67 +55,71 @@
     return query_term.reshape(tokens, group, depth), key_term, value_term
 
 
-def band_kernel(q_ref, g_ref, lse_ref, dl_ref, ps_ref, k_ref, v_ref, dq_ref, dk_ref, dv_ref):
+def band_kernel(halo, q_ref, g_ref, lse_ref, dl_ref, ps_ref, k_ref, v_ref, dq_ref, dk_ref, dv_ref):
     heads, tokens, depth = q_ref.shape
     tiles = tokens // BLOCK
-    reach = WINDOW_LENGTH // BLOCK + 1
+    reach = WINDOW_LENGTH // BLOCK
     dk_ref[...] = jnp.zeros(dk_ref.shape, jnp.float32)
     dv_ref[...] = jnp.zeros(dv_ref.shape, jnp.float32)
     last = (((0,), (0,)), ((), ()))
     cross = (((1,), (1,)), ((), ()))
-    row = lax.broadcasted_iota(jnp.int32, (BLOCK, BLOCK), 0)
+    gap = lax.broadcasted_iota(jnp.int32, (BLOCK, BLOCK), 0) - lax.broadcasted_iota(
+        jnp.int32, (BLOCK, BLOCK), 1
+    )
     col = lax.broadcasted_iota(jnp.int32, (BLOCK, BLOCK), 1)
-
-    def one_tile(t, carry):
-        first = pl.multiple_of(t * BLOCK, BLOCK)
-        starts = ps_ref[pl.ds(first, BLOCK), :]
+    for t in range(tiles):
+        rows = slice(t * BLOCK, (t + 1) * BLOCK)
+        if halo:
+            blocks = [(b, t + b) for b in range(reach - t)]
+        else:
+            blocks = [(b, t + b - reach) for b in range(reach - t, reach + 1)]
+        starts = ps_ref[rows, :]
         for h in range(heads):
-            query = q_ref[h, pl.ds(first, BLOCK), :]
-            grad = g_ref[h, pl.ds(first, BLOCK), :]
-            logsum = lse_ref[h, pl.ds(first, BLOCK), :]
-            delta = dl_ref[h, pl.ds(first, BLOCK), :]
+            query = q_ref[h, rows, :]
+            grad = g_ref[h, rows, :]
+            logsum = lse_ref[h, rows, :]
+            delta = dl_ref[h, rows, :]
             query_acc = jnp.zeros((BLOCK, depth), jnp.float32)
-            for b in range(reach):
-                key_first = pl.multiple_of((t + b) * BLOCK, BLOCK)
-                key = k_ref[pl.ds(key_first, BLOCK), :]
-                value = v_ref[pl.ds(key_first, BLOCK), :]
+            for b, kb in blocks:
+                keys_at = slice(kb * BLOCK, (kb + 1) * BLOCK)
+                key = k_ref[keys_at, :]
+                value = v_ref[keys_at, :]
                 scores = (
                     lax.dot_general(query, key, cross, preferred_element_type=jnp.float32)
                     * score_scale
                 )
-                gap = row - col + (WINDOW_LENGTH - b * BLOCK)
-                visible = (gap >= 0) & (gap < WINDOW_LENGTH) & (col + key_first >= starts)
+                key_first = kb * BLOCK + (0 if halo else WINDOW_LENGTH)
+                visible = col >= starts - key_first
+                if b == 0:
+                    visible = visible & (gap < 0)
+                if b == reach:
+                    visible = visible & (gap >= 0)
                 probs = jnp.where(visible, jnp.exp(scores - logsum), 0.0)
                 dprobs = lax.dot_general(grad, value, cross, preferred_element_type=jnp.float32)
                 low_scores = (probs * (dprobs - delta)).astype(jnp.bfloat16)
                 query_acc = query_acc + jnp.dot(
                     low_scores, key, preferred_element_type=jnp.float32
                 )
-                dk_ref[pl.ds(key_first, BLOCK), :] += lax.dot_general(
+                dk_ref[keys_at, :] += lax.dot_general(
                     low_scores, query, last, preferred_element_type=jnp.float32
                 )
-                dv_ref[pl.ds(key_first, BLOCK), :] += lax.dot_general(
+                dv_ref[keys_at, :] += lax.dot_general(
                     probs.astype(jnp.bfloat16), grad, last, preferred_element_type=jnp.float32
                 )
-            dq_ref[h, pl.ds(first, BLOCK), :] = query_acc
-        return carry
-
-    lax.fori_loop(0, tiles, one_tile, 0)
-
-
-def band_pallas(query, grad, logsum, delta, start, base, keys, values):
+            dq_ref[h, rows, :] = query_acc
+
+
+def band_part(halo, query, grad, logsum, delta, start_rel, keys, values):
     group, tokens, depth = query.shape
     total = keys.shape[0]
-    start_rel = (start - base + WINDOW_LENGTH)[:, None]
-    dq, dk, dv = pl.pallas_call(
-        band_kernel,
+    return pl.pallas_call(
+        partial(band_kernel, halo),
         out_shape=(
             jax.ShapeDtypeStruct((group, tokens, depth), jnp.float32),
             jax.ShapeDtypeStruct((total, depth), jnp.float32),
             jax.ShapeDtypeStruct((total, depth), jnp.float32),
         ),
     )(query, grad, logsum[..., None], delta[..., None], start_rel, keys, values)
-    return dq.transpose(1, 0, 2), dk, dv
 
 
 def split_three(x):
@@ -184,16 +190,16 @@
     forward_g = qf_packed[heads_here:]
     delta_g = jnp.einsum("gtd,gtd->gt", forward_g, grad_g, preferred_element_type=jnp.float32)
     base = lax.axis_index("sh") * tokens
-    keys = jnp.concatenate([far[0], key_own], axis=0)
-    values = jnp.concatenate([far[1], value_own], axis=0)
-    query_sum, key_sum, value_sum = band_pallas(
-        query_g, grad_g, logsum_g, delta_g, start_g, base, keys, values
-    )
-    back = shifted(
-        jnp.stack([key_sum[:WINDOW_LENGTH], value_sum[:WINDOW_LENGTH]]).astype(jnp.bfloat16),
-        "sh",
-        -1,
-    )
+    start_rel = (start_g - base + WINDOW_LENGTH)[:, None]
+    query_far, key_far, value_far = band_part(
+        True, query_g, grad_g, logsum_g, delta_g, start_rel, far[0], far[1]
+    )
+    back = shifted(jnp.stack([key_far, value_far]).astype(jnp.bfloat16), "sh", -1)
+    query_g, key_far = lax.optimization_barrier((query_g, key_far))
+    query_own, key_sum, value_sum = band_part(
+        False, query_g, grad_g, logsum_g, delta_g, start_rel, key_own, value_own
+    )
+    query_sum = (query_far + query_own).transpose(1, 0, 2)
 
     def to_tokens(x):
         items = x.shape[1]
@@ -203,8 +209,8 @@
 
     query_out = to_tokens((query_sum * score_scale).astype(jnp.bfloat16))
     query_out = query_out.reshape(query_out.shape[0], -1, depth)
-    key_total = key_sum[WINDOW_LENGTH:] + back[0].astype(jnp.float32)
-    value_total = value_sum[WINDOW_LENGTH:] + back[1].astype(jnp.float32)
+    key_total = key_sum + back[0].astype(jnp.float32)
+    value_total = value_sum + back[1].astype(jnp.float32)
     key_grad = (key_total * score_scale).astype(jnp.bfloat16)
     value_grad = value_total.astype(jnp.bfloat16)
     kv_out = to_tokens(jnp.stack([key_grad, value_grad], axis=1))

time: 122 us -> 124 us (1.016)
  Pallas kernels: 17.9 us -> 20.3 us
    all_to_all x2, waiting for transfers between devices: 12.3 us -> 18.9 us  [to_tokens(): lax.all_to_all(x, ('sl', 'head'), split_axis=0, concat_axis=1, tiled=True)]
    ppermute x2, waiting for transfers between devices: 5.56 us -> 0.01 us  [shifted(): return lax.ppermute(value, axis, pairs)]
    pallas_call x1 -> x2, Pallas kernels: 17.9 us -> 20.3 us  [band_part(): pl.pallas_call(partial(band_kernel, halo), out_shape=(jax.ShapeDtypeStruc...]
    another operation x2 -> x0, local copies, waits for them, and re-layouts: 2.23 us -> none  [on_device(): jnp.stack([key_sum[:WINDOW_LENGTH], value_sum[:WINDOW_LENGTH]])]
    convert_element_type x1, other arithmetic: 0.12 us -> 1.36 us  [on_device(): query_out = to_tokens((query_sum * score_scale).astype(jnp.bfloat16))]
  transfers between devices with their start and end apart: 7 -> 7, of which waited for: 6 -> 5; matrix products, arithmetic and copies ran while one was open for 12% -> 13% of each run, Pallas kernels for 0% -> 8%
where the time goes in v8:
time: 124 us; the launch traced here: 123 us
  waiting for transfers between devices  42.9 us (35%)
  starting transfers between devices  34.3 us (28%)
  Pallas kernels  20.3 us (16%)
  local copies, waits for them, and re-layouts  18.7 us (15%)
  other arithmetic  6.44 us (5%)
    pallas_call x2, Pallas kernels, band_part(): pl.pallas_call(partial(band_kernel, halo), out_shape=(jax.ShapeDtypeStruc...  20.3 us
    all_to_all x2, waiting for transfers between devices, to_tokens(): lax.all_to_all(x, ('sl', 'head'), split_axis=0, concat_axis=1, tiled=True)  18.9 us
    ppermute x2, starting transfers between devices, shifted(): return lax.ppermute(value, axis, pairs)  15.3 us
    all_to_all x1, waiting for transfers between devices, on_device(): lax.all_to_all(kv_packed, 'sl', split_axis=0, concat_axis=2, tiled=True)[0]  10.1 us
    all_to_all x1, waiting for transfers between devices, on_device(): lax.all_to_all(grad_g, ('sl', 'head'), split_axis=0, concat_axis=2, tiled...  8.13 us
    all_to_all x2, starting transfers between devices, to_tokens(): lax.all_to_all(x, ('sl', 'head'), split_axis=0, concat_axis=1, tiled=True)  7.28 us
    all_to_all x1, waiting for transfers between devices, on_device(): lax.all_to_all(qf_packed, 'sl', split_axis=0, concat_axis=2, tiled=True)[0]  5.79 us
    all_to_all x1, starting transfers between devices, on_device(): lax.all_to_all(kv_packed, 'sl', split_axis=0, concat_axis=2, tiled=True)[0]  4.59 us
  transfers between devices with their start and end apart: 7, of which 5 were waited for; matrix products, arithmetic and copies ran while one was open for 13% of the time, Pallas kernels for 8%

profile of v8, /device:TPU:4, one launch (start us, length us, event | category | flops | bytes accessed | tf_op | source)
XLA Modules:
  0.0 123.5 jit_solution(6948406460681548504)
XLA Ops:
  0.6 0.7 reshape.82
  1.3 0.0 copy-start.8
  1.4 0.7 copy-done.8
  2.1 0.0 copy-start.7
  2.1 1.3 %copy.86 = bf16[256,4,128]{0,1,2:T(4,128)(2,1)S(1)} copy(bf16[256,4,128]{2,1,0:T(4,128)(2,1)} %param.8) | data formatting | bytes 524288 | tf_op args[1]
  3.3 0.0 copy-done.7
  3.3 0.2 copy.87
  3.6 0.1 fusion.14
  3.7 0.7 pad_maximum_fusion.1
  4.4 1.0 copy.91
  5.4 0.0 copy-start.2
  5.4 4.6 %all-to-all-start.1 = ((bf16[4,3,256,128]{2,3,1,0:T(8,128)(2,1)}), bf16[4,3,256,128]{2,3,1,0:T(8,128)(2,1)S(1)}, u32[]{:S(2)}, u32[]{:S(2)}) async-start(bf16[4,3,256,128]{2,3,1,0:T(8,128)(2,1)} %copy.91), calls=%async_computation.1 | async-start | bytes 1572864 | tf_op jit(solution)/shard_map/all_to_all | solution.py:169
  10.0 0.0 copy-done.2
  10.0 0.0 copy-start.3
  10.0 0.1 copy.82
  10.0 1.0 copy-done.3
  11.0 0.1 copy.83
  11.1 1.1 pad_maximum_fusion
  12.2 0.0 copy-start.4
  12.2 10.1 %all-to-all-done.1 = bf16[4,3,256,128]{2,3,1,0:T(8,128)(2,1)S(1)} async-done(((bf16[4,3,256,128]{2,3,1,0:T(8,128)(2,1)}), bf16[4,3,256,128]{2,3,1,0:T(8,128)(2,1)S(1)}, u32[]{:S(2)}, u32[]{:S(2)}) %all-to-all-start.1) | async-done | bytes 786464 | tf_op jit(solution)/shard_map/all_to_all | solution.py:169
  22.2 3.5 %all-to-all-start = ((bf16[4,4,256,128]{3,2,1,0:T(8,128)(2,1)}), bf16[4,4,256,128]{3,2,1,0:T(8,128)(2,1)S(1)}, u32[]{:S(2)}, u32[]{:S(2)}) async-start(bf16[4,4,256,128]{3,2,1,0:T(8,128)(2,1)} %pad_maximum_fusion), calls=%async_computation | async-start | bytes 2097152 | tf_op jit(solution)/shard_map/all_to_all | solution.py:188
  25.8 0.0 copy-done.4
  25.8 1.0 copy.85
  26.8 0.4 copy.92
  27.2 1.0 copy.95
  28.2 3.8 %collective-permute-start = (bf16[2,1024,128]{2,1,0:T(8,128)(2,1)}, bf16[2,1024,128]{2,1,0:T(8,128)(2,1)S(1)}, u32[]{:S(2)}, u32[]{:S(2)}) collective-permute-start(bf16[2,1024,128]{2,1,0:T(8,128)(2,1)} %bitcast.35), channel_id=1, source_target_pairs={{0,4},{4,8},{8,12},{12,16},{16,20},{20,24},{24,28},{28,32},{32,36}... | collective-permute-start | bytes 1572872 | tf_op jit(solution)/shard_map/ppermute | solution.py:19
  32.0 0.8 slice_bitcast_fusion.4
  32.9 0.1 slice_convert_fusion
  33.0 1.2 fusion.5.ps_ref
  34.2 5.8 %all-to-all-done = bf16[4,4,256,128]{3,2,1,0:T(8,128)(2,1)S(1)} async-done(((bf16[4,4,256,128]{3,2,1,0:T(8,128)(2,1)}), bf16[4,4,256,128]{3,2,1,0:T(8,128)(2,1)S(1)}, u32[]{:S(2)}, u32[]{:S(2)}) %all-to-all-start) | async-done | bytes 1048608 | tf_op jit(solution)/shard_map/all_to_all | solution.py:188
  40.0 3.6 %all-to-all-start.2 = ((bf16[16,2,64,128]{3,2,1,0:T(8,128)(2,1)}), bf16[16,2,64,128]{3,2,1,0:T(8,128)(2,1)S(1)}, u32[]{:S(2)}, u32[]{:S(2)}) async-start(bf16[16,2,64,128]{3,2,1,0:T(8,128)(2,1)} %bitcast.9), calls=%async_computation.2 | async-start | bytes 1048576 | tf_op jit(solution)/shard_map/all_to_all | solution.py:172
  43.6 0.2 copy.94
  43.8 1.4 %copy.96.lse_ref = f32[2,1024,1]{2,1,0:T(8,128)} copy(f32[2,1024,1]{1,0,2:T(2,128)S(1)} %bitcast.140) | data formatting | bytes 16384 | tf_op jit(solution)/shard_map/broadcast_in_dim | solution.py:122
  45.2 0.1 copy.125
  45.3 0.9 fusion.20
  46.2 8.1 %all-to-all-done.2 = bf16[16,2,64,128]{3,2,1,0:T(8,128)(2,1)S(1)} async-done(((bf16[16,2,64,128]{3,2,1,0:T(8,128)(2,1)}), bf16[16,2,64,128]{3,2,1,0:T(8,128)(2,1)S(1)}, u32[]{:S(2)}, u32[]{:S(2)}) %all-to-all-start.2) | async-done | bytes 524320 | tf_op jit(solution)/shard_map/all_to_all | solution.py:172
  54.4 0.0 copy-start
  54.4 0.4 fusion
  54.8 0.4 copy-done
  55.2 1.3 %copy.97.dl_ref = f32[2,1024,1]{2,1,0:T(8,128)} copy(f32[2,1024,1]{1,0,2:T(2,128)S(1)} %bitcast.139) | data formatting | bytes 16384 | tf_op jit(solution)/shard_map/broadcast_in_dim | solution.py:122
  56.5 0.0 collective-permute-done
  56.5 0.9 slice_bitcast_fusion.2
  57.4 10.0 %shard_map.94 = (f32[2,1024,128]{2,1,0:T(8,128)}, f32[1024,128]{1,0:T(8,128)}, f32[1024,128]{1,0:T(8,128)}) custom-call(bf16[2,1024,128]{2,1,0:T(8,128)(2,1)} %bitcast.121, bf16[2,1024,128]{2,1,0:T(8,128)(2,1)} %bitcast.117, f32[2,1024,1]{2,1,0:T(8,128)} %copy.96.lse_ref, f32[2,1024,1]{2,1,0:T(8,128)} %copy.97.dl_ref, s32[1024,1]{1,0:T(8,128)} %fusion.5.ps_ref, ...), custom_call_target="tpu_custom_call" | custom-call | tf_op jit(solution)/shard_map/pallas_call | solution.py:115
  67.4 1.3 %convert_bitcast_fusion = (bf16[1,1024,128]{2,1,0:T(8,128)(2,1)S(1)}, bf16[1,1024,128]{2,1,0:T(8,128)(2,1)S(1)}) fusion(f32[1024,128]{1,0:T(8,128)} %get-tuple-element.19, f32[1024,128]{1,0:T(8,128)} %get-tuple-element.15), kind=kLoop, calls=%fused_computation.34 | loop fusion | flops 262144 | bytes 1572864 | tf_op jit(solution)/shard_map/stack | solution.py:197
  68.7 0.1 pad_maximum_fusion.2
  68.7 11.5 %collective-permute-start.1 = (bf16[2,1024,128]{2,1,0:T(8,128)(2,1)S(1)}, bf16[2,1024,128]{2,1,0:T(8,128)(2,1)S(1)}, u32[]{:S(2)}, u32[]{:S(2)}) collective-permute-start(bf16[2,1024,128]{2,1,0:T(8,128)(2,1)S(1)} %pad_maximum_fusion.2), channel_id=1, source_target_pairs={{4,0},{8,4},{12,8},{16,12},{20,16},{24,20},{28,24},{32,28},{36,32}... | collective-permute-start | bytes 1572872 | tf_op jit(solution)/shard_map/ppermute | solution.py:19
  80.3 0.0 copy-start.1
  80.3 10.2 %shard_map.95 = (f32[2,1024,128]{2,1,0:T(8,128)}, f32[1024,128]{1,0:T(8,128)}, f32[1024,128]{1,0:T(8,128)}) custom-call(bf16[2,1024,128]{2,1,0:T(8,128)(2,1)} %bitcast.122, bf16[2,1024,128]{2,1,0:T(8,128)(2,1)} %bitcast.118, f32[2,1024,1]{2,1,0:T(8,128)} %copy.96.lse_ref, f32[2,1024,1]{2,1,0:T(8,128)} %copy.97.dl_ref, s32[1024,1]{1,0:T(8,128)} %fusion.5.ps_ref, ...), custom_call_target="tpu_custom_call" | custom-call | tf_op jit(solution)/shard_map/pallas_call | solution.py:115
  90.5 0.0 copy-done.1
  90.5 1.4 %fusion.1 = bf16[1024,2,128]{2,0,1:T(8,128)(2,1)S(1)} fusion(f32[2,1024,128]{2,1,0:T(8,128)S(1)} %copy-done.1, f32[2,1024,128]{2,1,0:T(8,128)} %get-tuple-element.17), kind=kLoop, calls=%fused_computation.6 | loop fusion | flops 786432 | bytes 2621440 | tf_op jit(solution)/shard_map/convert_element_type | solution.py:210
  91.9 1.3 %copy.100 = bf16[1024,2,128]{2,1,0:T(2,128)(2,1)} copy(bf16[1024,2,128]{2,0,1:T(8,128)(2,1)S(1)} %fusion.1) | data formatting | bytes 1048576 | tf_op jit(solution)/shard_map/convert_element_type | solution.py:210
  93.2 3.7 %all-to-all-start.3 = ((bf16[1024,2,128]{2,1,0:T(2,128)(2,1)}), bf16[1024,2,128]{2,1,0:T(2,128)(2,1)S(1)}, u32[]{:S(2)}, u32[]{:S(2)}) async-start(bf16[1024,2,128]{2,1,0:T(2,128)(2,1)} %copy.100), calls=%async_computation.3 | async-start | bytes 1048576 | tf_op jit(solution)/shard_map/all_to_all | solution.py:206
  96.9 0.0 collective-permute-done.1
  97.0 0.0 copy-done.5
  97.0 0.0 copy-done.6
  97.0 0.1 fusion.11
  97.1 0.1 pad_maximum_fusion.3
  97.2 1.4 %copy.102 = bf16[1024,2,128]{2,1,0:T(2,128)(2,1)} copy(bf16[1024,2,128]{2,0,1:T(8,128)(2,1)S(1)} %pad_maximum_fusion.3) | data formatting | bytes 1048576 | tf_op jit(solution)/shard_map/stack | solution.py:216
  98.5 9.2 %all-to-all-done.3 = bf16[1024,2,128]{2,1,0:T(2,128)(2,1)S(1)} async-done(((bf16[1024,2,128]{2,1,0:T(2,128)(2,1)}), bf16[1024,2,128]{2,1,0:T(2,128)(2,1)S(1)}, u32[]{:S(2)}, u32[]{:S(2)}) %all-to-all-start.3) | async-done | bytes 524320 | tf_op jit(solution)/shard_map/all_to_all | solution.py:206
  107.7 3.6 %all-to-all-start.4 = ((bf16[1024,2,128]{2,1,0:T(2,128)(2,1)}), bf16[1024,2,128]{2,1,0:T(2,128)(2,1)S(1)}, u32[]{:S(2)}, u32[]{:S(2)}) async-start(bf16[1024,2,128]{2,1,0:T(2,128)(2,1)} %copy.102), calls=%async_computation.4 | async-start | bytes 1048576 | tf_op jit(solution)/shard_map/all_to_all | solution.py:206
  111.3 1.2 copy.101
  112.5 9.6 %all-to-all-done.4 = bf16[1024,2,128]{2,1,0:T(2,128)(2,1)S(1)} async-done(((bf16[1024,2,128]{2,1,0:T(2,128)(2,1)}), bf16[1024,2,128]{2,1,0:T(2,128)(2,1)S(1)}, u32[]{:S(2)}, u32[]{:S(2)}) %all-to-all-start.4) | async-done | bytes 524320 | tf_op jit(solution)/shard_map/all_to_all | solution.py:206
  122.1 0.4 copy.126
  122.5 1.0 fusion.21
  (16 shorter events, 0.2 us)
Async XLA Ops:
  1.3 0.7 copy-start.8
  2.1 1.3 %copy-start.7 = (bf16[256,4,128]{2,1,0:T(4,128)(2,1)S(1)}, bf16[256,4,128]{2,1,0:T(4,128)(2,1)}, u32[]{:S(2)}) copy-start(bf16[256,4,128]{2,1,0:T(4,128)(2,1)} %param.9) | copy-start | bytes 786436
  5.4 4.6 %copy-start.2 = (bf16[256,8,128]{2,1,0:T(8,128)(2,1)S(1)}, bf16[256,8,128]{2,1,0:T(8,128)(2,1)}, u32[]{:S(2)}) copy-start(bf16[256,8,128]{2,1,0:T(8,128)(2,1)} %param.7) | copy-start | bytes 1572868
  5.4 16.9 %all-to-all-start.1 = ((bf16[4,3,256,128]{2,3,1,0:T(8,128)(2,1)}), bf16[4,3,256,128]{2,3,1,0:T(8,128)(2,1)S(1)}, u32[]{:S(2)}, u32[]{:S(2)}) async-start(bf16[4,3,256,128]{2,3,1,0:T(8,128)(2,1)} %copy.91), calls=%async_computation.1 | async-start | bytes 1572864 | tf_op jit(solution)/shard_map/all_to_all | solution.py:169
  10.0 1.0 copy-start.3
  12.2 13.6 %copy-start.4 = (bf16[64,32,128]{2,1,0:T(8,128)(2,1)S(1)}, bf16[64,32,128]{2,1,0:T(8,128)(2,1)}, u32[]{:S(2)}) copy-start(bf16[64,32,128]{2,1,0:T(8,128)(2,1)} %param.11) | copy-start | bytes 1572868
  22.2 17.7 %all-to-all-start = ((bf16[4,4,256,128]{3,2,1,0:T(8,128)(2,1)}), bf16[4,4,256,128]{3,2,1,0:T(8,128)(2,1)S(1)}, u32[]{:S(2)}, u32[]{:S(2)}) async-start(bf16[4,4,256,128]{3,2,1,0:T(8,128)(2,1)} %pad_maximum_fusion), calls=%async_computation | async-start | bytes 2097152 | tf_op jit(solution)/shard_map/all_to_all | solution.py:188
  28.2 28.3 %collective-permute-start = (bf16[2,1024,128]{2,1,0:T(8,128)(2,1)}, bf16[2,1024,128]{2,1,0:T(8,128)(2,1)S(1)}, u32[]{:S(2)}, u32[]{:S(2)}) collective-permute-start(bf16[2,1024,128]{2,1,0:T(8,128)(2,1)} %bitcast.35), channel_id=1, source_target_pairs={{0,4},{4,8},{8,12},{12,16},{16,20},{20,24},{24,28},{28,32},{32,36}... | collective-permute-start | bytes 1572872 | tf_op jit(solution)/shard_map/ppermute | solution.py:19
  40.0 14.4 %all-to-all-start.2 = ((bf16[16,2,64,128]{3,2,1,0:T(8,128)(2,1)}), bf16[16,2,64,128]{3,2,1,0:T(8,128)(2,1)S(1)}, u32[]{:S(2)}, u32[]{:S(2)}) async-start(bf16[16,2,64,128]{3,2,1,0:T(8,128)(2,1)} %bitcast.9), calls=%async_computation.2 | async-start | bytes 1048576 | tf_op jit(solution)/shard_map/all_to_all | solution.py:172
  54.4 0.8 copy-start
  68.7 28.2 %collective-permute-start.1 = (bf16[2,1024,128]{2,1,0:T(8,128)(2,1)S(1)}, bf16[2,1024,128]{2,1,0:T(8,128)(2,1)S(1)}, u32[]{:S(2)}, u32[]{:S(2)}) collective-permute-start(bf16[2,1024,128]{2,1,0:T(8,128)(2,1)S(1)} %pad_maximum_fusion.2), channel_id=1, source_target_pairs={{4,0},{8,4},{12,8},{16,12},{20,16},{24,20},{28,24},{32,28},{36,32}... | collective-permute-start | bytes 1572872 | tf_op jit(solution)/shard_map/ppermute | solution.py:19
  80.3 10.3 %copy-start.1 = (f32[2,1024,128]{2,1,0:T(8,128)S(1)}, f32[2,1024,128]{2,1,0:T(8,128)}, u32[]{:S(2)}) copy-start(f32[2,1024,128]{2,1,0:T(8,128)} %get-tuple-element.14) | copy-start | bytes 3145732
  93.2 3.7 %copy-start.5 = (f32[1024,128]{1,0:T(8,128)S(1)}, f32[1024,128]{1,0:T(8,128)}, u32[]{:S(2)}) copy-start(f32[1024,128]{1,0:T(8,128)} %get-tuple-element.18) | copy-start | bytes 1572868
  93.2 3.7 %copy-start.6 = (f32[1024,128]{1,0:T(8,128)S(1)}, f32[1024,128]{1,0:T(8,128)}, u32[]{:S(2)}) copy-start(f32[1024,128]{1,0:T(8,128)} %get-tuple-element.20) | copy-start | bytes 1572868
  93.2 14.5 %all-to-all-start.3 = ((bf16[1024,2,128]{2,1,0:T(2,128)(2,1)}), bf16[1024,2,128]{2,1,0:T(2,128)(2,1)S(1)}, u32[]{:S(2)}, u32[]{:S(2)}) async-start(bf16[1024,2,128]{2,1,0:T(2,128)(2,1)} %copy.100), calls=%async_computation.3 | async-start | bytes 1048576 | tf_op jit(solution)/shard_map/all_to_all | solution.py:206
  107.7 14.4 %all-to-all-start.4 = ((bf16[1024,2,128]{2,1,0:T(2,128)(2,1)}), bf16[1024,2,128]{2,1,0:T(2,128)(2,1)S(1)}, u32[]{:S(2)}, u32[]{:S(2)}) async-start(bf16[1024,2,128]{2,1,0:T(2,128)(2,1)} %copy.102), calls=%async_computation.4 | async-start | bytes 1048576 | tf_op jit(solution)/shard_map/all_to_all | solution.py:206

commit v9 on v8

--- a/solution.py
+++ b/solution.py
@@ -207,16 +207,16 @@
         rows_out = x.shape[0]
         return x.reshape(rows_out, ring, head_size, items, depth).transpose(0, 2, 1, 3, 4)
 
-    query_out = to_tokens((query_sum * score_scale).astype(jnp.bfloat16))
-    query_out = query_out.reshape(query_out.shape[0], -1, depth)
     key_total = key_sum + back[0].astype(jnp.float32)
     value_total = value_sum + back[1].astype(jnp.float32)
-    key_grad = (key_total * score_scale).astype(jnp.bfloat16)
-    value_grad = value_total.astype(jnp.bfloat16)
-    kv_out = to_tokens(jnp.stack([key_grad, value_grad], axis=1))
-    rows_out = kv_out.shape[0]
-    key_out = kv_out[:, :, :, 0].reshape(rows_out, -1, depth)
-    value_out = kv_out[:, :, :, 1].reshape(rows_out, -1, depth)
+    query_grad = (query_sum * score_scale).astype(jnp.bfloat16)
+    key_grad = (key_total * score_scale).astype(jnp.bfloat16)[:, None]
+    value_grad = value_total.astype(jnp.bfloat16)[:, None]
+    outs = to_tokens(jnp.concatenate([query_grad, key_grad, value_grad], axis=1))
+    rows_out = outs.shape[0]
+    query_out = outs[:, :, :, :heads_here].reshape(rows_out, -1, depth)
+    key_out = outs[:, :, :, heads_here].reshape(rows_out, -1, depth)
+    value_out = outs[:, :, :, heads_here + 1].reshape(rows_out, -1, depth)
     return query_out, key_out, value_out
 
 

time: 124 us -> 116 us (0.935)
  blocking collectives: 0 us -> 19.1 us
  waiting for transfers between devices: 42.9 us -> 24.1 us
  starting transfers between devices: 34.3 us -> 27 us
  local copies, waits for them, and re-layouts: 18.7 us -> 16.5 us
    all_to_all x0 -> x1, blocking collectives: none -> 19.1 us  [to_tokens(): lax.all_to_all(x, ('sl', 'head'), split_axis=0, concat_axis=1, tiled=True)]
    all_to_all x2 -> x0, waiting for transfers between devices: 18.9 us -> none  [to_tokens(): lax.all_to_all(x, ('sl', 'head'), split_axis=0, concat_axis=1, tiled=True)]
    all_to_all x2 -> x0, starting transfers between devices: 7.28 us -> none  [to_tokens(): lax.all_to_all(x, ('sl', 'head'), split_axis=0, concat_axis=1, tiled=True)]
    slice x1 -> x3, local copies, waits for them, and re-layouts: 0.97 us -> 2.76 us  [the longest x2 1.79 us: on_device(): query_out = outs[:, :, :, :heads_here].reshape(rows_out, -1, depth)]
    another operation x1 -> x0, local copies, waits for them, and re-layouts: 1.35 us -> none  [on_device(): kv_out = to_tokens(jnp.stack([key_grad, value_grad], axis=1))]
    convert_element_type x1 -> x0, local copies, waits for them, and re-layouts: 1.33 us -> none  [on_device(): query_out = to_tokens((query_sum * score_scale).astype(jnp.bfloat16))]
  transfers between devices with their start and end apart: 7 -> 5, of which waited for: 5 -> 3; matrix products, arithmetic and copies ran while one was open for 13% -> 10% of each run, Pallas kernels for 8% -> 9%
where the time goes in v9:
time: 116 us; the launch traced here: 115 us
  starting transfers between devices  27 us (23%)
  waiting for transfers between devices  24.1 us (21%)
  Pallas kernels  20.3 us (18%)
  blocking collectives  19.1 us (16%)
  local copies, waits for them, and re-layouts  16.5 us (14%)
  other arithmetic  7.24 us (6%)
    pallas_call x2, Pallas kernels, band_part(): pl.pallas_call(partial(band_kernel, halo), out_shape=(jax.ShapeDtypeStruc...  20.3 us
    all_to_all x1, blocking collectives, to_tokens(): lax.all_to_all(x, ('sl', 'head'), split_axis=0, concat_axis=1, tiled=True)  19.1 us
    ppermute x2, starting transfers between devices, shifted(): return lax.ppermute(value, axis, pairs)  15.3 us
    all_to_all x1, waiting for transfers between devices, on_device(): lax.all_to_all(kv_packed, 'sl', split_axis=0, concat_axis=2, tiled=True)[0]  10.1 us
    all_to_all x1, waiting for transfers between devices, on_device(): lax.all_to_all(grad_g, ('sl', 'head'), split_axis=0, concat_axis=2, tiled...  8.15 us
    all_to_all x1, waiting for transfers between devices, on_device(): lax.all_to_all(qf_packed, 'sl', split_axis=0, concat_axis=2, tiled=True)[0]  5.82 us
    all_to_all x1, starting transfers between devices, on_device(): lax.all_to_all(kv_packed, 'sl', split_axis=0, concat_axis=2, tiled=True)[0]  4.59 us
    all_to_all x1, starting transfers between devices, on_device(): lax.all_to_all(grad_g, ('sl', 'head'), split_axis=0, concat_axis=2, tiled...  3.57 us
  transfers between devices with their start and end apart: 5, of which 3 were waited for; matrix products, arithmetic and copies ran while one was open for 10% of the time, Pallas kernels for 9%

profile of v9, /device:TPU:4, one launch (start us, length us, event | category | flops | bytes accessed | tf_op | source)
XLA Modules:
  0.0 115.2 jit_solution(14435589110713157114)
XLA Ops:
  0.6 0.0 copy-start.8
  0.6 0.7 reduce-precision_convert_fusion.3
  1.4 0.0 copy-done.8
  1.4 0.0 copy-start.7
  1.4 1.3 %copy.84 = bf16[256,4,128]{0,1,2:T(4,128)(2,1)S(1)} copy(bf16[256,4,128]{2,1,0:T(4,128)(2,1)} %param.8) | data formatting | bytes 524288 | tf_op args[1]
  2.7 0.0 copy-done.7
  2.7 0.2 copy.85
  3.0 0.1 fusion.14
  3.0 0.7 pad_maximum_fusion.2
  3.7 1.0 copy.89
  4.7 0.0 copy-start.2
  4.7 4.6 %all-to-all-start.1 = ((bf16[4,3,256,128]{2,3,1,0:T(8,128)(2,1)}), bf16[4,3,256,128]{2,3,1,0:T(8,128)(2,1)S(1)}, u32[]{:S(2)}, u32[]{:S(2)}) async-start(bf16[4,3,256,128]{2,3,1,0:T(8,128)(2,1)} %copy.89), calls=%async_computation.1 | async-start | bytes 1572864 | tf_op jit(solution)/shard_map/all_to_all | solution.py:169
  9.3 0.0 copy-done.2
  9.3 0.0 copy-start.3
  9.3 0.1 copy.80
  9.4 1.0 copy-done.3
  10.4 0.1 copy.81
  10.4 1.1 pad_maximum_fusion
  11.5 0.0 copy-start.4
  11.5 10.1 %all-to-all-done.1 = bf16[4,3,256,128]{2,3,1,0:T(8,128)(2,1)S(1)} async-done(((bf16[4,3,256,128]{2,3,1,0:T(8,128)(2,1)}), bf16[4,3,256,128]{2,3,1,0:T(8,128)(2,1)S(1)}, u32[]{:S(2)}, u32[]{:S(2)}) %all-to-all-start.1) | async-done | bytes 786464 | tf_op jit(solution)/shard_map/all_to_all | solution.py:169
  21.6 3.5 %all-to-all-start = ((bf16[4,4,256,128]{3,2,1,0:T(8,128)(2,1)}), bf16[4,4,256,128]{3,2,1,0:T(8,128)(2,1)S(1)}, u32[]{:S(2)}, u32[]{:S(2)}) async-start(bf16[4,4,256,128]{3,2,1,0:T(8,128)(2,1)} %pad_maximum_fusion), calls=%async_computation | async-start | bytes 2097152 | tf_op jit(solution)/shard_map/all_to_all | solution.py:188
  25.1 0.0 copy-done.4
  25.1 1.0 copy.83
  26.2 0.4 copy.90
  26.6 1.0 copy.93
  27.6 3.8 %collective-permute-start = (bf16[2,1024,128]{2,1,0:T(8,128)(2,1)}, bf16[2,1024,128]{2,1,0:T(8,128)(2,1)S(1)}, u32[]{:S(2)}, u32[]{:S(2)}) collective-permute-start(bf16[2,1024,128]{2,1,0:T(8,128)(2,1)} %bitcast.35), channel_id=1, source_target_pairs={{0,4},{4,8},{8,12},{12,16},{16,20},{20,24},{24,28},{28,32},{32,36}... | collective-permute-start | bytes 1572872 | tf_op jit(solution)/shard_map/ppermute | solution.py:19
  31.4 0.8 slice_bitcast_fusion.4
  32.2 0.1 slice_convert_fusion
  32.4 1.1 fusion.5.ps_ref
  33.5 5.8 %all-to-all-done = bf16[4,4,256,128]{3,2,1,0:T(8,128)(2,1)S(1)} async-done(((bf16[4,4,256,128]{3,2,1,0:T(8,128)(2,1)}), bf16[4,4,256,128]{3,2,1,0:T(8,128)(2,1)S(1)}, u32[]{:S(2)}, u32[]{:S(2)}) %all-to-all-start) | async-done | bytes 1048608 | tf_op jit(solution)/shard_map/all_to_all | solution.py:188
  39.3 3.6 %all-to-all-start.2 = ((bf16[16,2,64,128]{3,2,1,0:T(8,128)(2,1)}), bf16[16,2,64,128]{3,2,1,0:T(8,128)(2,1)S(1)}, u32[]{:S(2)}, u32[]{:S(2)}) async-start(bf16[16,2,64,128]{3,2,1,0:T(8,128)(2,1)} %bitcast.9), calls=%async_computation.2 | async-start | bytes 1048576 | tf_op jit(solution)/shard_map/all_to_all | solution.py:172
  43.0 0.2 copy.92
  43.2 1.4 %copy.94.lse_ref = f32[2,1024,1]{2,1,0:T(8,128)} copy(f32[2,1024,1]{1,0,2:T(2,128)S(1)} %bitcast.133) | data formatting | bytes 16384 | tf_op jit(solution)/shard_map/broadcast_in_dim | solution.py:122
  44.6 0.1 copy.123
  44.7 0.9 fusion.21
  45.6 8.2 %all-to-all-done.2 = bf16[16,2,64,128]{3,2,1,0:T(8,128)(2,1)S(1)} async-done(((bf16[16,2,64,128]{3,2,1,0:T(8,128)(2,1)}), bf16[16,2,64,128]{3,2,1,0:T(8,128)(2,1)S(1)}, u32[]{:S(2)}, u32[]{:S(2)}) %all-to-all-start.2) | async-done | bytes 524320 | tf_op jit(solution)/shard_map/all_to_all | solution.py:172
  53.7 0.0 copy-start
  53.8 0.4 fusion
  54.1 0.4 copy-done
  54.6 1.3 %copy.95.dl_ref = f32[2,1024,1]{2,1,0:T(8,128)} copy(f32[2,1024,1]{1,0,2:T(2,128)S(1)} %bitcast.132) | data formatting | bytes 16384 | tf_op jit(solution)/shard_map/broadcast_in_dim | solution.py:122
  55.9 0.0 collective-permute-done
  55.9 0.8 slice_bitcast_fusion.2
  56.7 10.0 %shard_map.94 = (f32[2,1024,128]{2,1,0:T(8,128)}, f32[1024,128]{1,0:T(8,128)}, f32[1024,128]{1,0:T(8,128)}) custom-call(bf16[2,1024,128]{2,1,0:T(8,128)(2,1)} %bitcast.114, bf16[2,1024,128]{2,1,0:T(8,128)(2,1)} %bitcast.110, f32[2,1024,1]{2,1,0:T(8,128)} %copy.94.lse_ref, f32[2,1024,1]{2,1,0:T(8,128)} %copy.95.dl_ref, s32[1024,1]{1,0:T(8,128)} %fusion.5.ps_ref, ...), custom_call_target="tpu_custom_call" | custom-call | tf_op jit(solution)/shard_map/pallas_call | solution.py:115
  66.8 1.3 %convert_bitcast_fusion = (bf16[1,1024,128]{2,1,0:T(8,128)(2,1)S(1)}, bf16[1,1024,128]{2,1,0:T(8,128)(2,1)S(1)}) fusion(f32[1024,128]{1,0:T(8,128)} %get-tuple-element.19, f32[1024,128]{1,0:T(8,128)} %get-tuple-element.15), kind=kLoop, calls=%fused_computation.34 | loop fusion | flops 262144 | bytes 1572864 | tf_op jit(solution)/shard_map/stack | solution.py:197
  68.0 0.1 pad_maximum_fusion.3
  68.1 11.5 %collective-permute-start.1 = (bf16[2,1024,128]{2,1,0:T(8,128)(2,1)S(1)}, bf16[2,1024,128]{2,1,0:T(8,128)(2,1)S(1)}, u32[]{:S(2)}, u32[]{:S(2)}) collective-permute-start(bf16[2,1024,128]{2,1,0:T(8,128)(2,1)S(1)} %pad_maximum_fusion.3), channel_id=1, source_target_pairs={{4,0},{8,4},{12,8},{16,12},{20,16},{24,20},{28,24},{32,28},{36,32}... | collective-permute-start | bytes 1572872 | tf_op jit(solution)/shard_map/ppermute | solution.py:19
  79.6 0.0 copy-start.1
  79.6 10.3 %shard_map.95 = (f32[2,1024,128]{2,1,0:T(8,128)}, f32[1024,128]{1,0:T(8,128)}, f32[1024,128]{1,0:T(8,128)}) custom-call(bf16[2,1024,128]{2,1,0:T(8,128)(2,1)} %bitcast.115, bf16[2,1024,128]{2,1,0:T(8,128)(2,1)} %bitcast.111, f32[2,1024,1]{2,1,0:T(8,128)} %copy.94.lse_ref, f32[2,1024,1]{2,1,0:T(8,128)} %copy.95.dl_ref, s32[1024,1]{1,0:T(8,128)} %fusion.5.ps_ref, ...), custom_call_target="tpu_custom_call" | custom-call | tf_op jit(solution)/shard_map/pallas_call | solution.py:115
  89.9 0.0 copy-done.1
  89.9 0.0 copy-start.5
  89.9 0.0 copy-start.6
  89.9 1.5 %fusion.1 = bf16[1024,2,128]{2,0,1:T(8,128)(2,1)S(1)} fusion(f32[2,1024,128]{2,1,0:T(8,128)S(1)} %copy-done.1, f32[2,1024,128]{2,1,0:T(8,128)} %get-tuple-element.17), kind=kLoop, calls=%fused_computation.8 | loop fusion | flops 786432 | bytes 2621440 | tf_op jit(solution)/shard_map/convert_element_type | solution.py:212
  91.4 0.0 collective-permute-done.1
  91.4 0.0 copy-done.5
  91.4 0.0 copy-done.6
  91.4 0.1 fusion.11
  91.6 0.1 pad_maximum_fusion.1
  91.7 0.8 copy.98
  92.5 19.1 %all_to_all.60 = bf16[1024,4,128]{2,1,0:T(4,128)(2,1)S(1)} all-to-all(bf16[1024,4,128]{2,1,0:T(4,128)(2,1)S(1)} %copy.98), channel_id=1, replica_groups=mesh['head'=4,'sh'=32,'sl'=4] {'sl','head'}, dimensions={0} | all-to-all | bytes 2097152 | tf_op jit(solution)/shard_map/all_to_all | solution.py:206
  111.6 0.8 copy.122
  112.4 0.2 slice.111
  112.6 1.0 fusion.20
  113.6 1.6 %copy.100 = bf16[64,4,4,2,128]{4,3,2,1,0:T(2,128)(2,1)} copy(bf16[64,4,4,2,128]{4,2,1,0,3:T(4,128)(2,1)S(1)} %slice.111) | data formatting | bytes 1048576 | tf_op jit(solution)/shard_map/slice | solution.py:217
  (14 shorter events, 0.2 us)
Async XLA Ops:
  0.6 0.7 copy-start.8
  1.4 1.3 %copy-start.7 = (bf16[256,4,128]{2,1,0:T(4,128)(2,1)S(1)}, bf16[256,4,128]{2,1,0:T(4,128)(2,1)}, u32[]{:S(2)}) copy-start(bf16[256,4,128]{2,1,0:T(4,128)(2,1)} %param.9) | copy-start | bytes 786436
  4.7 4.6 %copy-start.2 = (bf16[256,8,128]{2,1,0:T(8,128)(2,1)S(1)}, bf16[256,8,128]{2,1,0:T(8,128)(2,1)}, u32[]{:S(2)}) copy-start(bf16[256,8,128]{2,1,0:T(8,128)(2,1)} %param.7) | copy-start | bytes 1572868
  4.7 16.9 %all-to-all-start.1 = ((bf16[4,3,256,128]{2,3,1,0:T(8,128)(2,1)}), bf16[4,3,256,128]{2,3,1,0:T(8,128)(2,1)S(1)}, u32[]{:S(2)}, u32[]{:S(2)}) async-start(bf16[4,3,256,128]{2,3,1,0:T(8,128)(2,1)} %copy.89), calls=%async_computation.1 | async-start | bytes 1572864 | tf_op jit(solution)/shard_map/all_to_all | solution.py:169
  9.3 1.0 copy-start.3
  11.5 13.6 %copy-start.4 = (bf16[64,32,128]{2,1,0:T(8,128)(2,1)S(1)}, bf16[64,32,128]{2,1,0:T(8,128)(2,1)}, u32[]{:S(2)}) copy-start(bf16[64,32,128]{2,1,0:T(8,128)(2,1)} %param.11) | copy-start | bytes 1572868
  21.6 17.7 %all-to-all-start = ((bf16[4,4,256,128]{3,2,1,0:T(8,128)(2,1)}), bf16[4,4,256,128]{3,2,1,0:T(8,128)(2,1)S(1)}, u32[]{:S(2)}, u32[]{:S(2)}) async-start(bf16[4,4,256,128]{3,2,1,0:T(8,128)(2,1)} %pad_maximum_fusion), calls=%async_computation | async-start | bytes 2097152 | tf_op jit(solution)/shard_map/all_to_all | solution.py:188
  27.6 28.3 %collective-permute-start = (bf16[2,1024,128]{2,1,0:T(8,128)(2,1)}, bf16[2,1024,128]{2,1,0:T(8,128)(2,1)S(1)}, u32[]{:S(2)}, u32[]{:S(2)}) collective-permute-start(bf16[2,1024,128]{2,1,0:T(8,128)(2,1)} %bitcast.35), channel_id=1, source_target_pairs={{0,4},{4,8},{8,12},{12,16},{16,20},{20,24},{24,28},{28,32},{32,36}... | collective-permute-start | bytes 1572872 | tf_op jit(solution)/shard_map/ppermute | solution.py:19
  39.3 14.4 %all-to-all-start.2 = ((bf16[16,2,64,128]{3,2,1,0:T(8,128)(2,1)}), bf16[16,2,64,128]{3,2,1,0:T(8,128)(2,1)S(1)}, u32[]{:S(2)}, u32[]{:S(2)}) async-start(bf16[16,2,64,128]{3,2,1,0:T(8,128)(2,1)} %bitcast.9), calls=%async_computation.2 | async-start | bytes 1048576 | tf_op jit(solution)/shard_map/all_to_all | solution.py:172
  53.7 0.8 copy-start
  68.1 23.3 %collective-permute-start.1 = (bf16[2,1024,128]{2,1,0:T(8,128)(2,1)S(1)}, bf16[2,1024,128]{2,1,0:T(8,128)(2,1)S(1)}, u32[]{:S(2)}, u32[]{:S(2)}) collective-permute-start(bf16[2,1024,128]{2,1,0:T(8,128)(2,1)S(1)} %pad_maximum_fusion.3), channel_id=1, source_target_pairs={{4,0},{8,4},{12,8},{16,12},{20,16},{24,20},{28,24},{32,28},{36,32}... | collective-permute-start | bytes 1572872 | tf_op jit(solution)/shard_map/ppermute | solution.py:19
  79.6 10.3 %copy-start.1 = (f32[2,1024,128]{2,1,0:T(8,128)S(1)}, f32[2,1024,128]{2,1,0:T(8,128)}, u32[]{:S(2)}) copy-start(f32[2,1024,128]{2,1,0:T(8,128)} %get-tuple-element.14) | copy-start | bytes 3145732
  89.9 1.5 %copy-start.5 = (f32[1024,128]{1,0:T(8,128)S(1)}, f32[1024,128]{1,0:T(8,128)}, u32[]{:S(2)}) copy-start(f32[1024,128]{1,0:T(8,128)} %get-tuple-element.18) | copy-start | bytes 1572868
  89.9 1.5 %copy-start.6 = (f32[1024,128]{1,0:T(8,128)S(1)}, f32[1024,128]{1,0:T(8,128)}, u32[]{:S(2)}) copy-start(f32[1024,128]{1,0:T(8,128)} %get-tuple-element.20) | copy-start | bytes 1572868

commit v10 on v9

--- a/solution.py
+++ b/solution.py
@@ -61,50 +61,46 @@
     reach = WINDOW_LENGTH // BLOCK
     dk_ref[...] = jnp.zeros(dk_ref.shape, jnp.float32)
     dv_ref[...] = jnp.zeros(dv_ref.shape, jnp.float32)
-    last = (((0,), (0,)), ((), ()))
+    first = (((0,), (0,)), ((), ()))
     cross = (((1,), (1,)), ((), ()))
-    gap = lax.broadcasted_iota(jnp.int32, (BLOCK, BLOCK), 0) - lax.broadcasted_iota(
-        jnp.int32, (BLOCK, BLOCK), 1
-    )
-    col = lax.broadcasted_iota(jnp.int32, (BLOCK, BLOCK), 1)
+    key_row = lax.broadcasted_iota(jnp.int32, (BLOCK, BLOCK), 0)
+    gap = lax.broadcasted_iota(jnp.int32, (BLOCK, BLOCK), 1) - key_row
     for t in range(tiles):
         rows = slice(t * BLOCK, (t + 1) * BLOCK)
         if halo:
             blocks = [(b, t + b) for b in range(reach - t)]
         else:
             blocks = [(b, t + b - reach) for b in range(reach - t, reach + 1)]
-        starts = ps_ref[rows, :]
+        starts = ps_ref[:, rows]
         for h in range(heads):
             query = q_ref[h, rows, :]
             grad = g_ref[h, rows, :]
-            logsum = lse_ref[h, rows, :]
-            delta = dl_ref[h, rows, :]
+            logsum = lse_ref[h : h + 1, rows]
+            delta = dl_ref[h : h + 1, rows]
             query_acc = jnp.zeros((BLOCK, depth), jnp.float32)
             for b, kb in blocks:
                 keys_at = slice(kb * BLOCK, (kb + 1) * BLOCK)
                 key = k_ref[keys_at, :]
                 value = v_ref[keys_at, :]
                 scores = (
-                    lax.dot_general(query, key, cross, preferred_element_type=jnp.float32)
+                    lax.dot_general(key, query, cross, preferred_element_type=jnp.float32)
                     * score_scale
                 )
                 key_first = kb * BLOCK + (0 if halo else WINDOW_LENGTH)
-                visible = col >= starts - key_first
+                visible = key_row >= starts - key_first
                 if b == 0:
                     visible = visible & (gap < 0)
                 if b == reach:
                     visible = visible & (gap >= 0)
                 probs = jnp.where(visible, jnp.exp(scores - logsum), 0.0)
-                dprobs = lax.dot_general(grad, value, cross, preferred_element_type=jnp.float32)
+                dprobs = lax.dot_general(value, grad, cross, preferred_element_type=jnp.float32)
                 low_scores = (probs * (dprobs - delta)).astype(jnp.bfloat16)
-                query_acc = query_acc + jnp.dot(
-                    low_scores, key, preferred_element_type=jnp.float32
+                query_acc = query_acc + lax.dot_general(
+                    low_scores, key, first, preferred_element_type=jnp.float32
                 )
-                dk_ref[keys_at, :] += lax.dot_general(
-                    low_scores, query, last, preferred_element_type=jnp.float32
-                )
-                dv_ref[keys_at, :] += lax.dot_general(
-                    probs.astype(jnp.bfloat16), grad, last, preferred_element_type=jnp.float32
+                dk_ref[keys_at, :] += jnp.dot(low_scores, query, preferred_element_type=jnp.float32)
+                dv_ref[keys_at, :] += jnp.dot(
+                    probs.astype(jnp.bfloat16), grad, preferred_element_type=jnp.float32
                 )
             dq_ref[h, rows, :] = query_acc
 
@@ -119,7 +115,7 @@
             jax.ShapeDtypeStruct((total, depth), jnp.float32),
             jax.ShapeDtypeStruct((total, depth), jnp.float32),
         ),
-    )(query, grad, logsum[..., None], delta[..., None], start_rel, keys, values)
+    )(query, grad, logsum, delta, start_rel, keys, values)
 
 
 def split_three(x):
@@ -190,7 +186,7 @@
     forward_g = qf_packed[heads_here:]
     delta_g = jnp.einsum("gtd,gtd->gt", forward_g, grad_g, preferred_element_type=jnp.float32)
     base = lax.axis_index("sh") * tokens
-    start_rel = (start_g - base + WINDOW_LENGTH)[:, None]
+    start_rel = (start_g - base + WINDOW_LENGTH)[None, :]
     query_far, key_far, value_far = band_part(
         True, query_g, grad_g, logsum_g, delta_g, start_rel, far[0], far[1]
     )

time: 116 us -> 114 us (0.983)
  local copies, waits for them, and re-layouts: 16.5 us -> 14.4 us
  Pallas kernels: 20.3 us -> 18.7 us
  other arithmetic: 7.24 us -> 8.41 us
    broadcast_in_dim x2 -> x0, local copies, waits for them, and re-layouts: 2.71 us -> none  [the longest x1 1.37 us: band_part(): logsum[..., None]]
    all_to_all x1, waiting for transfers between devices: 10.1 us -> 8.1 us  [on_device(): lax.all_to_all(kv_packed, 'sl', split_axis=0, concat_axis=2, tiled=True)[0]]
    all_to_all x1, waiting for transfers between devices: 5.82 us -> 7.7 us  [on_device(): lax.all_to_all(qf_packed, 'sl', split_axis=0, concat_axis=2, tiled=True)[0]]
    pallas_call x2, Pallas kernels: 20.3 us -> 18.7 us  [band_part(): pl.pallas_call(partial(band_kernel, halo), out_shape=(jax.ShapeDtypeStruc...]
    unnamed x23 -> x22, local copies, waits for them, and re-layouts: 3.09 us -> 3.61 us
  transfers between devices with their start and end apart: 5 -> 5, of which waited for: 3 -> 3; matrix products, arithmetic and copies ran while one was open for 10% -> 9% of each run, Pallas kernels for 9% -> 8%
where the time goes in v10:
time: 114 us; the launch traced here: 113 us
  starting transfers between devices  27.2 us (24%)
  waiting for transfers between devices  23.9 us (21%)
  blocking collectives  19.9 us (17%)
  Pallas kernels  18.7 us (16%)
  local copies, waits for them, and re-layouts  14.4 us (13%)
  other arithmetic  8.41 us (7%)
    all_to_all x1, blocking collectives, to_tokens(): lax.all_to_all(x, ('sl', 'head'), split_axis=0, concat_axis=1, tiled=True)  19.9 us
    pallas_call x2, Pallas kernels, band_part(): pl.pallas_call(partial(band_kernel, halo), out_shape=(jax.ShapeDtypeStruc...  18.7 us
    ppermute x2, starting transfers between devices, shifted(): return lax.ppermute(value, axis, pairs)  15.5 us
    all_to_all x1, waiting for transfers between devices, on_device(): lax.all_to_all(kv_packed, 'sl', split_axis=0, concat_axis=2, tiled=True)[0]  8.1 us
    all_to_all x1, waiting for transfers between devices, on_device(): lax.all_to_all(grad_g, ('sl', 'head'), split_axis=0, concat_axis=2, tiled...  8.09 us
    all_to_all x1, waiting for transfers between devices, on_device(): lax.all_to_all(qf_packed, 'sl', split_axis=0, concat_axis=2, tiled=True)[0]  7.7 us
    all_to_all x1, starting transfers between devices, on_device(): lax.all_to_all(kv_packed, 'sl', split_axis=0, concat_axis=2, tiled=True)[0]  4.59 us
    unnamed x22, local copies, waits for them, and re-layouts  3.61 us
  transfers between devices with their start and end apart: 5, of which 3 were waited for; matrix products, arithmetic and copies ran while one was open for 9% of the time, Pallas kernels for 8%

profile of v10, /device:TPU:4, one launch (start us, length us, event | category | flops | bytes accessed | tf_op | source)
XLA Modules:
  0.0 113.3 jit_solution(15858573598930291115)
XLA Ops:
  0.6 0.0 copy-start.8
  0.6 0.7 reduce-precision_convert_fusion.3
  1.4 0.0 copy-done.8
  1.4 0.0 copy-start.7
  1.4 1.3 %copy.81 = bf16[256,4,128]{0,1,2:T(4,128)(2,1)S(1)} copy(bf16[256,4,128]{2,1,0:T(4,128)(2,1)} %param.8) | data formatting | bytes 524288 | tf_op args[1]
  2.7 0.0 copy-done.7
  2.7 0.2 copy.82
  3.0 0.1 fusion.15
  3.0 0.7 pad_maximum_fusion.2
  3.7 1.0 copy.86
  4.7 0.0 copy-start.2
  4.7 4.6 %all-to-all-start.1 = ((bf16[4,3,256,128]{2,3,1,0:T(8,128)(2,1)}), bf16[4,3,256,128]{2,3,1,0:T(8,128)(2,1)S(1)}, u32[]{:S(2)}, u32[]{:S(2)}) async-start(bf16[4,3,256,128]{2,3,1,0:T(8,128)(2,1)} %copy.86), calls=%async_computation.1 | async-start | bytes 1572864 | tf_op jit(solution)/shard_map/all_to_all | solution.py:165
  9.3 0.0 copy-done.2
  9.3 0.0 copy-start.3
  9.3 0.1 copy.77
  9.4 1.0 copy-done.3
  10.4 0.0 copy-start.4
  10.4 0.1 copy.78
  10.4 1.0 copy-done.4
  11.4 1.0 copy.80
  12.4 1.1 pad_maximum_fusion
  13.5 8.1 %all-to-all-done.1 = bf16[4,3,256,128]{2,3,1,0:T(8,128)(2,1)S(1)} async-done(((bf16[4,3,256,128]{2,3,1,0:T(8,128)(2,1)}), bf16[4,3,256,128]{2,3,1,0:T(8,128)(2,1)S(1)}, u32[]{:S(2)}, u32[]{:S(2)}) %all-to-all-start.1) | async-done | bytes 786464 | tf_op jit(solution)/shard_map/all_to_all | solution.py:165
  21.6 3.5 %all-to-all-start = ((bf16[4,4,256,128]{3,2,1,0:T(8,128)(2,1)}), bf16[4,4,256,128]{3,2,1,0:T(8,128)(2,1)S(1)}, u32[]{:S(2)}, u32[]{:S(2)}) async-start(bf16[4,4,256,128]{3,2,1,0:T(8,128)(2,1)} %pad_maximum_fusion), calls=%async_computation | async-start | bytes 2097152 | tf_op jit(solution)/shard_map/all_to_all | solution.py:184
  25.2 0.4 copy.87
  25.6 1.0 copy.93
  26.6 3.8 %collective-permute-start = (bf16[2,1024,128]{2,1,0:T(8,128)(2,1)}, bf16[2,1024,128]{2,1,0:T(8,128)(2,1)S(1)}, u32[]{:S(2)}, u32[]{:S(2)}) collective-permute-start(bf16[2,1024,128]{2,1,0:T(8,128)(2,1)} %bitcast.34), channel_id=1, source_target_pairs={{0,4},{4,8},{8,12},{12,16},{16,20},{20,24},{24,28},{28,32},{32,36}... | collective-permute-start | bytes 1572872 | tf_op jit(solution)/shard_map/ppermute | solution.py:19
  30.4 0.8 slice_bitcast_fusion.4
  31.3 0.2 copy.89
  31.5 0.1 slice_convert_fusion
  31.6 7.7 %all-to-all-done = bf16[4,4,256,128]{3,2,1,0:T(8,128)(2,1)S(1)} async-done(((bf16[4,4,256,128]{3,2,1,0:T(8,128)(2,1)}), bf16[4,4,256,128]{3,2,1,0:T(8,128)(2,1)S(1)}, u32[]{:S(2)}, u32[]{:S(2)}) %all-to-all-start) | async-done | bytes 1048608 | tf_op jit(solution)/shard_map/all_to_all | solution.py:184
  39.3 3.6 %all-to-all-start.2 = ((bf16[16,2,64,128]{3,2,1,0:T(8,128)(2,1)}), bf16[16,2,64,128]{3,2,1,0:T(8,128)(2,1)S(1)}, u32[]{:S(2)}, u32[]{:S(2)}) async-start(bf16[16,2,64,128]{3,2,1,0:T(8,128)(2,1)} %bitcast.9), calls=%async_computation.2 | async-start | bytes 1048576 | tf_op jit(solution)/shard_map/all_to_all | solution.py:168
  42.9 0.6 fusion.17.lse_ref
  43.5 1.1 fusion.6
  44.6 0.1 copy.127
  44.7 0.9 fusion.23
  45.6 8.1 %all-to-all-done.2 = bf16[16,2,64,128]{3,2,1,0:T(8,128)(2,1)S(1)} async-done(((bf16[16,2,64,128]{3,2,1,0:T(8,128)(2,1)}), bf16[16,2,64,128]{3,2,1,0:T(8,128)(2,1)S(1)}, u32[]{:S(2)}, u32[]{:S(2)}) %all-to-all-start.2) | async-done | bytes 524320 | tf_op jit(solution)/shard_map/all_to_all | solution.py:168
  53.8 0.0 copy-start
  53.8 1.0 fusion.dl_ref
  54.7 0.0 copy-done
  54.7 0.0 collective-permute-done
  54.7 0.8 slice_bitcast_fusion.2
  55.6 9.4 %shard_map.94 = (f32[2,1024,128]{2,1,0:T(8,128)}, f32[1024,128]{1,0:T(8,128)}, f32[1024,128]{1,0:T(8,128)}) custom-call(bf16[2,1024,128]{2,1,0:T(8,128)(2,1)} %bitcast.111, bf16[2,1024,128]{2,1,0:T(8,128)(2,1)} %bitcast.107, f32[2,1024]{1,0:T(2,128)} %fusion.17.lse_ref, f32[2,1024]{1,0:T(2,128)} %fusion.dl_ref, s32[1,1024]{1,0:T(1,128)} %bitcast.129, ...), custom_call_target="tpu_custom_call" | custom-call | tf_op jit(solution)/shard_map/pallas_call | solution.py:111
  65.0 1.3 %convert_bitcast_fusion = (bf16[1,1024,128]{2,1,0:T(8,128)(2,1)S(1)}, bf16[1,1024,128]{2,1,0:T(8,128)(2,1)S(1)}) fusion(f32[1024,128]{1,0:T(8,128)} %get-tuple-element.19, f32[1024,128]{1,0:T(8,128)} %get-tuple-element.15), kind=kLoop, calls=%fused_computation.35 | loop fusion | flops 262144 | bytes 1572864 | tf_op jit(solution)/shard_map/stack | solution.py:193
  66.3 0.1 pad_maximum_fusion.3
  66.3 0.0 copy-start.1
  66.3 11.7 %collective-permute-start.1 = (bf16[2,1024,128]{2,1,0:T(8,128)(2,1)S(1)}, bf16[2,1024,128]{2,1,0:T(8,128)(2,1)S(1)}, u32[]{:S(2)}, u32[]{:S(2)}) collective-permute-start(bf16[2,1024,128]{2,1,0:T(8,128)(2,1)S(1)} %pad_maximum_fusion.3), channel_id=1, source_target_pairs={{4,0},{8,4},{12,8},{16,12},{20,16},{24,20},{28,24},{32,28},{36,32}... | collective-permute-start | bytes 1572872 | tf_op jit(solution)/shard_map/ppermute | solution.py:19
  78.0 9.2 %shard_map.95 = (f32[2,1024,128]{2,1,0:T(8,128)}, f32[1024,128]{1,0:T(8,128)}, f32[1024,128]{1,0:T(8,128)}) custom-call(bf16[2,1024,128]{2,1,0:T(8,128)(2,1)} %bitcast.112, bf16[2,1024,128]{2,1,0:T(8,128)(2,1)} %bitcast.108, f32[2,1024]{1,0:T(2,128)} %fusion.17.lse_ref, f32[2,1024]{1,0:T(2,128)} %fusion.dl_ref, s32[1,1024]{1,0:T(1,128)} %bitcast.130, ...), custom_call_target="tpu_custom_call" | custom-call | tf_op jit(solution)/shard_map/pallas_call | solution.py:111
  87.2 0.0 copy-done.1
  87.2 0.0 copy-start.5
  87.2 0.0 copy-start.6
  87.2 1.5 %fusion.1 = bf16[1024,2,128]{2,0,1:T(8,128)(2,1)S(1)} fusion(f32[2,1024,128]{2,1,0:T(8,128)S(1)} %copy-done.1, f32[2,1024,128]{2,1,0:T(8,128)} %get-tuple-element.17), kind=kLoop, calls=%fused_computation.8 | loop fusion | flops 786432 | bytes 2621440 | tf_op jit(solution)/shard_map/convert_element_type | solution.py:208
  88.7 0.0 collective-permute-done.1
  88.7 0.0 copy-done.5
  88.7 0.0 copy-done.6
  88.8 0.1 fusion.12
  88.9 0.1 pad_maximum_fusion.1
  89.0 0.8 copy.94
  89.8 19.9 %all_to_all.60 = bf16[1024,4,128]{2,1,0:T(4,128)(2,1)S(1)} all-to-all(bf16[1024,4,128]{2,1,0:T(4,128)(2,1)S(1)} %copy.94), channel_id=1, replica_groups=mesh['head'=4,'sh'=32,'sl'=4] {'sl','head'}, dimensions={0} | all-to-all | bytes 2097152 | tf_op jit(solution)/shard_map/all_to_all | solution.py:202
  109.7 0.8 copy.126
  110.6 0.2 slice.111
  110.8 1.0 fusion.22
  111.7 1.6 %copy.96 = bf16[64,4,4,2,128]{4,3,2,1,0:T(2,128)(2,1)} copy(bf16[64,4,4,2,128]{4,2,1,0,3:T(4,128)(2,1)S(1)} %slice.111) | data formatting | bytes 1048576 | tf_op jit(solution)/shard_map/slice | solution.py:213
  (13 shorter events, 0.2 us)
Async XLA Ops:
  0.6 0.7 copy-start.8
  1.4 1.3 %copy-start.7 = (bf16[256,4,128]{2,1,0:T(4,128)(2,1)S(1)}, bf16[256,4,128]{2,1,0:T(4,128)(2,1)}, u32[]{:S(2)}) copy-start(bf16[256,4,128]{2,1,0:T(4,128)(2,1)} %param.9) | copy-start | bytes 786436
  4.7 4.6 %copy-start.2 = (bf16[256,8,128]{2,1,0:T(8,128)(2,1)S(1)}, bf16[256,8,128]{2,1,0:T(8,128)(2,1)}, u32[]{:S(2)}) copy-start(bf16[256,8,128]{2,1,0:T(8,128)(2,1)} %param.7) | copy-start | bytes 1572868
  4.7 16.9 %all-to-all-start.1 = ((bf16[4,3,256,128]{2,3,1,0:T(8,128)(2,1)}), bf16[4,3,256,128]{2,3,1,0:T(8,128)(2,1)S(1)}, u32[]{:S(2)}, u32[]{:S(2)}) async-start(bf16[4,3,256,128]{2,3,1,0:T(8,128)(2,1)} %copy.86), calls=%async_computation.1 | async-start | bytes 1572864 | tf_op jit(solution)/shard_map/all_to_all | solution.py:165
  9.3 1.0 copy-start.3
  10.4 1.0 copy-start.4
  21.6 17.7 %all-to-all-start = ((bf16[4,4,256,128]{3,2,1,0:T(8,128)(2,1)}), bf16[4,4,256,128]{3,2,1,0:T(8,128)(2,1)S(1)}, u32[]{:S(2)}, u32[]{:S(2)}) async-start(bf16[4,4,256,128]{3,2,1,0:T(8,128)(2,1)} %pad_maximum_fusion), calls=%async_computation | async-start | bytes 2097152 | tf_op jit(solution)/shard_map/all_to_all | solution.py:184
  26.6 28.2 %collective-permute-start = (bf16[2,1024,128]{2,1,0:T(8,128)(2,1)}, bf16[2,1024,128]{2,1,0:T(8,128)(2,1)S(1)}, u32[]{:S(2)}, u32[]{:S(2)}) collective-permute-start(bf16[2,1024,128]{2,1,0:T(8,128)(2,1)} %bitcast.34), channel_id=1, source_target_pairs={{0,4},{4,8},{8,12},{12,16},{16,20},{20,24},{24,28},{28,32},{32,36}... | collective-permute-start | bytes 1572872 | tf_op jit(solution)/shard_map/ppermute | solution.py:19
  39.3 14.4 %all-to-all-start.2 = ((bf16[16,2,64,128]{3,2,1,0:T(8,128)(2,1)}), bf16[16,2,64,128]{3,2,1,0:T(8,128)(2,1)S(1)}, u32[]{:S(2)}, u32[]{:S(2)}) async-start(bf16[16,2,64,128]{3,2,1,0:T(8,128)(2,1)} %bitcast.9), calls=%async_computation.2 | async-start | bytes 1048576 | tf_op jit(solution)/shard_map/all_to_all | solution.py:168
  53.8 1.0 copy-start
  66.3 20.9 %copy-start.1 = (f32[2,1024,128]{2,1,0:T(8,128)S(1)}, f32[2,1024,128]{2,1,0:T(8,128)}, u32[]{:S(2)}) copy-start(f32[2,1024,128]{2,1,0:T(8,128)} %get-tuple-element.14) | copy-start | bytes 3145732
  66.3 22.4 %collective-permute-start.1 = (bf16[2,1024,128]{2,1,0:T(8,128)(2,1)S(1)}, bf16[2,1024,128]{2,1,0:T(8,128)(2,1)S(1)}, u32[]{:S(2)}, u32[]{:S(2)}) collective-permute-start(bf16[2,1024,128]{2,1,0:T(8,128)(2,1)S(1)} %pad_maximum_fusion.3), channel_id=1, source_target_pairs={{4,0},{8,4},{12,8},{16,12},{20,16},{24,20},{28,24},{32,28},{36,32}... | collective-permute-start | bytes 1572872 | tf_op jit(solution)/shard_map/ppermute | solution.py:19
  87.2 1.5 %copy-start.5 = (f32[1024,128]{1,0:T(8,128)S(1)}, f32[1024,128]{1,0:T(8,128)}, u32[]{:S(2)}) copy-start(f32[1024,128]{1,0:T(8,128)} %get-tuple-element.18) | copy-start | bytes 1572868
  87.2 1.5 %copy-start.6 = (f32[1024,128]{1,0:T(8,128)S(1)}, f32[1024,128]{1,0:T(8,128)}, u32[]{:S(2)}) copy-start(f32[1024,128]{1,0:T(8,128)} %get-tuple-element.20) | copy-start | bytes 1572868

commit v11 on v10

--- a/solution.py
+++ b/solution.py
@@ -63,46 +63,47 @@
     dv_ref[...] = jnp.zeros(dv_ref.shape, jnp.float32)
     first = (((0,), (0,)), ((), ()))
     cross = (((1,), (1,)), ((), ()))
-    key_row = lax.broadcasted_iota(jnp.int32, (BLOCK, BLOCK), 0)
-    gap = lax.broadcasted_iota(jnp.int32, (BLOCK, BLOCK), 1) - key_row
+    width = heads * BLOCK
+    key_row = lax.broadcasted_iota(jnp.int32, (BLOCK, width), 0)
+    gap = lax.broadcasted_iota(jnp.int32, (BLOCK, width), 1) % BLOCK - key_row
     for t in range(tiles):
         rows = slice(t * BLOCK, (t + 1) * BLOCK)
         if halo:
             blocks = [(b, t + b) for b in range(reach - t)]
         else:
             blocks = [(b, t + b - reach) for b in range(reach - t, reach + 1)]
-        starts = ps_ref[:, rows]
+        starts = jnp.concatenate([ps_ref[:, rows]] * heads, axis=1)
+        query = jnp.concatenate([q_ref[h, rows, :] for h in range(heads)], axis=0)
+        grad = jnp.concatenate([g_ref[h, rows, :] for h in range(heads)], axis=0)
+        logsum = jnp.concatenate([lse_ref[h : h + 1, rows] for h in range(heads)], axis=1)
+        delta = jnp.concatenate([dl_ref[h : h + 1, rows] for h in range(heads)], axis=1)
+        query_acc = jnp.zeros((width, depth), jnp.float32)
+        for b, kb in blocks:
+            keys_at = slice(kb * BLOCK, (kb + 1) * BLOCK)
+            key = k_ref[keys_at, :]
+            value = v_ref[keys_at, :]
+            scores = (
+                lax.dot_general(key, query, cross, preferred_element_type=jnp.float32)
+                * score_scale
+            )
+            key_first = kb * BLOCK + (0 if halo else WINDOW_LENGTH)
+            visible = key_row >= starts - key_first
+            if b == 0:
+                visible = visible & (gap < 0)
+            if b == reach:
+                visible = visible & (gap >= 0)
+            probs = jnp.where(visible, jnp.exp(scores - logsum), 0.0)
+            dprobs = lax.dot_general(value, grad, cross, preferred_element_type=jnp.float32)
+            low_scores = (probs * (dprobs - delta)).astype(jnp.bfloat16)
+            query_acc = query_acc + lax.dot_general(
+                low_scores, key, first, preferred_element_type=jnp.float32
+            )
+            dk_ref[keys_at, :] += jnp.dot(low_scores, query, preferred_element_type=jnp.float32)
+            dv_ref[keys_at, :] += jnp.dot(
+                probs.astype(jnp.bfloat16), grad, preferred_element_type=jnp.float32
+            )
         for h in range(heads):
-            query = q_ref[h, rows, :]
-            grad = g_ref[h, rows, :]
-            logsum = lse_ref[h : h + 1, rows]
-            delta = dl_ref[h : h + 1, rows]
-            query_acc = jnp.zeros((BLOCK, depth), jnp.float32)
-            for b, kb in blocks:
-                keys_at = slice(kb * BLOCK, (kb + 1) * BLOCK)
-                key = k_ref[keys_at, :]
-                value = v_ref[keys_at, :]
-                scores = (
-                    lax.dot_general(key, query, cross, preferred_element_type=jnp.float32)
-                    * score_scale
-                )
-                key_first = kb * BLOCK + (0 if halo else WINDOW_LENGTH)
-                visible = key_row >= starts - key_first
-                if b == 0:
-                    visible = visible & (gap < 0)
-                if b == reach:
-                    visible = visible & (gap >= 0)
-                probs = jnp.where(visible, jnp.exp(scores - logsum), 0.0)
-                dprobs = lax.dot_general(value, grad, cross, preferred_element_type=jnp.float32)
-                low_scores = (probs * (dprobs - delta)).astype(jnp.bfloat16)
-                query_acc = query_acc + lax.dot_general(
-                    low_scores, key, first, preferred_element_type=jnp.float32
-                )
-                dk_ref[keys_at, :] += jnp.dot(low_scores, query, preferred_element_type=jnp.float32)
-                dv_ref[keys_at, :] += jnp.dot(
-                    probs.astype(jnp.bfloat16), grad, preferred_element_type=jnp.float32
-                )
-            dq_ref[h, rows, :] = query_acc
+            dq_ref[h, rows, :] = query_acc[h * BLOCK : (h + 1) * BLOCK]
 
 
 def band_part(halo, query, grad, logsum, delta, start_rel, keys, values):

time: 114 us -> 112 us (0.982)
  Pallas kernels: 18.7 us -> 15.3 us
  waiting for transfers between devices: 23.9 us -> 25.2 us
    pallas_call x2, Pallas kernels: 18.7 us -> 15.3 us  [band_part(): pl.pallas_call(partial(band_kernel, halo), out_shape=(jax.ShapeDtypeStruc...]
    ppermute x2, waiting for transfers between devices: 0.01 us -> 1.3 us  [shifted(): return lax.ppermute(value, axis, pairs)]
  transfers between devices with their start and end apart: 5 -> 5, of which waited for: 3 -> 4; matrix products, arithmetic and copies ran while one was open for 9% -> 9% of each run, Pallas kernels for 8% -> 7%
where the time goes in v11:
time: 112 us
  starting transfers between devices  27.2 us (24%)
  waiting for transfers between devices  25.2 us (22%)
  blocking collectives  20.3 us (18%)
  Pallas kernels  15.3 us (14%)
  local copies, waits for them, and re-layouts  14.3 us (13%)
  other arithmetic  8.41 us (8%)
    all_to_all x1, blocking collectives, to_tokens(): lax.all_to_all(x, ('sl', 'head'), split_axis=0, concat_axis=1, tiled=True)  20.3 us
    ppermute x2, starting transfers between devices, shifted(): return lax.ppermute(value, axis, pairs)  15.5 us
    pallas_call x2, Pallas kernels, band_part(): pl.pallas_call(partial(band_kernel, halo), out_shape=(jax.ShapeDtypeStruc...  15.3 us
    all_to_all x1, waiting for transfers between devices, on_device(): lax.all_to_all(kv_packed, 'sl', split_axis=0, concat_axis=2, tiled=True)[0]  8.1 us
    all_to_all x1, waiting for transfers between devices, on_device(): lax.all_to_all(grad_g, ('sl', 'head'), split_axis=0, concat_axis=2, tiled...  8.09 us
    all_to_all x1, waiting for transfers between devices, on_device(): lax.all_to_all(qf_packed, 'sl', split_axis=0, concat_axis=2, tiled=True)[0]  7.7 us
    all_to_all x1, starting transfers between devices, on_device(): lax.all_to_all(kv_packed, 'sl', split_axis=0, concat_axis=2, tiled=True)[0]  4.59 us
    unnamed x22, local copies, waits for them, and re-layouts  3.58 us
  transfers between devices with their start and end apart: 5, of which 4 were waited for; matrix products, arithmetic and copies ran while one was open for 9% of the time, Pallas kernels for 7%

profile of v11, /device:TPU:4, one launch (start us, length us, event | category | flops | bytes accessed | tf_op | source)
XLA Modules:
  0.0 111.6 jit_solution(16773663199340288482)
XLA Ops:
  0.6 0.0 copy-start.8
  0.6 0.7 reduce-precision_convert_fusion.3
  1.4 0.0 copy-done.8
  1.4 0.0 copy-start.7
  1.4 1.3 %copy.81 = bf16[256,4,128]{0,1,2:T(4,128)(2,1)S(1)} copy(bf16[256,4,128]{2,1,0:T(4,128)(2,1)} %param.8) | data formatting | bytes 524288 | tf_op args[1]
  2.7 0.0 copy-done.7
  2.7 0.2 copy.82
  3.0 0.1 fusion.15
  3.0 0.7 pad_maximum_fusion.2
  3.7 1.0 copy.86
  4.7 0.0 copy-start.2
  4.7 4.6 %all-to-all-start.1 = ((bf16[4,3,256,128]{2,3,1,0:T(8,128)(2,1)}), bf16[4,3,256,128]{2,3,1,0:T(8,128)(2,1)S(1)}, u32[]{:S(2)}, u32[]{:S(2)}) async-start(bf16[4,3,256,128]{2,3,1,0:T(8,128)(2,1)} %copy.86), calls=%async_computation.1 | async-start | bytes 1572864 | tf_op jit(solution)/shard_map/all_to_all | solution.py:166
  9.3 0.0 copy-done.2
  9.3 0.0 copy-start.3
  9.3 0.1 copy.77
  9.4 1.0 copy-done.3
  10.4 0.0 copy-start.4
  10.4 0.1 copy.78
  10.4 1.0 copy-done.4
  11.4 1.0 copy.80
  12.4 1.1 pad_maximum_fusion
  13.5 8.1 %all-to-all-done.1 = bf16[4,3,256,128]{2,3,1,0:T(8,128)(2,1)S(1)} async-done(((bf16[4,3,256,128]{2,3,1,0:T(8,128)(2,1)}), bf16[4,3,256,128]{2,3,1,0:T(8,128)(2,1)S(1)}, u32[]{:S(2)}, u32[]{:S(2)}) %all-to-all-start.1) | async-done | bytes 786464 | tf_op jit(solution)/shard_map/all_to_all | solution.py:166
  21.6 3.5 %all-to-all-start = ((bf16[4,4,256,128]{3,2,1,0:T(8,128)(2,1)}), bf16[4,4,256,128]{3,2,1,0:T(8,128)(2,1)S(1)}, u32[]{:S(2)}, u32[]{:S(2)}) async-start(bf16[4,4,256,128]{3,2,1,0:T(8,128)(2,1)} %pad_maximum_fusion), calls=%async_computation | async-start | bytes 2097152 | tf_op jit(solution)/shard_map/all_to_all | solution.py:185
  25.2 0.4 copy.87
  25.6 1.0 copy.93
  26.6 3.8 %collective-permute-start = (bf16[2,1024,128]{2,1,0:T(8,128)(2,1)}, bf16[2,1024,128]{2,1,0:T(8,128)(2,1)S(1)}, u32[]{:S(2)}, u32[]{:S(2)}) collective-permute-start(bf16[2,1024,128]{2,1,0:T(8,128)(2,1)} %bitcast.34), channel_id=1, source_target_pairs={{0,4},{4,8},{8,12},{12,16},{16,20},{20,24},{24,28},{28,32},{32,36}... | collective-permute-start | bytes 1572872 | tf_op jit(solution)/shard_map/ppermute | solution.py:19
  30.4 0.8 slice_bitcast_fusion.4
  31.3 0.2 copy.89
  31.5 0.1 slice_convert_fusion
  31.6 7.7 %all-to-all-done = bf16[4,4,256,128]{3,2,1,0:T(8,128)(2,1)S(1)} async-done(((bf16[4,4,256,128]{3,2,1,0:T(8,128)(2,1)}), bf16[4,4,256,128]{3,2,1,0:T(8,128)(2,1)S(1)}, u32[]{:S(2)}, u32[]{:S(2)}) %all-to-all-start) | async-done | bytes 1048608 | tf_op jit(solution)/shard_map/all_to_all | solution.py:185
  39.3 3.6 %all-to-all-start.2 = ((bf16[16,2,64,128]{3,2,1,0:T(8,128)(2,1)}), bf16[16,2,64,128]{3,2,1,0:T(8,128)(2,1)S(1)}, u32[]{:S(2)}, u32[]{:S(2)}) async-start(bf16[16,2,64,128]{3,2,1,0:T(8,128)(2,1)} %bitcast.9), calls=%async_computation.2 | async-start | bytes 1048576 | tf_op jit(solution)/shard_map/all_to_all | solution.py:169
  42.9 0.6 fusion.17.lse_ref
  43.5 1.1 %fusion.6 = s32[1024]{0:T(1024)} fusion(f32[1024,3]{1,0:T(8,128)S(1)} %slice_convert_fusion, s32[]{:T(128)S(6)} %mul.16), kind=kLoop, calls=%fused_computation.14 | loop fusion | flops 6144 | bytes 16388 | tf_op jit(solution)/shard_map/add | solution.py:190
  44.6 0.1 copy.127
  44.7 0.9 fusion.23
  45.6 8.1 %all-to-all-done.2 = bf16[16,2,64,128]{3,2,1,0:T(8,128)(2,1)S(1)} async-done(((bf16[16,2,64,128]{3,2,1,0:T(8,128)(2,1)}), bf16[16,2,64,128]{3,2,1,0:T(8,128)(2,1)S(1)}, u32[]{:S(2)}, u32[]{:S(2)}) %all-to-all-start.2) | async-done | bytes 524320 | tf_op jit(solution)/shard_map/all_to_all | solution.py:169
  53.8 0.0 copy-start
  53.8 1.0 fusion.dl_ref
  54.7 0.0 copy-done
  54.7 0.0 collective-permute-done
  54.7 0.8 slice_bitcast_fusion.2
  55.6 7.7 %shard_map.94 = (f32[2,1024,128]{2,1,0:T(8,128)}, f32[1024,128]{1,0:T(8,128)}, f32[1024,128]{1,0:T(8,128)}) custom-call(bf16[2,1024,128]{2,1,0:T(8,128)(2,1)} %bitcast.111, bf16[2,1024,128]{2,1,0:T(8,128)(2,1)} %bitcast.107, f32[2,1024]{1,0:T(2,128)} %fusion.17.lse_ref, f32[2,1024]{1,0:T(2,128)} %fusion.dl_ref, s32[1,1024]{1,0:T(1,128)} %bitcast.129, ...), custom_call_target="tpu_custom_call" | custom-call | tf_op jit(solution)/shard_map/pallas_call | solution.py:112
  63.2 1.3 %convert_bitcast_fusion = (bf16[1,1024,128]{2,1,0:T(8,128)(2,1)S(1)}, bf16[1,1024,128]{2,1,0:T(8,128)(2,1)S(1)}) fusion(f32[1024,128]{1,0:T(8,128)} %get-tuple-element.19, f32[1024,128]{1,0:T(8,128)} %get-tuple-element.15), kind=kLoop, calls=%fused_computation.35 | loop fusion | flops 262144 | bytes 1572864 | tf_op jit(solution)/shard_map/stack | solution.py:194
  64.5 0.1 pad_maximum_fusion.3
  64.6 0.0 copy-start.1
  64.6 11.7 %collective-permute-start.1 = (bf16[2,1024,128]{2,1,0:T(8,128)(2,1)S(1)}, bf16[2,1024,128]{2,1,0:T(8,128)(2,1)S(1)}, u32[]{:S(2)}, u32[]{:S(2)}) collective-permute-start(bf16[2,1024,128]{2,1,0:T(8,128)(2,1)S(1)} %pad_maximum_fusion.3), channel_id=1, source_target_pairs={{4,0},{8,4},{12,8},{16,12},{20,16},{24,20},{28,24},{32,28},{36,32}... | collective-permute-start | bytes 1572872 | tf_op jit(solution)/shard_map/ppermute | solution.py:19
  76.3 7.6 %shard_map.95 = (f32[2,1024,128]{2,1,0:T(8,128)}, f32[1024,128]{1,0:T(8,128)}, f32[1024,128]{1,0:T(8,128)}) custom-call(bf16[2,1024,128]{2,1,0:T(8,128)(2,1)} %bitcast.112, bf16[2,1024,128]{2,1,0:T(8,128)(2,1)} %bitcast.108, f32[2,1024]{1,0:T(2,128)} %fusion.17.lse_ref, f32[2,1024]{1,0:T(2,128)} %fusion.dl_ref, s32[1,1024]{1,0:T(1,128)} %bitcast.130, ...), custom_call_target="tpu_custom_call" | custom-call | tf_op jit(solution)/shard_map/pallas_call | solution.py:112
  83.9 0.0 copy-done.1
  83.9 0.0 copy-start.5
  83.9 0.0 copy-start.6
  83.9 1.5 %fusion.1 = bf16[1024,2,128]{2,0,1:T(8,128)(2,1)S(1)} fusion(f32[2,1024,128]{2,1,0:T(8,128)S(1)} %copy-done.1, f32[2,1024,128]{2,1,0:T(8,128)} %get-tuple-element.17), kind=kLoop, calls=%fused_computation.8 | loop fusion | flops 786432 | bytes 2621440 | tf_op jit(solution)/shard_map/convert_element_type | solution.py:209
  85.4 1.3 %collective-permute-done.1 = bf16[2,1024,128]{2,1,0:T(8,128)(2,1)S(1)} collective-permute-done((bf16[2,1024,128]{2,1,0:T(8,128)(2,1)S(1)}, bf16[2,1024,128]{2,1,0:T(8,128)(2,1)S(1)}, u32[]{:S(2)}, u32[]{:S(2)}) %collective-permute-start.1) | collective-permute-done | bytes 524320 | tf_op jit(solution)/shard_map/ppermute | solution.py:19
  86.7 0.0 copy-done.5
  86.7 0.0 copy-done.6
  86.7 0.1 fusion.12
  86.8 0.1 pad_maximum_fusion.1
  86.9 0.8 copy.94
  87.7 20.3 %all_to_all.60 = bf16[1024,4,128]{2,1,0:T(4,128)(2,1)S(1)} all-to-all(bf16[1024,4,128]{2,1,0:T(4,128)(2,1)S(1)} %copy.94), channel_id=1, replica_groups=mesh['head'=4,'sh'=32,'sl'=4] {'sl','head'}, dimensions={0} | all-to-all | bytes 2097152 | tf_op jit(solution)/shard_map/all_to_all | solution.py:203
  108.0 0.8 copy.126
  108.8 0.2 slice.111
  109.0 1.0 fusion.22
  110.0 1.6 %copy.96 = bf16[64,4,4,2,128]{4,3,2,1,0:T(2,128)(2,1)} copy(bf16[64,4,4,2,128]{4,2,1,0,3:T(4,128)(2,1)S(1)} %slice.111) | data formatting | bytes 1048576 | tf_op jit(solution)/shard_map/slice | solution.py:214
  (13 shorter events, 0.2 us)
Async XLA Ops:
  0.6 0.7 copy-start.8
  1.4 1.3 %copy-start.7 = (bf16[256,4,128]{2,1,0:T(4,128)(2,1)S(1)}, bf16[256,4,128]{2,1,0:T(4,128)(2,1)}, u32[]{:S(2)}) copy-start(bf16[256,4,128]{2,1,0:T(4,128)(2,1)} %param.9) | copy-start | bytes 786436
  4.7 4.6 %copy-start.2 = (bf16[256,8,128]{2,1,0:T(8,128)(2,1)S(1)}, bf16[256,8,128]{2,1,0:T(8,128)(2,1)}, u32[]{:S(2)}) copy-start(bf16[256,8,128]{2,1,0:T(8,128)(2,1)} %param.7) | copy-start | bytes 1572868
  4.7 16.9 %all-to-all-start.1 = ((bf16[4,3,256,128]{2,3,1,0:T(8,128)(2,1)}), bf16[4,3,256,128]{2,3,1,0:T(8,128)(2,1)S(1)}, u32[]{:S(2)}, u32[]{:S(2)}) async-start(bf16[4,3,256,128]{2,3,1,0:T(8,128)(2,1)} %copy.86), calls=%async_computation.1 | async-start | bytes 1572864 | tf_op jit(solution)/shard_map/all_to_all | solution.py:166
  9.3 1.0 copy-start.3
  10.4 1.0 copy-start.4
  21.6 17.7 %all-to-all-start = ((bf16[4,4,256,128]{3,2,1,0:T(8,128)(2,1)}), bf16[4,4,256,128]{3,2,1,0:T(8,128)(2,1)S(1)}, u32[]{:S(2)}, u32[]{:S(2)}) async-start(bf16[4,4,256,128]{3,2,1,0:T(8,128)(2,1)} %pad_maximum_fusion), calls=%async_computation | async-start | bytes 2097152 | tf_op jit(solution)/shard_map/all_to_all | solution.py:185
  26.6 28.2 %collective-permute-start = (bf16[2,1024,128]{2,1,0:T(8,128)(2,1)}, bf16[2,1024,128]{2,1,0:T(8,128)(2,1)S(1)}, u32[]{:S(2)}, u32[]{:S(2)}) collective-permute-start(bf16[2,1024,128]{2,1,0:T(8,128)(2,1)} %bitcast.34), channel_id=1, source_target_pairs={{0,4},{4,8},{8,12},{12,16},{16,20},{20,24},{24,28},{28,32},{32,36}... | collective-permute-start | bytes 1572872 | tf_op jit(solution)/shard_map/ppermute | solution.py:19
  39.3 14.4 %all-to-all-start.2 = ((bf16[16,2,64,128]{3,2,1,0:T(8,128)(2,1)}), bf16[16,2,64,128]{3,2,1,0:T(8,128)(2,1)S(1)}, u32[]{:S(2)}, u32[]{:S(2)}) async-start(bf16[16,2,64,128]{3,2,1,0:T(8,128)(2,1)} %bitcast.9), calls=%async_computation.2 | async-start | bytes 1048576 | tf_op jit(solution)/shard_map/all_to_all | solution.py:169
  53.8 1.0 copy-start
  64.6 19.3 %copy-start.1 = (f32[2,1024,128]{2,1,0:T(8,128)S(1)}, f32[2,1024,128]{2,1,0:T(8,128)}, u32[]{:S(2)}) copy-start(f32[2,1024,128]{2,1,0:T(8,128)} %get-tuple-element.14) | copy-start | bytes 3145732
  64.6 22.1 %collective-permute-start.1 = (bf16[2,1024,128]{2,1,0:T(8,128)(2,1)S(1)}, bf16[2,1024,128]{2,1,0:T(8,128)(2,1)S(1)}, u32[]{:S(2)}, u32[]{:S(2)}) collective-permute-start(bf16[2,1024,128]{2,1,0:T(8,128)(2,1)S(1)} %pad_maximum_fusion.3), channel_id=1, source_target_pairs={{4,0},{8,4},{12,8},{16,12},{20,16},{24,20},{28,24},{32,28},{36,32}... | collective-permute-start | bytes 1572872 | tf_op jit(solution)/shard_map/ppermute | solution.py:19
  83.9 2.8 %copy-start.5 = (f32[1024,128]{1,0:T(8,128)S(1)}, f32[1024,128]{1,0:T(8,128)}, u32[]{:S(2)}) copy-start(f32[1024,128]{1,0:T(8,128)} %get-tuple-element.18) | copy-start | bytes 1572868
  83.9 2.8 %copy-start.6 = (f32[1024,128]{1,0:T(8,128)S(1)}, f32[1024,128]{1,0:T(8,128)}, u32[]{:S(2)}) copy-start(f32[1024,128]{1,0:T(8,128)} %get-tuple-element.20) | copy-start | bytes 1572868

commit v12 on v11

--- a/solution.py
+++ b/solution.py
@@ -4,6 +4,7 @@
 import jax.numpy as jnp
 from jax import lax
 from jax.experimental import pallas as pl
+from jax.experimental.pallas import tpu as pltpu
 from jax.sharding import Mesh
 from jax.sharding import PartitionSpec as P
 
@@ -55,10 +56,14 @@
     return query_term.reshape(tokens, group, depth), key_term, value_term
 
 
-def band_kernel(halo, q_ref, g_ref, lse_ref, dl_ref, ps_ref, k_ref, v_ref, dq_ref, dk_ref, dv_ref):
+def band_kernel(halo, q_ref, g_ref, lse_ref, dl_ref, ps_ref, k_ref, v_ref, dq_ref, *rest):
     heads, tokens, depth = q_ref.shape
     tiles = tokens // BLOCK
     reach = WINDOW_LENGTH // BLOCK
+    if halo:
+        low_ref, dk_ref, dv_ref = rest
+    else:
+        dk_ref, dv_ref = rest
     dk_ref[...] = jnp.zeros(dk_ref.shape, jnp.float32)
     dv_ref[...] = jnp.zeros(dv_ref.shape, jnp.float32)
     first = (((0,), (0,)), ((), ()))
@@ -104,18 +109,27 @@
             )
         for h in range(heads):
             dq_ref[h, rows, :] = query_acc[h * BLOCK : (h + 1) * BLOCK]
+    if halo:
+        low_ref[0] = dk_ref[...].astype(jnp.bfloat16)
+        low_ref[1] = dv_ref[...].astype(jnp.bfloat16)
 
 
 def band_part(halo, query, grad, logsum, delta, start_rel, keys, values):
     group, tokens, depth = query.shape
     total = keys.shape[0]
+    sums = (
+        jax.ShapeDtypeStruct((total, depth), jnp.float32),
+        jax.ShapeDtypeStruct((total, depth), jnp.float32),
+    )
+    dq = jax.ShapeDtypeStruct((group, tokens, depth), jnp.float32)
+    if halo:
+        outs = (dq, jax.ShapeDtypeStruct((2, total, depth), jnp.bfloat16))
+        scratch = [pltpu.VMEM((total, depth), jnp.float32)] * 2
+    else:
+        outs = (dq,) + sums
+        scratch = []
     return pl.pallas_call(
-        partial(band_kernel, halo),
-        out_shape=(
-            jax.ShapeDtypeStruct((group, tokens, depth), jnp.float32),
-            jax.ShapeDtypeStruct((total, depth), jnp.float32),
-            jax.ShapeDtypeStruct((total, depth), jnp.float32),
-        ),
+        partial(band_kernel, halo), out_shape=outs, scratch_shapes=scratch
     )(query, grad, logsum, delta, start_rel, keys, values)
 
 
@@ -188,10 +202,10 @@
     delta_g = jnp.einsum("gtd,gtd->gt", forward_g, grad_g, preferred_element_type=jnp.float32)
     base = lax.axis_index("sh") * tokens
     start_rel = (start_g - base + WINDOW_LENGTH)[None, :]
-    query_far, key_far, value_far = band_part(
+    query_far, key_far = band_part(
         True, query_g, grad_g, logsum_g, delta_g, start_rel, far[0], far[1]
     )
-    back = shifted(jnp.stack([key_far, value_far]).astype(jnp.bfloat16), "sh", -1)
+    back = shifted(key_far, "sh", -1)
     query_g, key_far = lax.optimization_barrier((query_g, key_far))
     query_own, key_sum, value_sum = band_part(
         False, query_g, grad_g, logsum_g, delta_g, start_rel, key_own, value_own

time: 112 us -> 111 us (level)
  other arithmetic: 8.41 us -> 7.08 us
    another operation x3 -> x1, other arithmetic: 2.01 us -> 0.69 us  [the longest x2 1.32 us: on_device(): jnp.stack([key_far, value_far]).astype(jnp.bfloat16)]
where the time goes in v12:
time: 111 us; the launch traced here: 110 us
  starting transfers between devices  27.1 us (24%)
  waiting for transfers between devices  25.5 us (23%)
  blocking collectives  20.3 us (18%)
  Pallas kernels  15.2 us (14%)
  local copies, waits for them, and re-layouts  14.3 us (13%)
  other arithmetic  7.08 us (6%)
    all_to_all x1, blocking collectives, to_tokens(): lax.all_to_all(x, ('sl', 'head'), split_axis=0, concat_axis=1, tiled=True)  20.3 us
    ppermute x2, starting transfers between devices, shifted(): return lax.ppermute(value, axis, pairs)  15.5 us
    pallas_call x2, Pallas kernels, band_part(): pl.pallas_call(partial(band_kernel, halo), out_shape=outs, scratch_shapes...  15.2 us
    all_to_all x1, waiting for transfers between devices, on_device(): lax.all_to_all(kv_packed, 'sl', split_axis=0, concat_axis=2, tiled=True)[0]  8.12 us
    all_to_all x1, waiting for transfers between devices, on_device(): lax.all_to_all(grad_g, ('sl', 'head'), split_axis=0, concat_axis=2, tiled...  8.09 us
    all_to_all x1, waiting for transfers between devices, on_device(): lax.all_to_all(qf_packed, 'sl', split_axis=0, concat_axis=2, tiled=True)[0]  7.69 us
    all_to_all x1, starting transfers between devices, on_device(): lax.all_to_all(kv_packed, 'sl', split_axis=0, concat_axis=2, tiled=True)[0]  4.59 us
    unnamed x22, local copies, waits for them, and re-layouts  3.58 us
  transfers between devices with their start and end apart: 5, of which 4 were waited for; matrix products, arithmetic and copies ran while one was open for 9% of the time, Pallas kernels for 7%

profile of v12, /device:TPU:4, one launch (start us, length us, event | category | flops | bytes accessed | tf_op | source)
XLA Modules:
  0.0 110.4 jit_solution(8929143939307384168)
XLA Ops:
  0.6 0.0 copy-start.8
  0.6 0.7 reduce-precision_convert_fusion.3
  1.4 0.0 copy-done.8
  1.4 0.0 copy-start.7
  1.4 1.3 %copy.81 = bf16[256,4,128]{0,1,2:T(4,128)(2,1)S(1)} copy(bf16[256,4,128]{2,1,0:T(4,128)(2,1)} %param.8) | data formatting | bytes 524288 | tf_op args[1]
  2.7 0.0 copy-done.7
  2.7 0.2 copy.82
  3.0 0.1 fusion.15
  3.0 0.7 pad_maximum_fusion.2
  3.7 1.0 copy.86
  4.7 0.0 copy-start.2
  4.7 4.6 %all-to-all-start.1 = ((bf16[4,3,256,128]{2,3,1,0:T(8,128)(2,1)}), bf16[4,3,256,128]{2,3,1,0:T(8,128)(2,1)S(1)}, u32[]{:S(2)}, u32[]{:S(2)}) async-start(bf16[4,3,256,128]{2,3,1,0:T(8,128)(2,1)} %copy.86), calls=%async_computation.1 | async-start | bytes 1572864 | tf_op jit(solution)/shard_map/all_to_all | solution.py:180
  9.3 0.0 copy-done.2
  9.3 0.0 copy-start.3
  9.3 0.1 copy.77
  9.4 1.0 copy-done.3
  10.4 0.0 copy-start.4
  10.4 0.1 copy.78
  10.4 1.0 copy-done.4
  11.4 1.0 copy.80
  12.4 1.1 pad_maximum_fusion
  13.5 8.1 %all-to-all-done.1 = bf16[4,3,256,128]{2,3,1,0:T(8,128)(2,1)S(1)} async-done(((bf16[4,3,256,128]{2,3,1,0:T(8,128)(2,1)}), bf16[4,3,256,128]{2,3,1,0:T(8,128)(2,1)S(1)}, u32[]{:S(2)}, u32[]{:S(2)}) %all-to-all-start.1) | async-done | bytes 786464 | tf_op jit(solution)/shard_map/all_to_all | solution.py:180
  21.6 3.5 %all-to-all-start = ((bf16[4,4,256,128]{3,2,1,0:T(8,128)(2,1)}), bf16[4,4,256,128]{3,2,1,0:T(8,128)(2,1)S(1)}, u32[]{:S(2)}, u32[]{:S(2)}) async-start(bf16[4,4,256,128]{3,2,1,0:T(8,128)(2,1)} %pad_maximum_fusion), calls=%async_computation | async-start | bytes 2097152 | tf_op jit(solution)/shard_map/all_to_all | solution.py:199
  25.2 0.4 copy.87
  25.6 1.0 copy.93
  26.6 3.8 %collective-permute-start = (bf16[2,1024,128]{2,1,0:T(8,128)(2,1)}, bf16[2,1024,128]{2,1,0:T(8,128)(2,1)S(1)}, u32[]{:S(2)}, u32[]{:S(2)}) collective-permute-start(bf16[2,1024,128]{2,1,0:T(8,128)(2,1)} %bitcast.34), channel_id=1, source_target_pairs={{0,4},{4,8},{8,12},{12,16},{16,20},{20,24},{24,28},{28,32},{32,36}... | collective-permute-start | bytes 1572872 | tf_op jit(solution)/shard_map/ppermute | solution.py:20
  30.4 0.8 slice_bitcast_fusion.4
  31.3 0.2 copy.89
  31.5 0.1 slice_convert_fusion
  31.6 7.7 %all-to-all-done = bf16[4,4,256,128]{3,2,1,0:T(8,128)(2,1)S(1)} async-done(((bf16[4,4,256,128]{3,2,1,0:T(8,128)(2,1)}), bf16[4,4,256,128]{3,2,1,0:T(8,128)(2,1)S(1)}, u32[]{:S(2)}, u32[]{:S(2)}) %all-to-all-start) | async-done | bytes 1048608 | tf_op jit(solution)/shard_map/all_to_all | solution.py:199
  39.3 3.6 %all-to-all-start.2 = ((bf16[16,2,64,128]{3,2,1,0:T(8,128)(2,1)}), bf16[16,2,64,128]{3,2,1,0:T(8,128)(2,1)S(1)}, u32[]{:S(2)}, u32[]{:S(2)}) async-start(bf16[16,2,64,128]{3,2,1,0:T(8,128)(2,1)} %bitcast.9), calls=%async_computation.2 | async-start | bytes 1048576 | tf_op jit(solution)/shard_map/all_to_all | solution.py:183
  42.9 0.6 fusion.17.lse_ref
  43.5 1.1 %fusion.6 = s32[1024]{0:T(1024)} fusion(f32[1024,3]{1,0:T(8,128)S(1)} %slice_convert_fusion, s32[]{:T(128)S(6)} %mul.16), kind=kLoop, calls=%fused_computation.14 | loop fusion | flops 6144 | bytes 16388 | tf_op jit(solution)/shard_map/add | solution.py:204
  44.6 0.1 copy.127
  44.7 0.9 fusion.23
  45.6 8.1 %all-to-all-done.2 = bf16[16,2,64,128]{3,2,1,0:T(8,128)(2,1)S(1)} async-done(((bf16[16,2,64,128]{3,2,1,0:T(8,128)(2,1)}), bf16[16,2,64,128]{3,2,1,0:T(8,128)(2,1)S(1)}, u32[]{:S(2)}, u32[]{:S(2)}) %all-to-all-start.2) | async-done | bytes 524320 | tf_op jit(solution)/shard_map/all_to_all | solution.py:183
  53.8 0.0 copy-start
  53.8 1.0 fusion.dl_ref
  54.7 0.0 copy-done
  54.7 0.0 collective-permute-done
  54.7 0.8 slice_bitcast_fusion.2
  55.6 7.6 %shard_map.94 = (f32[2,1024,128]{2,1,0:T(8,128)}, bf16[2,1024,128]{2,1,0:T(8,128)(2,1)}) custom-call(bf16[2,1024,128]{2,1,0:T(8,128)(2,1)} %bitcast.107, bf16[2,1024,128]{2,1,0:T(8,128)(2,1)} %bitcast.103, f32[2,1024]{1,0:T(2,128)} %fusion.17.lse_ref, f32[2,1024]{1,0:T(2,128)} %fusion.dl_ref, s32[1,1024]{1,0:T(1,128)} %bitcast.125, ...), custom_call_target="tpu_custom_call" | custom-call | tf_op jit(solution)/shard_map/pallas_call | solution.py:131
  63.2 0.0 copy-start.1
  63.2 11.6 %collective-permute-start.1 = (bf16[2,1024,128]{2,1,0:T(8,128)(2,1)}, bf16[2,1024,128]{2,1,0:T(8,128)(2,1)S(1)}, u32[]{:S(2)}, u32[]{:S(2)}) collective-permute-start(bf16[2,1024,128]{2,1,0:T(8,128)(2,1)} %get-tuple-element.14), channel_id=1, source_target_pairs={{4,0},{8,4},{12,8},{16,12},{20,16},{24,20},{28,24},{32,28},{36,32}... | collective-permute-start | bytes 1572872 | tf_op jit(solution)/shard_map/ppermute | solution.py:20
  74.8 7.7 %shard_map.95 = (f32[2,1024,128]{2,1,0:T(8,128)}, f32[1024,128]{1,0:T(8,128)}, f32[1024,128]{1,0:T(8,128)}) custom-call(bf16[2,1024,128]{2,1,0:T(8,128)(2,1)} %bitcast.108, bf16[2,1024,128]{2,1,0:T(8,128)(2,1)} %bitcast.104, f32[2,1024]{1,0:T(2,128)} %fusion.17.lse_ref, f32[2,1024]{1,0:T(2,128)} %fusion.dl_ref, s32[1,1024]{1,0:T(1,128)} %bitcast.126, ...), custom_call_target="tpu_custom_call" | custom-call | tf_op jit(solution)/shard_map/pallas_call | solution.py:131
  82.5 0.0 copy-done.1
  82.5 0.0 copy-start.5
  82.5 0.0 copy-start.6
  82.5 1.5 %fusion.1 = bf16[1024,2,128]{2,0,1:T(8,128)(2,1)S(1)} fusion(f32[2,1024,128]{2,1,0:T(8,128)S(1)} %copy-done.1, f32[2,1024,128]{2,1,0:T(8,128)} %get-tuple-element.16), kind=kLoop, calls=%fused_computation.8 | loop fusion | flops 786432 | bytes 2621440 | tf_op jit(solution)/shard_map/convert_element_type | solution.py:223
  83.9 1.6 %collective-permute-done.1 = bf16[2,1024,128]{2,1,0:T(8,128)(2,1)S(1)} collective-permute-done((bf16[2,1024,128]{2,1,0:T(8,128)(2,1)}, bf16[2,1024,128]{2,1,0:T(8,128)(2,1)S(1)}, u32[]{:S(2)}, u32[]{:S(2)}) %collective-permute-start.1) | collective-permute-done | bytes 524320 | tf_op jit(solution)/shard_map/ppermute | solution.py:20
  85.5 0.0 copy-done.5
  85.5 0.0 copy-done.6
  85.5 0.1 fusion.12
  85.6 0.1 pad_maximum_fusion.1
  85.8 0.8 copy.94
  86.6 20.3 %all_to_all.60 = bf16[1024,4,128]{2,1,0:T(4,128)(2,1)S(1)} all-to-all(bf16[1024,4,128]{2,1,0:T(4,128)(2,1)S(1)} %copy.94), channel_id=1, replica_groups=mesh['head'=4,'sh'=32,'sl'=4] {'sl','head'}, dimensions={0} | all-to-all | bytes 2097152 | tf_op jit(solution)/shard_map/all_to_all | solution.py:217
  106.9 0.8 copy.126
  107.7 0.2 slice.111
  107.9 1.0 fusion.22
  108.8 1.6 %copy.96 = bf16[64,4,4,2,128]{4,3,2,1,0:T(2,128)(2,1)} copy(bf16[64,4,4,2,128]{4,2,1,0,3:T(4,128)(2,1)S(1)} %slice.111) | data formatting | bytes 1048576 | tf_op jit(solution)/shard_map/slice | solution.py:228
  (13 shorter events, 0.2 us)
Async XLA Ops:
  0.6 0.7 copy-start.8
  1.4 1.3 %copy-start.7 = (bf16[256,4,128]{2,1,0:T(4,128)(2,1)S(1)}, bf16[256,4,128]{2,1,0:T(4,128)(2,1)}, u32[]{:S(2)}) copy-start(bf16[256,4,128]{2,1,0:T(4,128)(2,1)} %param.9) | copy-start | bytes 786436
  4.7 4.6 %copy-start.2 = (bf16[256,8,128]{2,1,0:T(8,128)(2,1)S(1)}, bf16[256,8,128]{2,1,0:T(8,128)(2,1)}, u32[]{:S(2)}) copy-start(bf16[256,8,128]{2,1,0:T(8,128)(2,1)} %param.7) | copy-start | bytes 1572868
  4.7 16.9 %all-to-all-start.1 = ((bf16[4,3,256,128]{2,3,1,0:T(8,128)(2,1)}), bf16[4,3,256,128]{2,3,1,0:T(8,128)(2,1)S(1)}, u32[]{:S(2)}, u32[]{:S(2)}) async-start(bf16[4,3,256,128]{2,3,1,0:T(8,128)(2,1)} %copy.86), calls=%async_computation.1 | async-start | bytes 1572864 | tf_op jit(solution)/shard_map/all_to_all | solution.py:180
  9.3 1.0 copy-start.3
  10.4 1.0 copy-start.4
  21.6 17.7 %all-to-all-start = ((bf16[4,4,256,128]{3,2,1,0:T(8,128)(2,1)}), bf16[4,4,256,128]{3,2,1,0:T(8,128)(2,1)S(1)}, u32[]{:S(2)}, u32[]{:S(2)}) async-start(bf16[4,4,256,128]{3,2,1,0:T(8,128)(2,1)} %pad_maximum_fusion), calls=%async_computation | async-start | bytes 2097152 | tf_op jit(solution)/shard_map/all_to_all | solution.py:199
  26.6 28.2 %collective-permute-start = (bf16[2,1024,128]{2,1,0:T(8,128)(2,1)}, bf16[2,1024,128]{2,1,0:T(8,128)(2,1)S(1)}, u32[]{:S(2)}, u32[]{:S(2)}) collective-permute-start(bf16[2,1024,128]{2,1,0:T(8,128)(2,1)} %bitcast.34), channel_id=1, source_target_pairs={{0,4},{4,8},{8,12},{12,16},{16,20},{20,24},{24,28},{28,32},{32,36}... | collective-permute-start | bytes 1572872 | tf_op jit(solution)/shard_map/ppermute | solution.py:20
  39.3 14.4 %all-to-all-start.2 = ((bf16[16,2,64,128]{3,2,1,0:T(8,128)(2,1)}), bf16[16,2,64,128]{3,2,1,0:T(8,128)(2,1)S(1)}, u32[]{:S(2)}, u32[]{:S(2)}) async-start(bf16[16,2,64,128]{3,2,1,0:T(8,128)(2,1)} %bitcast.9), calls=%async_computation.2 | async-start | bytes 1048576 | tf_op jit(solution)/shard_map/all_to_all | solution.py:183
  53.8 1.0 copy-start
  63.2 19.3 %copy-start.1 = (f32[2,1024,128]{2,1,0:T(8,128)S(1)}, f32[2,1024,128]{2,1,0:T(8,128)}, u32[]{:S(2)}) copy-start(f32[2,1024,128]{2,1,0:T(8,128)} %get-tuple-element.13) | copy-start | bytes 3145732
  63.2 22.4 %collective-permute-start.1 = (bf16[2,1024,128]{2,1,0:T(8,128)(2,1)}, bf16[2,1024,128]{2,1,0:T(8,128)(2,1)S(1)}, u32[]{:S(2)}, u32[]{:S(2)}) collective-permute-start(bf16[2,1024,128]{2,1,0:T(8,128)(2,1)} %get-tuple-element.14), channel_id=1, source_target_pairs={{4,0},{8,4},{12,8},{16,12},{20,16},{24,20},{28,24},{32,28},{36,32}... | collective-permute-start | bytes 1572872 | tf_op jit(solution)/shard_map/ppermute | solution.py:20
  82.5 3.1 %copy-start.5 = (f32[1024,128]{1,0:T(8,128)S(1)}, f32[1024,128]{1,0:T(8,128)}, u32[]{:S(2)}) copy-start(f32[1024,128]{1,0:T(8,128)} %get-tuple-element.17) | copy-start | bytes 1572868
  82.5 3.1 %copy-start.6 = (f32[1024,128]{1,0:T(8,128)S(1)}, f32[1024,128]{1,0:T(8,128)}, u32[]{:S(2)}) copy-start(f32[1024,128]{1,0:T(8,128)} %get-tuple-element.18) | copy-start | bytes 1572868

commit v13 on v12

--- a/solution.py
+++ b/solution.py
@@ -56,14 +56,14 @@
     return query_term.reshape(tokens, group, depth), key_term, value_term
 
 
-def band_kernel(halo, q_ref, g_ref, lse_ref, dl_ref, ps_ref, k_ref, v_ref, dq_ref, *rest):
+def band_kernel(halo, q_ref, g_ref, lse_ref, dl_ref, ps_ref, k_ref, v_ref, *rest):
     heads, tokens, depth = q_ref.shape
     tiles = tokens // BLOCK
     reach = WINDOW_LENGTH // BLOCK
     if halo:
-        low_ref, dk_ref, dv_ref = rest
+        dq_ref, low_ref, dk_ref, dv_ref = rest
     else:
-        dk_ref, dv_ref = rest
+        dq_in_ref, dq_ref, dk_ref, dv_ref = rest
     dk_ref[...] = jnp.zeros(dk_ref.shape, jnp.float32)
     dv_ref[...] = jnp.zeros(dv_ref.shape, jnp.float32)
     first = (((0,), (0,)), ((), ()))
@@ -82,7 +82,10 @@
         grad = jnp.concatenate([g_ref[h, rows, :] for h in range(heads)], axis=0)
         logsum = jnp.concatenate([lse_ref[h : h + 1, rows] for h in range(heads)], axis=1)
         delta = jnp.concatenate([dl_ref[h : h + 1, rows] for h in range(heads)], axis=1)
-        query_acc = jnp.zeros((width, depth), jnp.float32)
+        if halo:
+            query_acc = jnp.zeros((width, depth), jnp.float32)
+        else:
+            query_acc = jnp.concatenate([dq_in_ref[h, rows, :] for h in range(heads)], axis=0)
         for b, kb in blocks:
             keys_at = slice(kb * BLOCK, (kb + 1) * BLOCK)
             key = k_ref[keys_at, :]
@@ -108,29 +111,33 @@
                 probs.astype(jnp.bfloat16), grad, preferred_element_type=jnp.float32
             )
         for h in range(heads):
-            dq_ref[h, rows, :] = query_acc[h * BLOCK : (h + 1) * BLOCK]
+            part = query_acc[h * BLOCK : (h + 1) * BLOCK]
+            dq_ref[h, rows, :] = part if halo else (part * score_scale).astype(jnp.bfloat16)
     if halo:
         low_ref[0] = dk_ref[...].astype(jnp.bfloat16)
         low_ref[1] = dv_ref[...].astype(jnp.bfloat16)
 
 
-def band_part(halo, query, grad, logsum, delta, start_rel, keys, values):
+def band_part(halo, query, grad, logsum, delta, start_rel, keys, values, dq_in=None):
     group, tokens, depth = query.shape
     total = keys.shape[0]
     sums = (
         jax.ShapeDtypeStruct((total, depth), jnp.float32),
         jax.ShapeDtypeStruct((total, depth), jnp.float32),
     )
-    dq = jax.ShapeDtypeStruct((group, tokens, depth), jnp.float32)
     if halo:
+        dq = jax.ShapeDtypeStruct((group, tokens, depth), jnp.float32)
         outs = (dq, jax.ShapeDtypeStruct((2, total, depth), jnp.bfloat16))
         scratch = [pltpu.VMEM((total, depth), jnp.float32)] * 2
+        extra = ()
     else:
+        dq = jax.ShapeDtypeStruct((group, tokens, depth), jnp.bfloat16)
         outs = (dq,) + sums
         scratch = []
+        extra = (dq_in,)
     return pl.pallas_call(
         partial(band_kernel, halo), out_shape=outs, scratch_shapes=scratch
-    )(query, grad, logsum, delta, start_rel, keys, values)
+    )(query, grad, logsum, delta, start_rel, keys, values, *extra)
 
 
 def split_three(x):
@@ -207,10 +214,10 @@
     )
     back = shifted(key_far, "sh", -1)
     query_g, key_far = lax.optimization_barrier((query_g, key_far))
-    query_own, key_sum, value_sum = band_part(
-        False, query_g, grad_g, logsum_g, delta_g, start_rel, key_own, value_own
-    )
-    query_sum = (query_far + query_own).transpose(1, 0, 2)
+    query_grad, key_sum, value_sum = band_part(
+        False, query_g, grad_g, logsum_g, delta_g, start_rel, key_own, value_own, query_far
+    )
+    query_grad = query_grad.transpose(1, 0, 2)
 
     def to_tokens(x):
         items = x.shape[1]
@@ -220,7 +227,6 @@
 
     key_total = key_sum + back[0].astype(jnp.float32)
     value_total = value_sum + back[1].astype(jnp.float32)
-    query_grad = (query_sum * score_scale).astype(jnp.bfloat16)
     key_grad = (key_total * score_scale).astype(jnp.bfloat16)[:, None]
     value_grad = value_total.astype(jnp.bfloat16)[:, None]
     outs = to_tokens(jnp.concatenate([query_grad, key_grad, value_grad], axis=1))

time: 111 us -> 112 us (level)
    convert_element_type x1 -> x0, other arithmetic: 1.45 us -> none  [on_device(): query_grad = (query_sum * score_scale).astype(jnp.bfloat16)]
    broadcast_in_dim x1, other arithmetic: 0.12 us -> 1.38 us  [on_device(): key_grad = (key_total * score_scale).astype(jnp.bfloat16)[:, None]]
    unnamed x22 -> x18, local copies, waits for them, and re-layouts: 3.58 us -> 3.57 us
  transfers between devices with their start and end apart: 5 -> 5, of which waited for: 4 -> 4; matrix products, arithmetic and copies ran while one was open for 9% -> 8% of each run, Pallas kernels for 7% -> 7%
where the time goes in v13:
time: 112 us
  starting transfers between devices  27 us (24%)
  waiting for transfers between devices  26.4 us (24%)
  blocking collectives  20.3 us (18%)
  Pallas kernels  15.8 us (14%)
  local copies, waits for them, and re-layouts  14.3 us (13%)
  other arithmetic  6.88 us (6%)
    all_to_all x1, blocking collectives, to_tokens(): lax.all_to_all(x, ('sl', 'head'), split_axis=0, concat_axis=1, tiled=True)  20.3 us
    pallas_call x2, Pallas kernels, band_part(): pl.pallas_call(partial(band_kernel, halo), out_shape=outs, scratch_shapes...  15.8 us
    ppermute x2, starting transfers between devices, shifted(): return lax.ppermute(value, axis, pairs)  15.3 us
    all_to_all x1, waiting for transfers between devices, on_device(): lax.all_to_all(kv_packed, 'sl', split_axis=0, concat_axis=2, tiled=True)[0]  8.13 us
    all_to_all x1, waiting for transfers between devices, on_device(): lax.all_to_all(grad_g, ('sl', 'head'), split_axis=0, concat_axis=2, tiled...  8.08 us
    all_to_all x1, waiting for transfers between devices, on_device(): lax.all_to_all(qf_packed, 'sl', split_axis=0, concat_axis=2, tiled=True)[0]  7.68 us
    all_to_all x1, starting transfers between devices, on_device(): lax.all_to_all(kv_packed, 'sl', split_axis=0, concat_axis=2, tiled=True)[0]  4.59 us
    unnamed x18, local copies, waits for them, and re-layouts  3.57 us
  transfers between devices with their start and end apart: 5, of which 4 were waited for; matrix products, arithmetic and copies ran while one was open for 8% of the time, Pallas kernels for 7%

profile of v13, /device:TPU:4, one launch (start us, length us, event | category | flops | bytes accessed | tf_op | source)
XLA Modules:
  0.0 111.6 jit_solution(6708834272602461801)
XLA Ops:
  0.6 0.0 copy-start.6
  0.6 0.7 reduce-precision_convert_fusion.3
  1.4 0.0 copy-done.6
  1.4 0.0 copy-start.5
  1.4 1.3 %copy.81 = bf16[256,4,128]{0,1,2:T(4,128)(2,1)S(1)} copy(bf16[256,4,128]{2,1,0:T(4,128)(2,1)} %param.8) | data formatting | bytes 524288 | tf_op args[1]
  2.7 0.0 copy-done.5
  2.7 0.2 copy.82
  3.0 0.1 fusion.14
  3.0 0.7 pad_maximum_fusion.2
  3.7 1.0 copy.86
  4.7 0.0 copy-start.1
  4.7 4.6 %all-to-all-start.1 = ((bf16[4,3,256,128]{2,3,1,0:T(8,128)(2,1)}), bf16[4,3,256,128]{2,3,1,0:T(8,128)(2,1)S(1)}, u32[]{:S(2)}, u32[]{:S(2)}) async-start(bf16[4,3,256,128]{2,3,1,0:T(8,128)(2,1)} %copy.86), calls=%async_computation.1 | async-start | bytes 1572864 | tf_op jit(solution)/shard_map/all_to_all | solution.py:187
  9.3 0.0 copy-done.1
  9.3 0.0 copy-start.2
  9.3 0.1 copy.77
  9.4 1.0 copy-done.2
  10.4 0.0 copy-start.3
  10.4 0.1 copy.78
  10.4 1.0 copy-done.3
  11.4 1.0 copy.80
  12.4 1.1 pad_maximum_fusion
  13.5 8.1 %all-to-all-done.1 = bf16[4,3,256,128]{2,3,1,0:T(8,128)(2,1)S(1)} async-done(((bf16[4,3,256,128]{2,3,1,0:T(8,128)(2,1)}), bf16[4,3,256,128]{2,3,1,0:T(8,128)(2,1)S(1)}, u32[]{:S(2)}, u32[]{:S(2)}) %all-to-all-start.1) | async-done | bytes 786464 | tf_op jit(solution)/shard_map/all_to_all | solution.py:187
  21.6 3.5 %all-to-all-start = ((bf16[4,4,256,128]{3,2,1,0:T(8,128)(2,1)}), bf16[4,4,256,128]{3,2,1,0:T(8,128)(2,1)S(1)}, u32[]{:S(2)}, u32[]{:S(2)}) async-start(bf16[4,4,256,128]{3,2,1,0:T(8,128)(2,1)} %pad_maximum_fusion), calls=%async_computation | async-start | bytes 2097152 | tf_op jit(solution)/shard_map/all_to_all | solution.py:206
  25.2 0.4 copy.87
  25.6 1.0 copy.93
  26.6 3.8 %collective-permute-start = (bf16[2,1024,128]{2,1,0:T(8,128)(2,1)}, bf16[2,1024,128]{2,1,0:T(8,128)(2,1)S(1)}, u32[]{:S(2)}, u32[]{:S(2)}) collective-permute-start(bf16[2,1024,128]{2,1,0:T(8,128)(2,1)} %bitcast.34), channel_id=1, source_target_pairs={{0,4},{4,8},{8,12},{12,16},{16,20},{20,24},{24,28},{28,32},{32,36}... | collective-permute-start | bytes 1572872 | tf_op jit(solution)/shard_map/ppermute | solution.py:20
  30.4 0.8 slice_bitcast_fusion.4
  31.3 0.2 copy.89
  31.5 0.1 slice_convert_fusion
  31.7 7.7 %all-to-all-done = bf16[4,4,256,128]{3,2,1,0:T(8,128)(2,1)S(1)} async-done(((bf16[4,4,256,128]{3,2,1,0:T(8,128)(2,1)}), bf16[4,4,256,128]{3,2,1,0:T(8,128)(2,1)S(1)}, u32[]{:S(2)}, u32[]{:S(2)}) %all-to-all-start) | async-done | bytes 1048608 | tf_op jit(solution)/shard_map/all_to_all | solution.py:206
  39.3 3.6 %all-to-all-start.2 = ((bf16[16,2,64,128]{3,2,1,0:T(8,128)(2,1)}), bf16[16,2,64,128]{3,2,1,0:T(8,128)(2,1)S(1)}, u32[]{:S(2)}, u32[]{:S(2)}) async-start(bf16[16,2,64,128]{3,2,1,0:T(8,128)(2,1)} %bitcast.9), calls=%async_computation.2 | async-start | bytes 1048576 | tf_op jit(solution)/shard_map/all_to_all | solution.py:190
  42.9 0.6 fusion.16.lse_ref
  43.5 1.1 %fusion.5 = s32[1024]{0:T(1024)} fusion(f32[1024,3]{1,0:T(8,128)S(1)} %slice_convert_fusion, s32[]{:T(128)S(6)} %mul.9), kind=kLoop, calls=%fused_computation.12 | loop fusion | flops 6144 | bytes 16388 | tf_op jit(solution)/shard_map/add | solution.py:211
  44.7 0.1 copy.127
  44.8 0.9 fusion.22
  45.6 8.1 %all-to-all-done.2 = bf16[16,2,64,128]{3,2,1,0:T(8,128)(2,1)S(1)} async-done(((bf16[16,2,64,128]{3,2,1,0:T(8,128)(2,1)}), bf16[16,2,64,128]{3,2,1,0:T(8,128)(2,1)S(1)}, u32[]{:S(2)}, u32[]{:S(2)}) %all-to-all-start.2) | async-done | bytes 524320 | tf_op jit(solution)/shard_map/all_to_all | solution.py:190
  53.8 0.0 copy-start
  53.8 1.0 fusion.dl_ref
  54.7 0.0 copy-done
  54.7 0.0 collective-permute-done
  54.7 0.8 slice_bitcast_fusion.2
  55.6 7.6 %shard_map.94 = (f32[2,1024,128]{2,1,0:T(8,128)}, bf16[2,1024,128]{2,1,0:T(8,128)(2,1)}) custom-call(bf16[2,1024,128]{2,1,0:T(8,128)(2,1)} %bitcast.106, bf16[2,1024,128]{2,1,0:T(8,128)(2,1)} %bitcast.102, f32[2,1024]{1,0:T(2,128)} %fusion.16.lse_ref, f32[2,1024]{1,0:T(2,128)} %fusion.dl_ref, s32[1,1024]{1,0:T(1,128)} %bitcast.125, ...), custom_call_target="tpu_custom_call" | custom-call | tf_op jit(solution)/shard_map/pallas_call | solution.py:138
  63.2 11.5 %collective-permute-start.1 = (bf16[2,1024,128]{2,1,0:T(8,128)(2,1)}, bf16[2,1024,128]{2,1,0:T(8,128)(2,1)S(1)}, u32[]{:S(2)}, u32[]{:S(2)}) collective-permute-start(bf16[2,1024,128]{2,1,0:T(8,128)(2,1)} %get-tuple-element.13), channel_id=1, source_target_pairs={{4,0},{8,4},{12,8},{16,12},{20,16},{24,20},{28,24},{32,28},{36,32}... | collective-permute-start | bytes 1572872 | tf_op jit(solution)/shard_map/ppermute | solution.py:20
  74.7 8.2 %shard_map.95 = (bf16[2,1024,128]{2,1,0:T(8,128)(2,1)}, f32[1024,128]{1,0:T(8,128)}, f32[1024,128]{1,0:T(8,128)}) custom-call(bf16[2,1024,128]{2,1,0:T(8,128)(2,1)} %bitcast.107, bf16[2,1024,128]{2,1,0:T(8,128)(2,1)} %bitcast.103, f32[2,1024]{1,0:T(2,128)} %fusion.16.lse_ref, f32[2,1024]{1,0:T(2,128)} %fusion.dl_ref, s32[1,1024]{1,0:T(1,128)} %bitcast.126, ...), custom_call_target="tpu_custom_call" | custom-call | tf_op jit(solution)/shard_map/pallas_call | solution.py:138
  82.9 2.5 %collective-permute-done.1 = bf16[2,1024,128]{2,1,0:T(8,128)(2,1)S(1)} collective-permute-done((bf16[2,1024,128]{2,1,0:T(8,128)(2,1)}, bf16[2,1024,128]{2,1,0:T(8,128)(2,1)S(1)}, u32[]{:S(2)}, u32[]{:S(2)}) %collective-permute-start.1) | collective-permute-done | bytes 524320 | tf_op jit(solution)/shard_map/ppermute | solution.py:20
  85.4 0.0 copy-start.4
  85.4 1.4 %fusion.11 = (bf16[1024,1,128]{2,0,1:T(8,128)(2,1)S(1)}, bf16[1024,1,128]{2,0,1:T(8,128)(2,1)S(1)}) fusion(f32[1024,128]{1,0:T(8,128)} %get-tuple-element.17, bf16[2,1024,128]{2,1,0:T(8,128)(2,1)S(1)} %collective-permute-done.1, f32[1024,128]{1,0:T(8,128)} %get-tuple-element.18), kind=kLoop, calls=%fused_computation.22 | loop fusion | flops 917504 | bytes 2097152 | tf_op jit(solution)/shard_map/broadcast_in_dim | solution.py:230
  86.8 0.0 copy-done.4
  86.8 0.1 pad_maximum_fusion.1
  86.9 0.8 copy.94
  87.7 20.3 %all_to_all.60 = bf16[1024,4,128]{2,1,0:T(4,128)(2,1)S(1)} all-to-all(bf16[1024,4,128]{2,1,0:T(4,128)(2,1)S(1)} %copy.94), channel_id=1, replica_groups=mesh['head'=4,'sh'=32,'sl'=4] {'sl','head'}, dimensions={0} | all-to-all | bytes 2097152 | tf_op jit(solution)/shard_map/all_to_all | solution.py:224
  108.0 0.8 copy.126
  108.8 0.2 slice.111
  109.0 1.0 fusion.21
  110.0 1.6 %copy.96 = bf16[64,4,4,2,128]{4,3,2,1,0:T(2,128)(2,1)} copy(bf16[64,4,4,2,128]{4,2,1,0,3:T(4,128)(2,1)S(1)} %slice.111) | data formatting | bytes 1048576 | tf_op jit(solution)/shard_map/slice | solution.py:234
  (13 shorter events, 0.2 us)
Async XLA Ops:
  0.6 0.7 copy-start.6
  1.4 1.3 %copy-start.5 = (bf16[256,4,128]{2,1,0:T(4,128)(2,1)S(1)}, bf16[256,4,128]{2,1,0:T(4,128)(2,1)}, u32[]{:S(2)}) copy-start(bf16[256,4,128]{2,1,0:T(4,128)(2,1)} %param.9) | copy-start | bytes 786436
  4.7 4.6 %copy-start.1 = (bf16[256,8,128]{2,1,0:T(8,128)(2,1)S(1)}, bf16[256,8,128]{2,1,0:T(8,128)(2,1)}, u32[]{:S(2)}) copy-start(bf16[256,8,128]{2,1,0:T(8,128)(2,1)} %param.7) | copy-start | bytes 1572868
  4.7 16.9 %all-to-all-start.1 = ((bf16[4,3,256,128]{2,3,1,0:T(8,128)(2,1)}), bf16[4,3,256,128]{2,3,1,0:T(8,128)(2,1)S(1)}, u32[]{:S(2)}, u32[]{:S(2)}) async-start(bf16[4,3,256,128]{2,3,1,0:T(8,128)(2,1)} %copy.86), calls=%async_computation.1 | async-start | bytes 1572864 | tf_op jit(solution)/shard_map/all_to_all | solution.py:187
  9.3 1.0 copy-start.2
  10.4 1.0 copy-start.3
  21.6 17.7 %all-to-all-start = ((bf16[4,4,256,128]{3,2,1,0:T(8,128)(2,1)}), bf16[4,4,256,128]{3,2,1,0:T(8,128)(2,1)S(1)}, u32[]{:S(2)}, u32[]{:S(2)}) async-start(bf16[4,4,256,128]{3,2,1,0:T(8,128)(2,1)} %pad_maximum_fusion), calls=%async_computation | async-start | bytes 2097152 | tf_op jit(solution)/shard_map/all_to_all | solution.py:206
  26.6 28.1 %collective-permute-start = (bf16[2,1024,128]{2,1,0:T(8,128)(2,1)}, bf16[2,1024,128]{2,1,0:T(8,128)(2,1)S(1)}, u32[]{:S(2)}, u32[]{:S(2)}) collective-permute-start(bf16[2,1024,128]{2,1,0:T(8,128)(2,1)} %bitcast.34), channel_id=1, source_target_pairs={{0,4},{4,8},{8,12},{12,16},{16,20},{20,24},{24,28},{28,32},{32,36}... | collective-permute-start | bytes 1572872 | tf_op jit(solution)/shard_map/ppermute | solution.py:20
  39.3 14.4 %all-to-all-start.2 = ((bf16[16,2,64,128]{3,2,1,0:T(8,128)(2,1)}), bf16[16,2,64,128]{3,2,1,0:T(8,128)(2,1)S(1)}, u32[]{:S(2)}, u32[]{:S(2)}) async-start(bf16[16,2,64,128]{3,2,1,0:T(8,128)(2,1)} %bitcast.9), calls=%async_computation.2 | async-start | bytes 1048576 | tf_op jit(solution)/shard_map/all_to_all | solution.py:190
  53.8 1.0 copy-start
  63.2 22.2 %collective-permute-start.1 = (bf16[2,1024,128]{2,1,0:T(8,128)(2,1)}, bf16[2,1024,128]{2,1,0:T(8,128)(2,1)S(1)}, u32[]{:S(2)}, u32[]{:S(2)}) collective-permute-start(bf16[2,1024,128]{2,1,0:T(8,128)(2,1)} %get-tuple-element.13), channel_id=1, source_target_pairs={{4,0},{8,4},{12,8},{16,12},{20,16},{24,20},{28,24},{32,28},{36,32}... | collective-permute-start | bytes 1572872 | tf_op jit(solution)/shard_map/ppermute | solution.py:20
  85.4 1.4 %copy-start.4 = (bf16[2,1024,128]{2,1,0:T(8,128)(2,1)S(1)}, bf16[2,1024,128]{2,1,0:T(8,128)(2,1)}, u32[]{:S(2)}) copy-start(bf16[2,1024,128]{2,1,0:T(8,128)(2,1)} %get-tuple-element.16) | copy-start | bytes 1572868
